TPU v7x, 1024 devices: a whole 4x4x32 slice. The times are simulated.
1024 devices in a mesh: gx: 8 (over y, x_lo), gy: 4 (over x_hi, core), gz: 32 (over z).
Axes of the slice: x: 4 (x_hi: 2, x_lo: 2; x = x_hi * 2 + x_lo), y: 4, z: 32, core: 2. Of those that a mesh axis runs over, the one named last changes fastest.
Arguments:
- vorticity: float32 [8, 4, 32, 32768], P('gx', 'gy', 'gz'), may hold values from -6 to 6
- green_spectrum: float32 [64, 4096], replicated, may hold values from 0.05 to 1
- coupling: float32 [2, 2, 2], replicated, may hold values from 0.5 to 1.5
Outputs:
- potential: float32 [8, 4, 32, 32768], P('gx', 'gy', 'gz')
All inputs are finite; a program needn't handle non-finite values.
Results may differ from a plain program's by a relative error of at most 0.0015.
Values sent between devices are 32-bit elements; how exact they have to be, the bound alone decides.
No kernel may reach another device: no remote copies, remote signals or barrier semaphores. Data moves between devices by JAX's collectives and lax.ppermute only.
A program may use at most 32 MiB of HBM per device.

v0:
```python
import math

import jax
import jax.numpy as jnp
from jax import lax
from jax.sharding import PartitionSpec as P

PX = 32
PY = 32
PZ = 32
CB = 16


def from_behind(block, axis, distance):
    devices = range(lax.axis_size(axis))
    route = [(i - distance, i) for i in devices if i - distance in devices]
    return lax.ppermute(block, axis, route)


def from_partner(value, axis, apart):
    mask = 2**apart
    pairs = [(source, source ^ mask) for source in range(lax.axis_size(axis))]
    return lax.ppermute(value, axis, pairs)


def angle_tables(count_out, count_in, offset, length, factor):
    rows = lax.iota(jnp.int32, count_out)[:, None]
    cols = lax.iota(jnp.int32, count_in)[None, :]
    phase = (rows * (cols + offset) % length).astype(jnp.float32) * (2.0 * math.pi / length)
    return (
        (jnp.cos(phase) * factor).astype(jnp.bfloat16),
        (jnp.sin(phase) * factor).astype(jnp.bfloat16),
    )


def mixed(form, table, data):
    return jnp.einsum(form, table, data, preferred_element_type=jnp.float32)


def local_box(patch, green_spectrum):
    bf = jnp.bfloat16
    px, py, pz = patch.shape
    bx, by, bz = green_spectrum.shape
    wb = patch.astype(bf)
    cosx, sinx = angle_tables(bx, px, px // 2, bx, 1.0)
    cosy, siny = angle_tables(by, py, py // 2, by, 1.0)
    cosz, sinz = angle_tables(bz, pz, pz // 2, bz, 1.0)
    real = mixed("kn,nyz->kyz", cosx, wb).astype(bf)
    imag = (-mixed("kn,nyz->kyz", sinx, wb)).astype(bf)
    for form, cosv, sinv in (("ky,xyz->xkz", cosy, siny), ("kz,xyz->xyk", cosz, sinz)):
        new_real = (mixed(form, cosv, real) + mixed(form, sinv, imag)).astype(bf)
        imag = (mixed(form, cosv, imag) - mixed(form, sinv, real)).astype(bf)
        real = new_real
    real = (real.astype(jnp.float32) * green_spectrum).astype(bf)
    imag = (imag.astype(jnp.float32) * green_spectrum).astype(bf)
    icosz, isinz = angle_tables(bz, bz, 0, bz, 1.0 / bz)
    icosy, isiny = angle_tables(by, by, 0, by, 1.0 / by)
    icosx, isinx = angle_tables(bx, bx, 0, bx, 1.0 / bx)
    for form, cosv, sinv in (("nk,xyk->xyn", icosz, isinz), ("nk,xkz->xnz", icosy, isiny)):
        new_real = (mixed(form, cosv, real) - mixed(form, sinv, imag)).astype(bf)
        imag = (mixed(form, cosv, imag) + mixed(form, sinv, real)).astype(bf)
        real = new_real
    return mixed("nk,kyz->nyz", icosx, real) - mixed("nk,kyz->nyz", isinx, imag)


def move_x(part, step):
    return from_behind(part, "gx", step)


def move_y(part, step):
    return from_behind(part, "gy", step)


def move_z(part, step):
    return from_behind(part, "gz", step)


def fold_margin(field, dim, mover):
    quarter = field.shape[dim] // 4
    low_rim = lax.slice_in_dim(field, 0, quarter, axis=dim)
    first = lax.slice_in_dim(field, quarter, 2 * quarter, axis=dim)
    second = lax.slice_in_dim(field, 2 * quarter, 3 * quarter, axis=dim)
    high_rim = lax.slice_in_dim(field, 3 * quarter, 4 * quarter, axis=dim)
    from_left = mover(high_rim, 1)
    from_right = mover(low_rim, -1)
    return jnp.concatenate([first + from_left, second + from_right], axis=dim)


def local(vorticity, green_spectrum, coupling):
    px, py, pz = (PX, PY, PZ)
    patch = vorticity.reshape(px, py, pz)
    spectrum = green_spectrum.reshape(2 * px, 2 * py, 2 * pz)
    box = local_box(patch, spectrum)
    order = ((2, move_z), (1, move_y), (0, move_x))
    near = box
    for dim, mover in order:
        near = fold_margin(near, dim, mover)
    cx, cy, cz = (px // CB, py // CB, pz // CB)
    scale = 1.0 / math.sqrt(CB**3)
    coarse = patch.reshape(cx, CB, cy, CB, cz, CB).sum(axis=(1, 3, 5)) * scale
    flat = coarse.reshape(-1)
    count = lax.axis_size(("gx", "gy", "gz"))
    levels = count.bit_length() - 1
    total = jnp.zeros_like(flat)
    running = flat
    for bit in range(levels):
        running = running + from_partner(running, ("gx", "gy", "gz"), bit)
        total = total + running / math.sqrt(2 ** (bit + 1))
    far = total.reshape(cx, cy, cz) * coupling
    far_cells = jnp.broadcast_to(far[:, None, :, None, :, None], (cx, CB, cy, CB, cz, CB)).reshape(
        px, py, pz
    )
    return (near + far_cells).reshape(1, 1, 1, px * py * pz)


def solution(mesh):
    return jax.shard_map(
        local,
        mesh=mesh,
        in_specs=(P("gx", "gy", "gz", None), P(), P()),
        out_specs=P("gx", "gy", "gz", None),
        check_vma=False,
    )
```

profile of v0, /device:TPU:6, one launch (start us, length us, event | category | flops | bytes accessed | tf_op | source)
XLA Modules:
  0.0 198.2 jit_solution(11715729633278657275)
XLA Ops:
  2.4 2.0 %reshape.39 = f32[64,64,64]{2,1,0:T(8,128)S(1)} reshape(f32[64,4096]{1,0:T(8,128)} %param.4) | data formatting | bytes 2097152 | tf_op jit(solution)/shard_map/reshape | solution.py:92
  17.7 4.2 %copy.25 = f32[64,64,64]{0,1,2:T(8,128)} copy(f32[64,64,64]{2,1,0:T(8,128)} %fusion.45) | data formatting | bytes 2097152 | tf_op jit(solution)/shard_map/nk,xkz->xnz/dot_general | solution.py:37
  21.8 3.1 %copy.26 = f32[64,64,64]{0,1,2:T(8,128)} copy(f32[64,64,64]{2,1,0:T(8,128)S(1)} %fusion.37) | data formatting | bytes 2097152 | tf_op jit(solution)/shard_map/nk,xkz->xnz/dot_general | solution.py:37
  24.9 2.7 %subtract_convert_fusion = bf16[64,64,64]{0,1,2:T(8,128)(2,1)S(1)} fusion(f32[64,64,64]{0,1,2:T(8,128)} %copy.25, f32[64,64,64]{0,1,2:T(8,128)} %copy.26), kind=kLoop, calls=%fused_computation.1 | loop fusion | flops 524288 | bytes 2621440 | tf_op jit(solution)/shard_map/convert_element_type | solution.py:60
  28.2 4.4 %copy.27 = f32[64,64,64]{0,1,2:T(8,128)} copy(f32[64,64,64]{2,1,0:T(8,128)} %fusion.41) | data formatting | bytes 2097152 | tf_op jit(solution)/shard_map/nk,xkz->xnz/dot_general | solution.py:37
  32.5 4.1 %copy.28 = f32[64,64,64]{0,1,2:T(8,128)} copy(f32[64,64,64]{2,1,0:T(8,128)} %fusion.35) | data formatting | bytes 2097152 | tf_op jit(solution)/shard_map/nk,xkz->xnz/dot_general | solution.py:37
  36.7 2.7 %add_convert_fusion = bf16[64,64,64]{0,1,2:T(8,128)(2,1)S(1)} fusion(f32[64,64,64]{0,1,2:T(8,128)} %copy.27, f32[64,64,64]{0,1,2:T(8,128)} %copy.28), kind=kLoop, calls=%fused_computation | loop fusion | flops 524288 | bytes 2621440 | tf_op jit(solution)/shard_map/convert_element_type | solution.py:61
  40.3 3.9 %collective-permute-start = (f32[64,64,16]{0,2,1:T(8,128)S(1)}, f32[64,64,16]{0,2,1:T(8,128)S(1)}, u32[]{:S(2)}, u32[]{:S(2)}) collective-permute-start(f32[64,64,16]{0,2,1:T(8,128)S(1)} %slice.49), channel_id=1, source_target_pairs={{0,1},{1,2},{2,3},{3,4},{4,5},{5,6},{6,7},{7,8},{8,9},{9,10},{10,1... | collective-permute-start | bytes 786440 | tf_op jit(solution)/shard_map/ppermute | solution.py:17
  44.2 11.1 %collective-permute-done = f32[64,64,16]{0,2,1:T(8,128)S(1)} collective-permute-done((f32[64,64,16]{0,2,1:T(8,128)S(1)}, f32[64,64,16]{0,2,1:T(8,128)S(1)}, u32[]{:S(2)}, u32[]{:S(2)}) %collective-permute-start) | collective-permute-done | bytes 262176 | tf_op jit(solution)/shard_map/ppermute | solution.py:17
  56.9 14.2 %collective-permute-done.1 = f32[64,64,16]{0,2,1:T(8,128)S(1)} collective-permute-done((f32[64,64,16]{0,2,1:T(8,128)S(1)}, f32[64,64,16]{0,2,1:T(8,128)S(1)}, u32[]{:S(2)}, u32[]{:S(2)}) %collective-permute-start.1) | collective-permute-done | bytes 262176 | tf_op jit(solution)/shard_map/ppermute | solution.py:17
  73.2 7.3 %collective-permute-done.2 = f32[64,16,32]{0,2,1:T(8,128)S(1)} collective-permute-done((f32[64,16,32]{0,2,1:T(8,128)S(1)}, f32[64,16,32]{0,2,1:T(8,128)S(1)}, u32[]{:S(2)}, u32[]{:S(2)}) %collective-permute-start.2) | collective-permute-done | bytes 131104 | tf_op jit(solution)/shard_map/ppermute | solution.py:17
  86.5 3.7 %collective-permute-start.4 = (f32[16,32,32]{0,2,1:T(8,128)S(1)}, f32[16,32,32]{0,2,1:T(8,128)S(1)}, u32[]{:S(2)}, u32[]{:S(2)}) collective-permute-start(f32[16,32,32]{0,2,1:T(8,128)S(1)} %fusion.8), channel_id=1, source_target_pairs={{0,128},{128,256},{256,384},{384,512},{512,640},{640,768},{768,896... | collective-permute-start | bytes 196616 | tf_op jit(solution)/shard_map/ppermute | solution.py:17
  90.4 3.8 %collective-permute-start.6 = (f32[8]{0:T(128)S(1)}, f32[8]{0:T(128)S(1)}, u32[]{:S(2)}, u32[]{:S(2)}) collective-permute-start(f32[8]{0:T(128)S(1)} %mul.263), channel_id=1, source_target_pairs={{0,1},{1,0},{2,3},{3,2},{4,5},{5,4},{6,7},{7,6},{8,9},{9,8},{10,11... | collective-permute-start | bytes 104 | tf_op jit(solution)/shard_map/ppermute | solution.py:23
  95.8 7.5 %collective-permute-start.7 = (f32[8]{0:T(128)S(1)}, f32[8]{0:T(128)S(1)}, u32[]{:S(2)}, u32[]{:S(2)}) collective-permute-start(f32[8]{0:T(128)S(1)} %add.196), channel_id=1, source_target_pairs={{0,2},{1,3},{2,0},{3,1},{4,6},{5,7},{6,4},{7,5},{8,10},{9,11},{10,... | collective-permute-start | bytes 104 | tf_op jit(solution)/shard_map/ppermute | solution.py:23
  104.9 9.1 %collective-permute-start.8 = (f32[8]{0:T(128)S(1)}, f32[8]{0:T(128)S(1)}, u32[]{:S(2)}, u32[]{:S(2)}) collective-permute-start(f32[8]{0:T(128)S(1)} %add.197), channel_id=1, source_target_pairs={{0,4},{1,5},{2,6},{3,7},{4,0},{5,1},{6,2},{7,3},{8,12},{9,13},{10,... | collective-permute-start | bytes 104 | tf_op jit(solution)/shard_map/ppermute | solution.py:23
  115.5 15.7 %collective-permute-start.9 = (f32[8]{0:T(128)S(1)}, f32[8]{0:T(128)S(1)}, u32[]{:S(2)}, u32[]{:S(2)}) collective-permute-start(f32[8]{0:T(128)S(1)} %add.199), channel_id=1, source_target_pairs={{0,8},{1,9},{2,10},{3,11},{4,12},{5,13},{6,14},{7,15},{8,0},{9,1},... | collective-permute-start | bytes 104 | tf_op jit(solution)/shard_map/ppermute | solution.py:23
  132.8 23.0 %collective-permute-start.10 = (f32[8]{0:T(128)S(1)}, f32[8]{0:T(128)S(1)}, u32[]{:S(2)}, u32[]{:S(2)}) collective-permute-start(f32[8]{0:T(128)S(1)} %add.201), channel_id=1, source_target_pairs={{0,16},{1,17},{2,18},{3,19},{4,20},{5,21},{6,22},{7,23},{8,24},{9,... | collective-permute-start | bytes 104 | tf_op jit(solution)/shard_map/ppermute | solution.py:23
  162.2 5.0 %collective-permute-done.12 = f32[8]{0:T(128)S(1)} collective-permute-done((f32[8]{0:T(128)S(1)}, f32[8]{0:T(128)S(1)}, u32[]{:S(2)}, u32[]{:S(2)}) %collective-permute-start.12) | collective-permute-done | bytes 64 | tf_op jit(solution)/shard_map/ppermute | solution.py:23
  167.3 2.1 %collective-permute-start.13 = (f32[8]{0:T(128)S(1)}, f32[8]{0:T(128)S(1)}, u32[]{:S(2)}, u32[]{:S(2)}) collective-permute-start(f32[8]{0:T(128)S(1)} %add.207), channel_id=1, source_target_pairs={{0,128},{1,129},{2,130},{3,131},{4,132},{5,133},{6,134},{7,135},{8... | collective-permute-start | bytes 104 | tf_op jit(solution)/shard_map/ppermute | solution.py:23
  169.4 3.3 %collective-permute-done.13 = f32[8]{0:T(128)S(1)} collective-permute-done((f32[8]{0:T(128)S(1)}, f32[8]{0:T(128)S(1)}, u32[]{:S(2)}, u32[]{:S(2)}) %collective-permute-start.13) | collective-permute-done | bytes 64 | tf_op jit(solution)/shard_map/ppermute | solution.py:23
  172.7 3.5 %collective-permute-start.14 = (f32[8]{0:T(128)S(1)}, f32[8]{0:T(128)S(1)}, u32[]{:S(2)}, u32[]{:S(2)}) collective-permute-start(f32[8]{0:T(128)S(1)} %add.209), channel_id=1, source_target_pairs={{0,256},{1,257},{2,258},{3,259},{4,260},{5,261},{6,262},{7,263},{8... | collective-permute-start | bytes 104 | tf_op jit(solution)/shard_map/ppermute | solution.py:23
  178.2 4.8 %collective-permute-start.15 = (f32[8]{0:T(128)S(1)}, f32[8]{0:T(128)S(1)}, u32[]{:S(2)}, u32[]{:S(2)}) collective-permute-start(f32[8]{0:T(128)S(1)} %add.211), channel_id=1, source_target_pairs={{0,512},{1,513},{2,514},{3,515},{4,516},{5,517},{6,518},{7,519},{8... | collective-permute-start | bytes 104 | tf_op jit(solution)/shard_map/ppermute | solution.py:23
  183.2 2.4 %collective-permute-start.5 = (f32[16,32,32]{0,2,1:T(8,128)S(1)}, f32[16,32,32]{0,2,1:T(8,128)S(1)}, u32[]{:S(2)}, u32[]{:S(2)}) collective-permute-start(f32[16,32,32]{0,2,1:T(8,128)S(1)} %get-tuple-element.10), channel_id=1, source_target_pairs={{128,0},{256,128},{384,256},{512,384},{640,512},{768,640},{896,768... | collective-permute-start | bytes 196616 | tf_op jit(solution)/shard_map/ppermute | solution.py:17
  187.7 8.5 %collective-permute-done.5 = f32[16,32,32]{0,2,1:T(8,128)S(1)} collective-permute-done((f32[16,32,32]{0,2,1:T(8,128)S(1)}, f32[16,32,32]{0,2,1:T(8,128)S(1)}, u32[]{:S(2)}, u32[]{:S(2)}) %collective-permute-start.5) | collective-permute-done | bytes 65568 | tf_op jit(solution)/shard_map/ppermute | solution.py:17
  (79 shorter events, 45.8 us)
Async XLA Ops:
  40.3 15.0 %collective-permute-start = (f32[64,64,16]{0,2,1:T(8,128)S(1)}, f32[64,64,16]{0,2,1:T(8,128)S(1)}, u32[]{:S(2)}, u32[]{:S(2)}) collective-permute-start(f32[64,64,16]{0,2,1:T(8,128)S(1)} %slice.49), channel_id=1, source_target_pairs={{0,1},{1,2},{2,3},{3,4},{4,5},{5,6},{6,7},{7,8},{8,9},{9,10},{10,1... | collective-permute-start | bytes 786440 | tf_op jit(solution)/shard_map/ppermute | solution.py:17
  55.5 27.4 %copy-start = (f32[1,1,1,32768]{3,2,1,0:T(1,128)S(1)}, f32[1,1,1,32768]{3,2,1,0:T(1,128)}, u32[]{:S(2)}) copy-start(f32[1,1,1,32768]{3,2,1,0:T(1,128)} %param.3) | copy-start | bytes 393220
  55.5 15.6 %collective-permute-start.1 = (f32[64,64,16]{0,2,1:T(8,128)S(1)}, f32[64,64,16]{0,2,1:T(8,128)S(1)}, u32[]{:S(2)}, u32[]{:S(2)}) collective-permute-start(f32[64,64,16]{0,2,1:T(8,128)S(1)} %get-tuple-element.6), channel_id=1, source_target_pairs={{1,0},{2,1},{3,2},{4,3},{5,4},{6,5},{7,6},{8,7},{9,8},{10,9},{11,1... | collective-permute-start | bytes 786440 | tf_op jit(solution)/shard_map/ppermute | solution.py:17
  71.2 9.2 %collective-permute-start.2 = (f32[64,16,32]{0,2,1:T(8,128)S(1)}, f32[64,16,32]{0,2,1:T(8,128)S(1)}, u32[]{:S(2)}, u32[]{:S(2)}) collective-permute-start(f32[64,16,32]{0,2,1:T(8,128)S(1)} %fusion.19), channel_id=1, source_target_pairs={{0,32},{32,64},{64,96},{1,33},{33,65},{65,97},{2,34},{34,66},{66,9... | collective-permute-start | bytes 393224 | tf_op jit(solution)/shard_map/ppermute | solution.py:17
  80.5 5.8 %collective-permute-start.3 = (f32[64,16,32]{0,2,1:T(8,128)S(1)}, f32[64,16,32]{0,2,1:T(8,128)S(1)}, u32[]{:S(2)}, u32[]{:S(2)}) collective-permute-start(f32[64,16,32]{0,2,1:T(8,128)S(1)} %get-tuple-element.8), channel_id=1, source_target_pairs={{32,0},{64,32},{96,64},{33,1},{65,33},{97,65},{34,2},{66,34},{98,6... | collective-permute-start | bytes 393224 | tf_op jit(solution)/shard_map/ppermute | solution.py:17
  85.9 99.8 %copy-start.1 = (f32[2,2,2]{2,1,0:T(2,128)S(1)}, f32[2,2,2]{2,1,0:T(2,128)}, u32[]{:S(2)}) copy-start(f32[2,2,2]{2,1,0:T(2,128)} %param.5) | copy-start | bytes 100
  86.5 96.4 %collective-permute-start.4 = (f32[16,32,32]{0,2,1:T(8,128)S(1)}, f32[16,32,32]{0,2,1:T(8,128)S(1)}, u32[]{:S(2)}, u32[]{:S(2)}) collective-permute-start(f32[16,32,32]{0,2,1:T(8,128)S(1)} %fusion.8), channel_id=1, source_target_pairs={{0,128},{128,256},{256,384},{384,512},{512,640},{640,768},{768,896... | collective-permute-start | bytes 196616 | tf_op jit(solution)/shard_map/ppermute | solution.py:17
  90.4 5.5 %collective-permute-start.6 = (f32[8]{0:T(128)S(1)}, f32[8]{0:T(128)S(1)}, u32[]{:S(2)}, u32[]{:S(2)}) collective-permute-start(f32[8]{0:T(128)S(1)} %mul.263), channel_id=1, source_target_pairs={{0,1},{1,0},{2,3},{3,2},{4,5},{5,4},{6,7},{7,6},{8,9},{9,8},{10,11... | collective-permute-start | bytes 104 | tf_op jit(solution)/shard_map/ppermute | solution.py:23
  95.8 9.0 %collective-permute-start.7 = (f32[8]{0:T(128)S(1)}, f32[8]{0:T(128)S(1)}, u32[]{:S(2)}, u32[]{:S(2)}) collective-permute-start(f32[8]{0:T(128)S(1)} %add.196), channel_id=1, source_target_pairs={{0,2},{1,3},{2,0},{3,1},{4,6},{5,7},{6,4},{7,5},{8,10},{9,11},{10,... | collective-permute-start | bytes 104 | tf_op jit(solution)/shard_map/ppermute | solution.py:23
  104.9 10.6 %collective-permute-start.8 = (f32[8]{0:T(128)S(1)}, f32[8]{0:T(128)S(1)}, u32[]{:S(2)}, u32[]{:S(2)}) collective-permute-start(f32[8]{0:T(128)S(1)} %add.197), channel_id=1, source_target_pairs={{0,4},{1,5},{2,6},{3,7},{4,0},{5,1},{6,2},{7,3},{8,12},{9,13},{10,... | collective-permute-start | bytes 104 | tf_op jit(solution)/shard_map/ppermute | solution.py:23
  115.5 17.3 %collective-permute-start.9 = (f32[8]{0:T(128)S(1)}, f32[8]{0:T(128)S(1)}, u32[]{:S(2)}, u32[]{:S(2)}) collective-permute-start(f32[8]{0:T(128)S(1)} %add.199), channel_id=1, source_target_pairs={{0,8},{1,9},{2,10},{3,11},{4,12},{5,13},{6,14},{7,15},{8,0},{9,1},... | collective-permute-start | bytes 104 | tf_op jit(solution)/shard_map/ppermute | solution.py:23
  132.8 24.5 %collective-permute-start.10 = (f32[8]{0:T(128)S(1)}, f32[8]{0:T(128)S(1)}, u32[]{:S(2)}, u32[]{:S(2)}) collective-permute-start(f32[8]{0:T(128)S(1)} %add.201), channel_id=1, source_target_pairs={{0,16},{1,17},{2,18},{3,19},{4,20},{5,21},{6,22},{7,23},{8,24},{9,... | collective-permute-start | bytes 104 | tf_op jit(solution)/shard_map/ppermute | solution.py:23
  157.3 3.0 %collective-permute-start.11 = (f32[8]{0:T(128)S(1)}, f32[8]{0:T(128)S(1)}, u32[]{:S(2)}, u32[]{:S(2)}) collective-permute-start(f32[8]{0:T(128)S(1)} %add.203), channel_id=1, source_target_pairs={{0,32},{1,33},{2,34},{3,35},{4,36},{5,37},{6,38},{7,39},{8,40},{9,... | collective-permute-start | bytes 104 | tf_op jit(solution)/shard_map/ppermute | solution.py:23
  160.3 7.0 %collective-permute-start.12 = (f32[8]{0:T(128)S(1)}, f32[8]{0:T(128)S(1)}, u32[]{:S(2)}, u32[]{:S(2)}) collective-permute-start(f32[8]{0:T(128)S(1)} %add.205), channel_id=1, source_target_pairs={{0,64},{1,65},{2,66},{3,67},{4,68},{5,69},{6,70},{7,71},{8,72},{9,... | collective-permute-start | bytes 104 | tf_op jit(solution)/shard_map/ppermute | solution.py:23
  167.3 5.5 %collective-permute-start.13 = (f32[8]{0:T(128)S(1)}, f32[8]{0:T(128)S(1)}, u32[]{:S(2)}, u32[]{:S(2)}) collective-permute-start(f32[8]{0:T(128)S(1)} %add.207), channel_id=1, source_target_pairs={{0,128},{1,129},{2,130},{3,131},{4,132},{5,133},{6,134},{7,135},{8... | collective-permute-start | bytes 104 | tf_op jit(solution)/shard_map/ppermute | solution.py:23
  172.7 5.5 %collective-permute-start.14 = (f32[8]{0:T(128)S(1)}, f32[8]{0:T(128)S(1)}, u32[]{:S(2)}, u32[]{:S(2)}) collective-permute-start(f32[8]{0:T(128)S(1)} %add.209), channel_id=1, source_target_pairs={{0,256},{1,257},{2,258},{3,259},{4,260},{5,261},{6,262},{7,263},{8... | collective-permute-start | bytes 104 | tf_op jit(solution)/shard_map/ppermute | solution.py:23
  178.2 7.4 %collective-permute-start.15 = (f32[8]{0:T(128)S(1)}, f32[8]{0:T(128)S(1)}, u32[]{:S(2)}, u32[]{:S(2)}) collective-permute-start(f32[8]{0:T(128)S(1)} %add.211), channel_id=1, source_target_pairs={{0,512},{1,513},{2,514},{3,515},{4,516},{5,517},{6,518},{7,519},{8... | collective-permute-start | bytes 104 | tf_op jit(solution)/shard_map/ppermute | solution.py:23
  183.2 13.1 %collective-permute-start.5 = (f32[16,32,32]{0,2,1:T(8,128)S(1)}, f32[16,32,32]{0,2,1:T(8,128)S(1)}, u32[]{:S(2)}, u32[]{:S(2)}) collective-permute-start(f32[16,32,32]{0,2,1:T(8,128)S(1)} %get-tuple-element.10), channel_id=1, source_target_pairs={{128,0},{256,128},{384,256},{512,384},{640,512},{768,640},{896,768... | collective-permute-start | bytes 196616 | tf_op jit(solution)/shard_map/ppermute | solution.py:17
where the time goes:
time: 199 us; the launch traced here: 198 us
  starting transfers between devices  88.5 us (44%)
  waiting for transfers between devices  60.7 us (31%)
  local copies, waits for them, and re-layouts  23 us (12%)
  matrix products  14.8 us (7%)
  other arithmetic  10.8 us (5%)
    ppermute x10, starting transfers between devices, from_partner(): return lax.ppermute(value, axis, pairs)  73.2 us
    ppermute x6, waiting for transfers between devices, from_behind(): return lax.ppermute(block, axis, route)  41.4 us
    ppermute x10, waiting for transfers between devices, from_partner(): return lax.ppermute(value, axis, pairs)  19.2 us
    dot_general x4, local copies, waits for them, and re-layouts, mixed(): return jnp.einsum(form, table, data, preferred_element_type=jnp.float32)  15.7 us
    ppermute x6, starting transfers between devices, from_behind(): return lax.ppermute(block, axis, route)  15.3 us
    dot_general x16, matrix products, mixed(): return jnp.einsum(form, table, data, preferred_element_type=jnp.float32)  13.1 us
  transfers between devices with their start and end apart: 16, of which 14 were waited for; matrix products, arithmetic and copies ran while one was open for 3% of the time, Pallas kernels for 0%

commit v1 on v0

--- a/solution.py
+++ b/solution.py
@@ -81,9 +81,30 @@
     first = lax.slice_in_dim(field, quarter, 2 * quarter, axis=dim)
     second = lax.slice_in_dim(field, 2 * quarter, 3 * quarter, axis=dim)
     high_rim = lax.slice_in_dim(field, 3 * quarter, 4 * quarter, axis=dim)
+    low_rim, high_rim = lax.optimization_barrier((low_rim, high_rim))
     from_left = mover(high_rim, 1)
     from_right = mover(low_rim, -1)
     return jnp.concatenate([first + from_left, second + from_right], axis=dim)
+
+
+def far_sum(flat):
+    nz, ny, nx = (lax.axis_size("gz"), lax.axis_size("gy"), lax.axis_size("gx"))
+    c, b, a = (lax.axis_index("gz"), lax.axis_index("gy"), lax.axis_index("gx"))
+    zslots = lax.iota(jnp.int32, nz)
+    line = lax.psum(jnp.where((zslots == c)[:, None], flat[None, :], 0.0), "gz")
+    ab = a * ny + b
+    abslots = lax.iota(jnp.int32, nx * ny)
+    plane = lax.psum(jnp.where((abslots == ab)[:, None], flat[None, :], 0.0), ("gx", "gy", "gz"))
+    total = jnp.zeros_like(flat)
+    zlevels = nz.bit_length() - 1
+    for level in range(1, zlevels + 1):
+        mask = (zslots >> level) == (c >> level)
+        total = total + jnp.sum(jnp.where(mask[:, None], line, 0.0), axis=0) / math.sqrt(2**level)
+    for level in range(1, (nx * ny).bit_length()):
+        mask = (abslots >> level) == (ab >> level)
+        group = 2 ** (level + zlevels)
+        total = total + jnp.sum(jnp.where(mask[:, None], plane, 0.0), axis=0) / math.sqrt(group)
+    return total
 
 
 def local(vorticity, green_spectrum, coupling):
@@ -99,13 +120,7 @@
     scale = 1.0 / math.sqrt(CB**3)
     coarse = patch.reshape(cx, CB, cy, CB, cz, CB).sum(axis=(1, 3, 5)) * scale
     flat = coarse.reshape(-1)
-    count = lax.axis_size(("gx", "gy", "gz"))
-    levels = count.bit_length() - 1
-    total = jnp.zeros_like(flat)
-    running = flat
-    for bit in range(levels):
-        running = running + from_partner(running, ("gx", "gy", "gz"), bit)
-        total = total + running / math.sqrt(2 ** (bit + 1))
+    total = far_sum(flat)
     far = total.reshape(cx, cy, cz) * coupling
     far_cells = jnp.broadcast_to(far[:, None, :, None, :, None], (cx, CB, cy, CB, cz, CB)).reshape(
         px, py, pz

time: 199 us -> 304 us (1.53)
  the two profiles are of different devices: /device:TPU:6 before, /device:TPU:1 now
where the time goes in v1:
time: 304 us; the launch traced here: 303 us
  blocking collectives  211 us (69%)
  starting transfers between devices  31.1 us (10%)
  waiting for transfers between devices  20.5 us (7%)
  local copies, waits for them, and re-layouts  16.8 us (6%)
  matrix products  15.4 us (5%)
  other arithmetic  7.7 us (3%)
    psum x1, blocking collectives, far_sum(): lax.psum(jnp.where((abslots == ab)[:, None], flat[None, :], 0.0), ('gx',...  152 us
    psum x1, blocking collectives, far_sum(): line = lax.psum(jnp.where((zslots == c)[:, None], flat[None, :], 0.0), 'gz')  58.9 us
    ppermute x6, starting transfers between devices, from_behind(): return lax.ppermute(block, axis, route)  31.1 us
    ppermute x6, waiting for transfers between devices, from_behind(): return lax.ppermute(block, axis, route)  20.5 us
    dot_general x16, matrix products, mixed(): return jnp.einsum(form, table, data, preferred_element_type=jnp.float32)  11.1 us
  transfers between devices with their start and end apart: 6, of which 2 were waited for; matrix products, arithmetic and copies ran while one was open for 2% of the time, Pallas kernels for 0%

profile of v1, /device:TPU:1, one launch (start us, length us, event | category | flops | bytes accessed | tf_op | source)
XLA Modules:
  0.0 303.2 jit_solution(15319508214494610983)
XLA Ops:
  0.0 1.2 convert_reduce_fusion
  4.3 2.2 reshape.121
  12.8 1.6 fusion
  14.3 4.0 %copy.37 = bf16[64,64,64]{0,2,1:T(8,128)(2,1)} copy(bf16[64,64,64]{1,2,0:T(8,128)(2,1)} %fusion) | data formatting | bytes 1048576 | tf_op jit(solution)/shard_map/convert_element_type | solution.py:60
  18.3 3.1 %fusion.51 = f32[64,4096]{0,1} fusion(bf16[64,4096]{0,1:T(8,128)(2,1)} %bitcast.66), kind=kOutput, calls=%fused_computation.90 | convolution fusion | flops 33619968 | bytes 1572864
  21.4 1.6 fusion.1
  23.0 3.3 %copy.40 = bf16[64,64,64]{0,2,1:T(8,128)(2,1)S(1)} copy(bf16[64,64,64]{1,2,0:T(8,128)(2,1)} %fusion.1) | data formatting | bytes 1048576 | tf_op jit(solution)/shard_map/convert_element_type | solution.py:61
  26.9 1.0 copy-done
  28.3 1.1 fusion.164
  29.4 5.2 %collective-permute-start = (f32[64,64,16]{0,2,1:T(8,128)}, f32[64,64,16]{0,2,1:T(8,128)}, u32[]{:S(2)}, u32[]{:S(2)}) collective-permute-start(f32[64,64,16]{0,2,1:T(8,128)} %get-tuple-element.11), channel_id=1, source_target_pairs={{0,1},{1,2},{2,3},{3,4},{4,5},{5,6},{6,7},{7,8},{8,9},{9,10},{10,1... | collective-permute-start | bytes 786440 | tf_op jit(solution)/shard_map/ppermute | solution.py:17
  34.6 1.5 collective-permute-start.1
  36.6 0.9 reduce.5
  37.6 1.4 reshape_reshape.3
  39.8 58.9 %psum.14 = f32[32,8]{0,1:T(8,128)S(1)} all-reduce(f32[32,8]{0,1:T(8,128)S(1)} %get-tuple-element.39), channel_id=1, replica_groups=mesh['gx'=8,'gy'=4,'gz'=32] {'gz'}, use_global_device_ids=true, to_apply=%region_1.2 | all-reduce | flops 256 | bytes 2048 | tf_op jit(solution)/shard_map/psum | solution.py:94
  98.9 1.3 slice_add_fusion
  100.3 18.7 %collective-permute-start.2 = (f32[64,16,32]{0,2,1:T(8,128)S(1)}, f32[64,16,32]{0,2,1:T(8,128)S(1)}, u32[]{:S(2)}, u32[]{:S(2)}) collective-permute-start(f32[64,16,32]{0,2,1:T(8,128)S(1)} %get-tuple-element.13), channel_id=1, source_target_pairs={{0,32},{32,64},{64,96},{1,33},{33,65},{65,97},{2,34},{34,66},{66,9... | collective-permute-start | bytes 393224 | tf_op jit(solution)/shard_map/ppermute | solution.py:17
  119.0 1.9 collective-permute-start.3
  121.0 152.5 %psum.15 = f32[32,8]{0,1:T(8,128)S(1)} all-reduce(f32[32,8]{0,1:T(8,128)S(1)} %get-tuple-element.40), channel_id=1, replica_groups=mesh['gx'=8,'gy'=4,'gz'=32] {'gx','gy','gz'}, use_global_device_ids=true, to_apply=%region_7.8 | all-reduce | flops 256 | bytes 2048 | tf_op jit(solution)/shard_map/psum | solution.py:97
  273.7 1.0 fusion.6
  274.7 2.5 collective-permute-start.4
  277.2 1.3 collective-permute-start.5
  279.2 1.4 reshape.122
  280.6 7.5 %collective-permute-done.4 = f32[16,32,32]{0,2,1:T(8,128)S(1)} collective-permute-done((f32[16,32,32]{0,2,1:T(8,128)}, f32[16,32,32]{0,2,1:T(8,128)S(1)}, u32[]{:S(2)}, u32[]{:S(2)}) %collective-permute-start.4) | collective-permute-done | bytes 65568 | tf_op jit(solution)/shard_map/ppermute | solution.py:17
  288.1 13.0 %collective-permute-done.5 = f32[16,32,32]{0,2,1:T(8,128)S(1)} collective-permute-done((f32[16,32,32]{0,2,1:T(8,128)S(1)}, f32[16,32,32]{0,2,1:T(8,128)S(1)}, u32[]{:S(2)}, u32[]{:S(2)}) %collective-permute-start.5) | collective-permute-done | bytes 65568 | tf_op jit(solution)/shard_map/ppermute | solution.py:17
  (57 shorter events, 14.7 us)
Async XLA Ops:
  26.3 1.6 copy-start
  28.3 8.3 %copy-start.1 = (f32[1,1,1,32768]{3,2,1,0:T(1,128)S(1)}, f32[1,1,1,32768]{3,2,1,0:T(1,128)}, u32[]{:S(2)}) copy-start(f32[1,1,1,32768]{3,2,1,0:T(1,128)} %param.3) | copy-start | bytes 393220
  29.4 69.5 %collective-permute-start = (f32[64,64,16]{0,2,1:T(8,128)}, f32[64,64,16]{0,2,1:T(8,128)}, u32[]{:S(2)}, u32[]{:S(2)}) collective-permute-start(f32[64,64,16]{0,2,1:T(8,128)} %get-tuple-element.11), channel_id=1, source_target_pairs={{0,1},{1,2},{2,3},{3,4},{4,5},{5,6},{6,7},{7,8},{8,9},{9,10},{10,1... | collective-permute-start | bytes 786440 | tf_op jit(solution)/shard_map/ppermute | solution.py:17
  34.6 64.3 %collective-permute-start.1 = (f32[64,64,16]{0,2,1:T(8,128)}, f32[64,64,16]{0,2,1:T(8,128)}, u32[]{:S(2)}, u32[]{:S(2)}) collective-permute-start(f32[64,64,16]{0,2,1:T(8,128)} %get-tuple-element.12), channel_id=1, source_target_pairs={{1,0},{2,1},{3,2},{4,3},{5,4},{6,5},{7,6},{8,7},{9,8},{10,9},{11,1... | collective-permute-start | bytes 786440 | tf_op jit(solution)/shard_map/ppermute | solution.py:17
  100.3 178.3 %copy-start.2 = (f32[2,2,2]{2,1,0:T(2,128)S(1)}, f32[2,2,2]{2,1,0:T(2,128)}, u32[]{:S(2)}) copy-start(f32[2,2,2]{2,1,0:T(2,128)} %param.5) | copy-start | bytes 100
  100.3 173.3 %collective-permute-start.2 = (f32[64,16,32]{0,2,1:T(8,128)S(1)}, f32[64,16,32]{0,2,1:T(8,128)S(1)}, u32[]{:S(2)}, u32[]{:S(2)}) collective-permute-start(f32[64,16,32]{0,2,1:T(8,128)S(1)} %get-tuple-element.13), channel_id=1, source_target_pairs={{0,32},{32,64},{64,96},{1,33},{33,65},{65,97},{2,34},{34,66},{66,9... | collective-permute-start | bytes 393224 | tf_op jit(solution)/shard_map/ppermute | solution.py:17
  119.0 154.6 %collective-permute-start.3 = (f32[64,16,32]{0,2,1:T(8,128)S(1)}, f32[64,16,32]{0,2,1:T(8,128)S(1)}, u32[]{:S(2)}, u32[]{:S(2)}) collective-permute-start(f32[64,16,32]{0,2,1:T(8,128)S(1)} %get-tuple-element.14), channel_id=1, source_target_pairs={{32,0},{64,32},{96,64},{33,1},{65,33},{97,65},{34,2},{66,34},{98,6... | collective-permute-start | bytes 393224 | tf_op jit(solution)/shard_map/ppermute | solution.py:17
  274.7 13.4 %collective-permute-start.4 = (f32[16,32,32]{0,2,1:T(8,128)}, f32[16,32,32]{0,2,1:T(8,128)S(1)}, u32[]{:S(2)}, u32[]{:S(2)}) collective-permute-start(f32[16,32,32]{0,2,1:T(8,128)} %get-tuple-element.15), channel_id=1, source_target_pairs={{0,128},{128,256},{256,384},{384,512},{512,640},{640,768},{768,896... | collective-permute-start | bytes 196616 | tf_op jit(solution)/shard_map/ppermute | solution.py:17
  277.2 23.9 %collective-permute-start.5 = (f32[16,32,32]{0,2,1:T(8,128)S(1)}, f32[16,32,32]{0,2,1:T(8,128)S(1)}, u32[]{:S(2)}, u32[]{:S(2)}) collective-permute-start(f32[16,32,32]{0,2,1:T(8,128)S(1)} %get-tuple-element.16), channel_id=1, source_target_pairs={{128,0},{256,128},{384,256},{512,384},{640,512},{768,640},{896,768... | collective-permute-start | bytes 196616 | tf_op jit(solution)/shard_map/ppermute | solution.py:17

commit v2 on v0

--- a/solution.py
+++ b/solution.py
@@ -81,9 +81,25 @@
     first = lax.slice_in_dim(field, quarter, 2 * quarter, axis=dim)
     second = lax.slice_in_dim(field, 2 * quarter, 3 * quarter, axis=dim)
     high_rim = lax.slice_in_dim(field, 3 * quarter, 4 * quarter, axis=dim)
+    low_rim, high_rim = lax.optimization_barrier((low_rim, high_rim))
     from_left = mover(high_rim, 1)
     from_right = mover(low_rim, -1)
     return jnp.concatenate([first + from_left, second + from_right], axis=dim)
+
+
+def far_sum(flat):
+    axes = ("gx", "gy", "gz")
+    count = lax.axis_size(axes)
+    me = lax.axis_index(axes)
+    slots = lax.iota(jnp.int32, count)
+    table = jnp.where((slots == me)[:, None], flat[None, :], 0.0)
+    table = jnp.concatenate([table, jnp.zeros_like(table)], axis=0)
+    table = lax.psum(table, axes)[:count]
+    total = jnp.zeros_like(flat)
+    for level in range(1, count.bit_length()):
+        mask = (slots >> level) == (me >> level)
+        total = total + jnp.sum(jnp.where(mask[:, None], table, 0.0), axis=0) / math.sqrt(2**level)
+    return total
 
 
 def local(vorticity, green_spectrum, coupling):
@@ -99,13 +115,7 @@
     scale = 1.0 / math.sqrt(CB**3)
     coarse = patch.reshape(cx, CB, cy, CB, cz, CB).sum(axis=(1, 3, 5)) * scale
     flat = coarse.reshape(-1)
-    count = lax.axis_size(("gx", "gy", "gz"))
-    levels = count.bit_length() - 1
-    total = jnp.zeros_like(flat)
-    running = flat
-    for bit in range(levels):
-        running = running + from_partner(running, ("gx", "gy", "gz"), bit)
-        total = total + running / math.sqrt(2 ** (bit + 1))
+    total = far_sum(flat)
     far = total.reshape(cx, cy, cz) * coupling
     far_cells = jnp.broadcast_to(far[:, None, :, None, :, None], (cx, CB, cy, CB, cz, CB)).reshape(
         px, py, pz

time: 199 us -> 923 us (4.64)
  the two profiles are of different devices: /device:TPU:6 before, /device:TPU:1 now
where the time goes in v2:
time: 923 us; the launch traced here: 921 us
  waiting for transfers between devices  840 us (91%)
  starting transfers between devices  25.1 us (3%)
  local copies, waits for them, and re-layouts  18.1 us (2%)
  matrix products  15.4 us (2%)
  between operations  13.8 us (1%)
    psum x1, waiting for transfers between devices, far_sum(): table = lax.psum(table, axes)[:count]  812 us
    ppermute x6, waiting for transfers between devices, from_behind(): return lax.ppermute(block, axis, route)  28 us
    ppermute x6, starting transfers between devices, from_behind(): return lax.ppermute(block, axis, route)  25.1 us
  transfers between devices with their start and end apart: 7, of which 5 were waited for; matrix products, arithmetic and copies ran while one was open for 3% of the time, Pallas kernels for 0%

profile of v2, /device:TPU:1, one launch (start us, length us, event | category | flops | bytes accessed | tf_op | source)
XLA Modules:
  0.0 921.1 jit_solution(16249655811272888281)
XLA Ops:
  7.1 1.9 reduce.5
  8.9 1.4 reshape_reshape.3
  15.2 2.2 reshape.127
  23.7 1.6 fusion
  25.3 4.0 copy.37
  29.2 3.1 fusion.51
  32.4 1.6 fusion.1
  33.9 3.3 copy.40
  37.8 1.0 copy-done
  40.1 4.4 collective-permute-start
  44.5 1.3 collective-permute-start.1
  45.9 5.1 collective-permute-done
  51.8 3.3 collective-permute-done.1
  55.1 1.3 slice_add_fusion
  56.5 10.6 %collective-permute-start.2 = (f32[64,16,32]{0,2,1:T(8,128)S(1)}, f32[64,16,32]{0,2,1:T(8,128)S(1)}, u32[]{:S(2)}, u32[]{:S(2)}) collective-permute-start(f32[64,16,32]{0,2,1:T(8,128)S(1)} %get-tuple-element.13), channel_id=1, source_target_pairs={{0,32},{32,64},{64,96},{1,33},{33,65},{65,97},{2,34},{34,66},{66,9... | collective-permute-start | bytes 393224 | tf_op jit(solution)/shard_map/ppermute | solution.py:17
  67.2 4.3 collective-permute-start.3
  71.5 812.3 %all-reduce.3.cloned.1.call-done = f32[2048,8]{0,1:T(8,128)} async-done(((f32[2048,8]{0,1:T(8,128)}), f32[2048,8]{0,1:T(8,128)}) %all-reduce.3.cloned.1.call-update) | async-done | bytes 65552 | tf_op jit(solution)/shard_map/psum | solution.py:97
  883.8 1.1 select_reduce_fusion.9
  885.0 1.0 fusion.6
  886.0 2.9 collective-permute-start.4
  888.9 1.5 collective-permute-start.5
  891.1 1.4 reshape.128
  892.5 6.6 collective-permute-done.4
  899.1 13.1 %collective-permute-done.5 = f32[16,32,32]{0,2,1:T(8,128)S(1)} collective-permute-done((f32[16,32,32]{0,2,1:T(8,128)S(1)}, f32[16,32,32]{0,2,1:T(8,128)S(1)}, u32[]{:S(2)}, u32[]{:S(2)}) %collective-permute-start.5) | collective-permute-done | bytes 65568 | tf_op jit(solution)/shard_map/ppermute | solution.py:17
  (59 shorter events, 17.1 us)
Async XLA Ops:
  6.5 5.3 copy-start.1
  6.5 877.3 %all-reduce.3.cloned.1.call-start = ((), (), s32[]{:S(2)}) async-start(), calls=%async_computation | async-start | bytes 131072 | tf_op jit(solution)/shard_map/psum | solution.py:97
  37.2 1.6 copy-start
  40.1 10.8 %collective-permute-start = (f32[64,64,16]{0,2,1:T(8,128)}, f32[64,64,16]{0,2,1:T(8,128)S(1)}, u32[]{:S(2)}, u32[]{:S(2)}) collective-permute-start(f32[64,64,16]{0,2,1:T(8,128)} %get-tuple-element.11), channel_id=1, source_target_pairs={{0,1},{1,2},{2,3},{3,4},{4,5},{5,6},{6,7},{7,8},{8,9},{9,10},{10,1... | collective-permute-start | bytes 786440 | tf_op jit(solution)/shard_map/ppermute | solution.py:17
  44.5 10.6 %collective-permute-start.1 = (f32[64,64,16]{0,2,1:T(8,128)S(1)}, f32[64,64,16]{0,2,1:T(8,128)}, u32[]{:S(2)}, u32[]{:S(2)}) collective-permute-start(f32[64,64,16]{0,2,1:T(8,128)S(1)} %get-tuple-element.12), channel_id=1, source_target_pairs={{1,0},{2,1},{3,2},{4,3},{5,4},{6,5},{7,6},{8,7},{9,8},{10,9},{11,1... | collective-permute-start | bytes 786440 | tf_op jit(solution)/shard_map/ppermute | solution.py:17
  51.0 0.8 copy-start.2
  56.5 834.0 %copy-start.3 = (f32[2,2,2]{2,1,0:T(2,128)S(1)}, f32[2,2,2]{2,1,0:T(2,128)}, u32[]{:S(2)}) copy-start(f32[2,2,2]{2,1,0:T(2,128)} %param.5) | copy-start | bytes 100
  56.5 828.4 %collective-permute-start.2 = (f32[64,16,32]{0,2,1:T(8,128)S(1)}, f32[64,16,32]{0,2,1:T(8,128)S(1)}, u32[]{:S(2)}, u32[]{:S(2)}) collective-permute-start(f32[64,16,32]{0,2,1:T(8,128)S(1)} %get-tuple-element.13), channel_id=1, source_target_pairs={{0,32},{32,64},{64,96},{1,33},{33,65},{65,97},{2,34},{34,66},{66,9... | collective-permute-start | bytes 393224 | tf_op jit(solution)/shard_map/ppermute | solution.py:17
  67.2 817.7 %collective-permute-start.3 = (f32[64,16,32]{0,2,1:T(8,128)S(1)}, f32[64,16,32]{0,2,1:T(8,128)S(1)}, u32[]{:S(2)}, u32[]{:S(2)}) collective-permute-start(f32[64,16,32]{0,2,1:T(8,128)S(1)} %get-tuple-element.14), channel_id=1, source_target_pairs={{32,0},{64,32},{96,64},{33,1},{65,33},{97,65},{34,2},{66,34},{98,6... | collective-permute-start | bytes 393224 | tf_op jit(solution)/shard_map/ppermute | solution.py:17
  886.0 13.2 %collective-permute-start.4 = (f32[16,32,32]{0,2,1:T(8,128)}, f32[16,32,32]{0,2,1:T(8,128)S(1)}, u32[]{:S(2)}, u32[]{:S(2)}) collective-permute-start(f32[16,32,32]{0,2,1:T(8,128)} %get-tuple-element.15), channel_id=1, source_target_pairs={{0,128},{128,256},{256,384},{384,512},{512,640},{640,768},{768,896... | collective-permute-start | bytes 196616 | tf_op jit(solution)/shard_map/ppermute | solution.py:17
  888.9 23.3 %collective-permute-start.5 = (f32[16,32,32]{0,2,1:T(8,128)S(1)}, f32[16,32,32]{0,2,1:T(8,128)S(1)}, u32[]{:S(2)}, u32[]{:S(2)}) collective-permute-start(f32[16,32,32]{0,2,1:T(8,128)S(1)} %get-tuple-element.16), channel_id=1, source_target_pairs={{128,0},{256,128},{384,256},{512,384},{640,512},{768,640},{896,768... | collective-permute-start | bytes 196616 | tf_op jit(solution)/shard_map/ppermute | solution.py:17
Sparse Core Ops, SparseCore 0:
  12.8 870.9 all-reduce.2

commit v3 on v0

--- a/solution.py
+++ b/solution.py
@@ -81,9 +81,36 @@
     first = lax.slice_in_dim(field, quarter, 2 * quarter, axis=dim)
     second = lax.slice_in_dim(field, 2 * quarter, 3 * quarter, axis=dim)
     high_rim = lax.slice_in_dim(field, 3 * quarter, 4 * quarter, axis=dim)
+    low_rim, high_rim = lax.optimization_barrier((low_rim, high_rim))
     from_left = mover(high_rim, 1)
     from_right = mover(low_rim, -1)
     return jnp.concatenate([first + from_left, second + from_right], axis=dim)
+
+
+def gather_rows(value, axes):
+    count = lax.axis_size(axes)
+    rows = jnp.broadcast_to(value[None, :], (count, value.shape[0]))
+    return lax.all_to_all(rows, axes, 0, 0, tiled=True)
+
+
+def level_sums(rows, me, first_level, group_of):
+    slots = lax.iota(jnp.int32, rows.shape[0])
+    total = jnp.zeros(rows.shape[1:], rows.dtype)
+    for level in range(1, rows.shape[0].bit_length()):
+        mask = (slots >> level) == (me >> level)
+        total = total + jnp.sum(jnp.where(mask[:, None], rows, 0.0), axis=0) / math.sqrt(group_of(level))
+    return total
+
+
+def far_sum(flat):
+    nz = lax.axis_size("gz")
+    zlevels = nz.bit_length() - 1
+    line = gather_rows(flat, "gz")
+    total = level_sums(line, lax.axis_index("gz"), 1, lambda level: 2**level)
+    line_sum = jnp.sum(line, axis=0)
+    plane = gather_rows(line_sum, ("gx", "gy"))
+    ab = lax.axis_index(("gx", "gy"))
+    return total + level_sums(plane, ab, 1, lambda level: 2 ** (level + zlevels))
 
 
 def local(vorticity, green_spectrum, coupling):
@@ -99,13 +126,7 @@
     scale = 1.0 / math.sqrt(CB**3)
     coarse = patch.reshape(cx, CB, cy, CB, cz, CB).sum(axis=(1, 3, 5)) * scale
     flat = coarse.reshape(-1)
-    count = lax.axis_size(("gx", "gy", "gz"))
-    levels = count.bit_length() - 1
-    total = jnp.zeros_like(flat)
-    running = flat
-    for bit in range(levels):
-        running = running + from_partner(running, ("gx", "gy", "gz"), bit)
-        total = total + running / math.sqrt(2 ** (bit + 1))
+    total = far_sum(flat)
     far = total.reshape(cx, cy, cz) * coupling
     far_cells = jnp.broadcast_to(far[:, None, :, None, :, None], (cx, CB, cy, CB, cz, CB)).reshape(
         px, py, pz

time: 199 us -> 124 us (0.62)
  the two profiles are of different devices: /device:TPU:6 before, /device:TPU:1 now
where the time goes in v3:
time: 124 us; the launch traced here: 123 us
  starting transfers between devices  54 us (44%)
  waiting for transfers between devices  27.2 us (22%)
  local copies, waits for them, and re-layouts  18.5 us (15%)
  matrix products  15.4 us (12%)
  other arithmetic  7.53 us (6%)
    all_to_all x2, starting transfers between devices, gather_rows(): return lax.all_to_all(rows, axes, 0, 0, tiled=True)  38 us
    ppermute x6, waiting for transfers between devices, from_behind(): return lax.ppermute(block, axis, route)  27.2 us
    ppermute x6, starting transfers between devices, from_behind(): return lax.ppermute(block, axis, route)  16 us
    dot_general x16, matrix products, mixed(): return jnp.einsum(form, table, data, preferred_element_type=jnp.float32)  11.1 us
    unnamed x4, matrix products  4.34 us
    convert_element_type x1, local copies, waits for them, and re-layouts, local_box(): new_real = (mixed(form, cosv, real) - mixed(form, sinv, imag)).astype(bf)  3.98 us
    convert_element_type x1, local copies, waits for them, and re-layouts, local_box(): imag = (mixed(form, cosv, imag) + mixed(form, sinv, real)).astype(bf)  3.3 us
  transfers between devices with their start and end apart: 8, of which 5 were waited for; matrix products, arithmetic and copies ran while one was open for 25% of the time, Pallas kernels for 0%

profile of v3, /device:TPU:1, one launch (start us, length us, event | category | flops | bytes accessed | tf_op | source)
XLA Modules:
  0.0 123.1 jit_solution(3408403279268873541)
XLA Ops:
  0.5 1.9 %reduce.6 = f32[32768]{0:T(1024)S(1)} reduce(f32[1,1,1,32768]{3,2,1,0:T(1,128)} %param.3, f32[]{:T(128)} %broadcast.410), dimensions={0,1,2}, to_apply=%param.3.reduce_sub_computation.3 | reduce | bytes 262148 | tf_op args[0]
  2.4 1.4 %reshape_reshape.3 = f32[2,16,2,16,2,16]{5,4,3,2,1,0:T(2,128)S(1)} reshape(f32[32768]{0:T(1024)S(1)} %reduce.6) | data formatting | bytes 262144 | tf_op jit(solution)/shard_map/reshape;reshape | solution.py:127
  5.1 29.5 %all-to-all-start = ((f32[32,1,8]{2,1,0:T(1,128)}), f32[32,1,8]{2,1,0:T(1,128)S(1)}, u32[]{:S(2)}, u32[]{:S(2)}) async-start(f32[32,1,8]{2,1,0:T(1,128)} %broadcast_in_dim.106), calls=%async_computation | async-start | bytes 32768 | tf_op jit(solution)/shard_map/all_to_all | solution.py:93
  38.0 2.0 %reshape.128 = f32[64,64,64]{2,1,0:T(8,128)S(1)} reshape(f32[64,4096]{1,0:T(8,128)} %param.4) | data formatting | bytes 2097152 | tf_op jit(solution)/shard_map/reshape | solution.py:119
  46.3 1.6 %fusion = bf16[64,64,64]{1,2,0:T(8,128)(2,1)} fusion(f32[64,64,64]{2,1,0:T(8,128)S(1)} %fusion.45, bf16[64,64,64]{2,1,0:T(8,128)(2,1)S(1)} %add_convert_fusion.1), kind=kOutput, calls=%fused_computation.14 | convolution fusion | flops 34144256 | bytes 2097152 | tf_op jit(solution)/shard_map/nk,xkz->xnz/dot_general | solution.py:37
  47.9 4.0 %copy.37 = bf16[64,64,64]{0,2,1:T(8,128)(2,1)} copy(bf16[64,64,64]{1,2,0:T(8,128)(2,1)} %fusion) | data formatting | bytes 1048576 | tf_op jit(solution)/shard_map/convert_element_type | solution.py:60
  51.8 3.1 %fusion.51 = f32[64,4096]{0,1} fusion(bf16[64,4096]{0,1:T(8,128)(2,1)} %bitcast.68), kind=kOutput, calls=%fused_computation.100 | convolution fusion | flops 33619968 | bytes 1572864
  55.0 1.6 %fusion.1 = bf16[64,64,64]{1,2,0:T(8,128)(2,1)} fusion(f32[64,64,64]{2,1,0:T(8,128)S(1)} %fusion.41, bf16[64,64,64]{2,1,0:T(8,128)(2,1)S(1)} %subtract_convert_fusion.1), kind=kOutput, calls=%fused_computation.15 | convolution fusion | flops 34144256 | bytes 2097152 | tf_op jit(solution)/shard_map/nk,xkz->xnz/dot_general | solution.py:37
  56.5 3.3 %copy.40 = bf16[64,64,64]{0,2,1:T(8,128)(2,1)S(1)} copy(bf16[64,64,64]{1,2,0:T(8,128)(2,1)} %fusion.1) | data formatting | bytes 1048576 | tf_op jit(solution)/shard_map/convert_element_type | solution.py:61
  60.4 1.0 copy-done
  62.7 3.0 %collective-permute-start = (f32[64,64,16]{0,2,1:T(8,128)}, f32[64,64,16]{0,2,1:T(8,128)S(1)}, u32[]{:S(2)}, u32[]{:S(2)}) collective-permute-start(f32[64,64,16]{0,2,1:T(8,128)} %get-tuple-element.11), channel_id=1, source_target_pairs={{0,1},{1,2},{2,3},{3,4},{4,5},{5,6},{6,7},{7,8},{8,9},{9,10},{10,1... | collective-permute-start | bytes 786440 | tf_op jit(solution)/shard_map/ppermute | solution.py:17
  65.7 1.3 %collective-permute-start.1 = (f32[64,64,16]{0,2,1:T(8,128)S(1)}, f32[64,64,16]{0,2,1:T(8,128)}, u32[]{:S(2)}, u32[]{:S(2)}) collective-permute-start(f32[64,64,16]{0,2,1:T(8,128)S(1)} %get-tuple-element.12), channel_id=1, source_target_pairs={{1,0},{2,1},{3,2},{4,3},{5,4},{6,5},{7,6},{8,7},{9,8},{10,9},{11,1... | collective-permute-start | bytes 786440 | tf_op jit(solution)/shard_map/ppermute | solution.py:17
  67.8 8.6 %all-to-all-start.1 = ((f32[32,1,8]{2,1,0:T(1,128)}), f32[32,1,8]{2,1,0:T(1,128)S(1)}, u32[]{:S(2)}, u32[]{:S(2)}) async-start(f32[32,1,8]{2,1,0:T(1,128)} %broadcast_in_dim.113), calls=%async_computation.1 | async-start | bytes 32768 | tf_op jit(solution)/shard_map/all_to_all | solution.py:93
  77.3 2.5 %collective-permute-done.1 = f32[64,64,16]{0,2,1:T(8,128)} collective-permute-done((f32[64,64,16]{0,2,1:T(8,128)S(1)}, f32[64,64,16]{0,2,1:T(8,128)}, u32[]{:S(2)}, u32[]{:S(2)}) %collective-permute-start.1) | collective-permute-done | bytes 262176 | tf_op jit(solution)/shard_map/ppermute | solution.py:17
  79.7 1.3 %slice_add_fusion = (f32[64,64,16]{0,2,1:T(8,128)S(1)}, f32[64,64,16]{0,2,1:T(8,128)S(1)}) fusion(f32[64,64,16]{0,2,1:T(8,128)} %collective-permute-done.1, f32[64,64,64]{0,2,1:T(8,128)S(1)} %sub.21, f32[64,64,16]{0,2,1:T(8,128)} %copy-done.2), kind=kLoop, calls=%fused_computation.34 | loop fusion | flops 131072 | bytes 1572864 | tf_op jit(solution)/shard_map/add | solution.py:87
  81.1 6.9 %collective-permute-start.2 = (f32[64,16,32]{0,2,1:T(8,128)S(1)}, f32[64,16,32]{0,2,1:T(8,128)S(1)}, u32[]{:S(2)}, u32[]{:S(2)}) collective-permute-start(f32[64,16,32]{0,2,1:T(8,128)S(1)} %get-tuple-element.13), channel_id=1, source_target_pairs={{0,32},{32,64},{64,96},{1,33},{33,65},{65,97},{2,34},{34,66},{66,9... | collective-permute-start | bytes 393224 | tf_op jit(solution)/shard_map/ppermute | solution.py:17
  88.0 1.9 %collective-permute-start.3 = (f32[64,16,32]{0,2,1:T(8,128)S(1)}, f32[64,16,32]{0,2,1:T(8,128)S(1)}, u32[]{:S(2)}, u32[]{:S(2)}) collective-permute-start(f32[64,16,32]{0,2,1:T(8,128)S(1)} %get-tuple-element.14), channel_id=1, source_target_pairs={{32,0},{64,32},{96,64},{33,1},{65,33},{97,65},{34,2},{66,34},{98,6... | collective-permute-start | bytes 393224 | tf_op jit(solution)/shard_map/ppermute | solution.py:17
  90.2 1.1 collective-permute-done.2
  91.3 6.9 %collective-permute-done.3 = f32[64,16,32]{0,2,1:T(8,128)S(1)} collective-permute-done((f32[64,16,32]{0,2,1:T(8,128)S(1)}, f32[64,16,32]{0,2,1:T(8,128)S(1)}, u32[]{:S(2)}, u32[]{:S(2)}) %collective-permute-start.3) | collective-permute-done | bytes 131104 | tf_op jit(solution)/shard_map/ppermute | solution.py:17
  99.3 1.6 %collective-permute-start.4 = (f32[16,32,32]{0,2,1:T(8,128)}, f32[16,32,32]{0,2,1:T(8,128)S(1)}, u32[]{:S(2)}, u32[]{:S(2)}) collective-permute-start(f32[16,32,32]{0,2,1:T(8,128)} %get-tuple-element.15), channel_id=1, source_target_pairs={{0,128},{128,256},{256,384},{384,512},{512,640},{640,768},{768,896... | collective-permute-start | bytes 196616 | tf_op jit(solution)/shard_map/ppermute | solution.py:17
  100.9 1.3 %collective-permute-start.5 = (f32[16,32,32]{0,2,1:T(8,128)S(1)}, f32[16,32,32]{0,2,1:T(8,128)S(1)}, u32[]{:S(2)}, u32[]{:S(2)}) collective-permute-start(f32[16,32,32]{0,2,1:T(8,128)S(1)} %get-tuple-element.16), channel_id=1, source_target_pairs={{128,0},{256,128},{384,256},{512,384},{640,512},{768,640},{896,768... | collective-permute-start | bytes 196616 | tf_op jit(solution)/shard_map/ppermute | solution.py:17
  102.8 1.4 %reshape.129 = f32[1,1,1,32768]{3,2,1,0:T(1,128)S(1)} reshape(f32[2,16,2,16,2,16]{5,4,3,2,1,0:T(2,128)S(1)} %broadcast_in_dim.118) | data formatting | bytes 262144 | tf_op jit(solution)/shard_map/reshape | solution.py:131
  104.3 3.0 %collective-permute-done.4 = f32[16,32,32]{0,2,1:T(8,128)S(1)} collective-permute-done((f32[16,32,32]{0,2,1:T(8,128)}, f32[16,32,32]{0,2,1:T(8,128)S(1)}, u32[]{:S(2)}, u32[]{:S(2)}) %collective-permute-start.4) | collective-permute-done | bytes 65568 | tf_op jit(solution)/shard_map/ppermute | solution.py:17
  107.3 13.7 %collective-permute-done.5 = f32[16,32,32]{0,2,1:T(8,128)S(1)} collective-permute-done((f32[16,32,32]{0,2,1:T(8,128)S(1)}, f32[16,32,32]{0,2,1:T(8,128)S(1)}, u32[]{:S(2)}, u32[]{:S(2)}) %collective-permute-start.5) | collective-permute-done | bytes 65568 | tf_op jit(solution)/shard_map/ppermute | solution.py:17
  (62 shorter events, 18.9 us)
Async XLA Ops:
  0.0 34.6 %copy-start.1 = (f32[1,1,1,32768]{3,2,1,0:T(1,128)S(1)}, f32[1,1,1,32768]{3,2,1,0:T(1,128)}, u32[]{:S(2)}) copy-start(f32[1,1,1,32768]{3,2,1,0:T(1,128)} %param.3) | copy-start | bytes 393220
  5.1 62.0 %all-to-all-start = ((f32[32,1,8]{2,1,0:T(1,128)}), f32[32,1,8]{2,1,0:T(1,128)S(1)}, u32[]{:S(2)}, u32[]{:S(2)}) async-start(f32[32,1,8]{2,1,0:T(1,128)} %broadcast_in_dim.106), calls=%async_computation | async-start | bytes 32768 | tf_op jit(solution)/shard_map/all_to_all | solution.py:93
  59.8 1.6 %copy-start = (f32[64,4096]{0,1:S(1)}, f32[64,4096]{0,1}, u32[]{:S(2)}) copy-start(f32[64,4096]{0,1} %fusion.51) | copy-start | bytes 3145732
  62.7 13.7 %collective-permute-start = (f32[64,64,16]{0,2,1:T(8,128)}, f32[64,64,16]{0,2,1:T(8,128)S(1)}, u32[]{:S(2)}, u32[]{:S(2)}) collective-permute-start(f32[64,64,16]{0,2,1:T(8,128)} %get-tuple-element.11), channel_id=1, source_target_pairs={{0,1},{1,2},{2,3},{3,4},{4,5},{5,6},{6,7},{7,8},{8,9},{9,10},{10,1... | collective-permute-start | bytes 786440 | tf_op jit(solution)/shard_map/ppermute | solution.py:17
  65.7 14.0 %collective-permute-start.1 = (f32[64,64,16]{0,2,1:T(8,128)S(1)}, f32[64,64,16]{0,2,1:T(8,128)}, u32[]{:S(2)}, u32[]{:S(2)}) collective-permute-start(f32[64,64,16]{0,2,1:T(8,128)S(1)} %get-tuple-element.12), channel_id=1, source_target_pairs={{1,0},{2,1},{3,2},{4,3},{5,4},{6,5},{7,6},{8,7},{9,8},{10,9},{11,1... | collective-permute-start | bytes 786440 | tf_op jit(solution)/shard_map/ppermute | solution.py:17
  67.8 22.2 %all-to-all-start.1 = ((f32[32,1,8]{2,1,0:T(1,128)}), f32[32,1,8]{2,1,0:T(1,128)S(1)}, u32[]{:S(2)}, u32[]{:S(2)}) async-start(f32[32,1,8]{2,1,0:T(1,128)} %broadcast_in_dim.113), calls=%async_computation.1 | async-start | bytes 32768 | tf_op jit(solution)/shard_map/all_to_all | solution.py:93
  76.4 0.8 copy-start.2
  81.1 21.2 %copy-start.3 = (f32[2,2,2]{2,1,0:T(2,128)S(1)}, f32[2,2,2]{2,1,0:T(2,128)}, u32[]{:S(2)}) copy-start(f32[2,2,2]{2,1,0:T(2,128)} %param.5) | copy-start | bytes 100
  81.1 10.2 %collective-permute-start.2 = (f32[64,16,32]{0,2,1:T(8,128)S(1)}, f32[64,16,32]{0,2,1:T(8,128)S(1)}, u32[]{:S(2)}, u32[]{:S(2)}) collective-permute-start(f32[64,16,32]{0,2,1:T(8,128)S(1)} %get-tuple-element.13), channel_id=1, source_target_pairs={{0,32},{32,64},{64,96},{1,33},{33,65},{65,97},{2,34},{34,66},{66,9... | collective-permute-start | bytes 393224 | tf_op jit(solution)/shard_map/ppermute | solution.py:17
  88.0 10.2 %collective-permute-start.3 = (f32[64,16,32]{0,2,1:T(8,128)S(1)}, f32[64,16,32]{0,2,1:T(8,128)S(1)}, u32[]{:S(2)}, u32[]{:S(2)}) collective-permute-start(f32[64,16,32]{0,2,1:T(8,128)S(1)} %get-tuple-element.14), channel_id=1, source_target_pairs={{32,0},{64,32},{96,64},{33,1},{65,33},{97,65},{34,2},{66,34},{98,6... | collective-permute-start | bytes 393224 | tf_op jit(solution)/shard_map/ppermute | solution.py:17
  99.3 8.0 %collective-permute-start.4 = (f32[16,32,32]{0,2,1:T(8,128)}, f32[16,32,32]{0,2,1:T(8,128)S(1)}, u32[]{:S(2)}, u32[]{:S(2)}) collective-permute-start(f32[16,32,32]{0,2,1:T(8,128)} %get-tuple-element.15), channel_id=1, source_target_pairs={{0,128},{128,256},{256,384},{384,512},{512,640},{640,768},{768,896... | collective-permute-start | bytes 196616 | tf_op jit(solution)/shard_map/ppermute | solution.py:17
  100.9 20.1 %collective-permute-start.5 = (f32[16,32,32]{0,2,1:T(8,128)S(1)}, f32[16,32,32]{0,2,1:T(8,128)S(1)}, u32[]{:S(2)}, u32[]{:S(2)}) collective-permute-start(f32[16,32,32]{0,2,1:T(8,128)S(1)} %get-tuple-element.16), channel_id=1, source_target_pairs={{128,0},{256,128},{384,256},{512,384},{640,512},{768,640},{896,768... | collective-permute-start | bytes 196616 | tf_op jit(solution)/shard_map/ppermute | solution.py:17

commit v4 on v3

--- a/solution.py
+++ b/solution.py
@@ -4,6 +4,7 @@
 import jax.numpy as jnp
 from jax import lax
 from jax.sharding import PartitionSpec as P
+
 
 PX = 32
 PY = 32
@@ -15,12 +16,6 @@
     devices = range(lax.axis_size(axis))
     route = [(i - distance, i) for i in devices if i - distance in devices]
     return lax.ppermute(block, axis, route)
-
-
-def from_partner(value, axis, apart):
-    mask = 2**apart
-    pairs = [(source, source ^ mask) for source in range(lax.axis_size(axis))]
-    return lax.ppermute(value, axis, pairs)
 
 
 def angle_tables(count_out, count_in, offset, length, factor):
@@ -93,7 +88,7 @@
     return lax.all_to_all(rows, axes, 0, 0, tiled=True)
 
 
-def level_sums(rows, me, first_level, group_of):
+def level_sums(rows, me, group_of):
     slots = lax.iota(jnp.int32, rows.shape[0])
     total = jnp.zeros(rows.shape[1:], rows.dtype)
     for level in range(1, rows.shape[0].bit_length()):
@@ -106,11 +101,11 @@
     nz = lax.axis_size("gz")
     zlevels = nz.bit_length() - 1
     line = gather_rows(flat, "gz")
-    total = level_sums(line, lax.axis_index("gz"), 1, lambda level: 2**level)
+    total = level_sums(line, lax.axis_index("gz"), lambda level: 2**level)
     line_sum = jnp.sum(line, axis=0)
     plane = gather_rows(line_sum, ("gx", "gy"))
     ab = lax.axis_index(("gx", "gy"))
-    return total + level_sums(plane, ab, 1, lambda level: 2 ** (level + zlevels))
+    return total + level_sums(plane, ab, lambda level: 2 ** (level + zlevels))
 
 
 def local(vorticity, green_spectrum, coupling):

time: 124 us -> 124 us (level)
  no operation moved by 1% of the time
where the time goes in v4:
time: 124 us; the launch traced here: 123 us
  starting transfers between devices  54 us (44%)
  waiting for transfers between devices  27.2 us (22%)
  local copies, waits for them, and re-layouts  18.5 us (15%)
  matrix products  15.4 us (12%)
  other arithmetic  7.53 us (6%)
    all_to_all x2, starting transfers between devices, gather_rows(): return lax.all_to_all(rows, axes, 0, 0, tiled=True)  38 us
    ppermute x6, waiting for transfers between devices, from_behind(): return lax.ppermute(block, axis, route)  27.2 us
    ppermute x6, starting transfers between devices, from_behind(): return lax.ppermute(block, axis, route)  16 us
    dot_general x16, matrix products, mixed(): return jnp.einsum(form, table, data, preferred_element_type=jnp.float32)  11.1 us
    unnamed x4, matrix products  4.34 us
    convert_element_type x1, local copies, waits for them, and re-layouts, local_box(): new_real = (mixed(form, cosv, real) - mixed(form, sinv, imag)).astype(bf)  3.98 us
    convert_element_type x1, local copies, waits for them, and re-layouts, local_box(): imag = (mixed(form, cosv, imag) + mixed(form, sinv, real)).astype(bf)  3.3 us
  transfers between devices with their start and end apart: 8, of which 5 were waited for; matrix products, arithmetic and copies ran while one was open for 25% of the time, Pallas kernels for 0%

profile of v4, /device:TPU:1, one launch (start us, length us, event | category | flops | bytes accessed | tf_op | source)
XLA Modules:
  0.0 123.1 jit_solution(3408403279268873541)
XLA Ops:
  0.5 1.9 %reduce.6 = f32[32768]{0:T(1024)S(1)} reduce(f32[1,1,1,32768]{3,2,1,0:T(1,128)} %param.3, f32[]{:T(128)} %broadcast.410), dimensions={0,1,2}, to_apply=%param.3.reduce_sub_computation.3 | reduce | bytes 262148 | tf_op args[0]
  2.4 1.4 %reshape_reshape.3 = f32[2,16,2,16,2,16]{5,4,3,2,1,0:T(2,128)S(1)} reshape(f32[32768]{0:T(1024)S(1)} %reduce.6) | data formatting | bytes 262144 | tf_op jit(solution)/shard_map/reshape;reshape | solution.py:122
  5.1 29.5 %all-to-all-start = ((f32[32,1,8]{2,1,0:T(1,128)}), f32[32,1,8]{2,1,0:T(1,128)S(1)}, u32[]{:S(2)}, u32[]{:S(2)}) async-start(f32[32,1,8]{2,1,0:T(1,128)} %broadcast_in_dim.106), calls=%async_computation | async-start | bytes 32768 | tf_op jit(solution)/shard_map/all_to_all | solution.py:88
  38.0 2.0 %reshape.128 = f32[64,64,64]{2,1,0:T(8,128)S(1)} reshape(f32[64,4096]{1,0:T(8,128)} %param.4) | data formatting | bytes 2097152 | tf_op jit(solution)/shard_map/reshape | solution.py:114
  46.3 1.6 %fusion = bf16[64,64,64]{1,2,0:T(8,128)(2,1)} fusion(f32[64,64,64]{2,1,0:T(8,128)S(1)} %fusion.45, bf16[64,64,64]{2,1,0:T(8,128)(2,1)S(1)} %add_convert_fusion.1), kind=kOutput, calls=%fused_computation.14 | convolution fusion | flops 34144256 | bytes 2097152 | tf_op jit(solution)/shard_map/nk,xkz->xnz/dot_general | solution.py:32
  47.9 4.0 %copy.37 = bf16[64,64,64]{0,2,1:T(8,128)(2,1)} copy(bf16[64,64,64]{1,2,0:T(8,128)(2,1)} %fusion) | data formatting | bytes 1048576 | tf_op jit(solution)/shard_map/convert_element_type | solution.py:55
  51.8 3.1 %fusion.51 = f32[64,4096]{0,1} fusion(bf16[64,4096]{0,1:T(8,128)(2,1)} %bitcast.68), kind=kOutput, calls=%fused_computation.100 | convolution fusion | flops 33619968 | bytes 1572864
  55.0 1.6 %fusion.1 = bf16[64,64,64]{1,2,0:T(8,128)(2,1)} fusion(f32[64,64,64]{2,1,0:T(8,128)S(1)} %fusion.41, bf16[64,64,64]{2,1,0:T(8,128)(2,1)S(1)} %subtract_convert_fusion.1), kind=kOutput, calls=%fused_computation.15 | convolution fusion | flops 34144256 | bytes 2097152 | tf_op jit(solution)/shard_map/nk,xkz->xnz/dot_general | solution.py:32
  56.5 3.3 %copy.40 = bf16[64,64,64]{0,2,1:T(8,128)(2,1)S(1)} copy(bf16[64,64,64]{1,2,0:T(8,128)(2,1)} %fusion.1) | data formatting | bytes 1048576 | tf_op jit(solution)/shard_map/convert_element_type | solution.py:56
  60.4 1.0 copy-done
  62.7 3.0 %collective-permute-start = (f32[64,64,16]{0,2,1:T(8,128)}, f32[64,64,16]{0,2,1:T(8,128)S(1)}, u32[]{:S(2)}, u32[]{:S(2)}) collective-permute-start(f32[64,64,16]{0,2,1:T(8,128)} %get-tuple-element.11), channel_id=1, source_target_pairs={{0,1},{1,2},{2,3},{3,4},{4,5},{5,6},{6,7},{7,8},{8,9},{9,10},{10,1... | collective-permute-start | bytes 786440 | tf_op jit(solution)/shard_map/ppermute | solution.py:18
  65.7 1.3 %collective-permute-start.1 = (f32[64,64,16]{0,2,1:T(8,128)S(1)}, f32[64,64,16]{0,2,1:T(8,128)}, u32[]{:S(2)}, u32[]{:S(2)}) collective-permute-start(f32[64,64,16]{0,2,1:T(8,128)S(1)} %get-tuple-element.12), channel_id=1, source_target_pairs={{1,0},{2,1},{3,2},{4,3},{5,4},{6,5},{7,6},{8,7},{9,8},{10,9},{11,1... | collective-permute-start | bytes 786440 | tf_op jit(solution)/shard_map/ppermute | solution.py:18
  67.8 8.6 %all-to-all-start.1 = ((f32[32,1,8]{2,1,0:T(1,128)}), f32[32,1,8]{2,1,0:T(1,128)S(1)}, u32[]{:S(2)}, u32[]{:S(2)}) async-start(f32[32,1,8]{2,1,0:T(1,128)} %broadcast_in_dim.113), calls=%async_computation.1 | async-start | bytes 32768 | tf_op jit(solution)/shard_map/all_to_all | solution.py:88
  77.3 2.5 %collective-permute-done.1 = f32[64,64,16]{0,2,1:T(8,128)} collective-permute-done((f32[64,64,16]{0,2,1:T(8,128)S(1)}, f32[64,64,16]{0,2,1:T(8,128)}, u32[]{:S(2)}, u32[]{:S(2)}) %collective-permute-start.1) | collective-permute-done | bytes 262176 | tf_op jit(solution)/shard_map/ppermute | solution.py:18
  79.7 1.3 %slice_add_fusion = (f32[64,64,16]{0,2,1:T(8,128)S(1)}, f32[64,64,16]{0,2,1:T(8,128)S(1)}) fusion(f32[64,64,16]{0,2,1:T(8,128)} %collective-permute-done.1, f32[64,64,64]{0,2,1:T(8,128)S(1)} %sub.21, f32[64,64,16]{0,2,1:T(8,128)} %copy-done.2), kind=kLoop, calls=%fused_computation.34 | loop fusion | flops 131072 | bytes 1572864 | tf_op jit(solution)/shard_map/add | solution.py:82
  81.1 6.9 %collective-permute-start.2 = (f32[64,16,32]{0,2,1:T(8,128)S(1)}, f32[64,16,32]{0,2,1:T(8,128)S(1)}, u32[]{:S(2)}, u32[]{:S(2)}) collective-permute-start(f32[64,16,32]{0,2,1:T(8,128)S(1)} %get-tuple-element.13), channel_id=1, source_target_pairs={{0,32},{32,64},{64,96},{1,33},{33,65},{65,97},{2,34},{34,66},{66,9... | collective-permute-start | bytes 393224 | tf_op jit(solution)/shard_map/ppermute | solution.py:18
  88.0 1.9 %collective-permute-start.3 = (f32[64,16,32]{0,2,1:T(8,128)S(1)}, f32[64,16,32]{0,2,1:T(8,128)S(1)}, u32[]{:S(2)}, u32[]{:S(2)}) collective-permute-start(f32[64,16,32]{0,2,1:T(8,128)S(1)} %get-tuple-element.14), channel_id=1, source_target_pairs={{32,0},{64,32},{96,64},{33,1},{65,33},{97,65},{34,2},{66,34},{98,6... | collective-permute-start | bytes 393224 | tf_op jit(solution)/shard_map/ppermute | solution.py:18
  90.2 1.1 collective-permute-done.2
  91.3 6.9 %collective-permute-done.3 = f32[64,16,32]{0,2,1:T(8,128)S(1)} collective-permute-done((f32[64,16,32]{0,2,1:T(8,128)S(1)}, f32[64,16,32]{0,2,1:T(8,128)S(1)}, u32[]{:S(2)}, u32[]{:S(2)}) %collective-permute-start.3) | collective-permute-done | bytes 131104 | tf_op jit(solution)/shard_map/ppermute | solution.py:18
  99.3 1.6 %collective-permute-start.4 = (f32[16,32,32]{0,2,1:T(8,128)}, f32[16,32,32]{0,2,1:T(8,128)S(1)}, u32[]{:S(2)}, u32[]{:S(2)}) collective-permute-start(f32[16,32,32]{0,2,1:T(8,128)} %get-tuple-element.15), channel_id=1, source_target_pairs={{0,128},{128,256},{256,384},{384,512},{512,640},{640,768},{768,896... | collective-permute-start | bytes 196616 | tf_op jit(solution)/shard_map/ppermute | solution.py:18
  100.9 1.3 %collective-permute-start.5 = (f32[16,32,32]{0,2,1:T(8,128)S(1)}, f32[16,32,32]{0,2,1:T(8,128)S(1)}, u32[]{:S(2)}, u32[]{:S(2)}) collective-permute-start(f32[16,32,32]{0,2,1:T(8,128)S(1)} %get-tuple-element.16), channel_id=1, source_target_pairs={{128,0},{256,128},{384,256},{512,384},{640,512},{768,640},{896,768... | collective-permute-start | bytes 196616 | tf_op jit(solution)/shard_map/ppermute | solution.py:18
  102.8 1.4 %reshape.129 = f32[1,1,1,32768]{3,2,1,0:T(1,128)S(1)} reshape(f32[2,16,2,16,2,16]{5,4,3,2,1,0:T(2,128)S(1)} %broadcast_in_dim.118) | data formatting | bytes 262144 | tf_op jit(solution)/shard_map/reshape | solution.py:126
  104.3 3.0 %collective-permute-done.4 = f32[16,32,32]{0,2,1:T(8,128)S(1)} collective-permute-done((f32[16,32,32]{0,2,1:T(8,128)}, f32[16,32,32]{0,2,1:T(8,128)S(1)}, u32[]{:S(2)}, u32[]{:S(2)}) %collective-permute-start.4) | collective-permute-done | bytes 65568 | tf_op jit(solution)/shard_map/ppermute | solution.py:18
  107.3 13.7 %collective-permute-done.5 = f32[16,32,32]{0,2,1:T(8,128)S(1)} collective-permute-done((f32[16,32,32]{0,2,1:T(8,128)S(1)}, f32[16,32,32]{0,2,1:T(8,128)S(1)}, u32[]{:S(2)}, u32[]{:S(2)}) %collective-permute-start.5) | collective-permute-done | bytes 65568 | tf_op jit(solution)/shard_map/ppermute | solution.py:18
  (62 shorter events, 18.9 us)
Async XLA Ops:
  0.0 34.6 %copy-start.1 = (f32[1,1,1,32768]{3,2,1,0:T(1,128)S(1)}, f32[1,1,1,32768]{3,2,1,0:T(1,128)}, u32[]{:S(2)}) copy-start(f32[1,1,1,32768]{3,2,1,0:T(1,128)} %param.3) | copy-start | bytes 393220
  5.1 62.0 %all-to-all-start = ((f32[32,1,8]{2,1,0:T(1,128)}), f32[32,1,8]{2,1,0:T(1,128)S(1)}, u32[]{:S(2)}, u32[]{:S(2)}) async-start(f32[32,1,8]{2,1,0:T(1,128)} %broadcast_in_dim.106), calls=%async_computation | async-start | bytes 32768 | tf_op jit(solution)/shard_map/all_to_all | solution.py:88
  59.8 1.6 %copy-start = (f32[64,4096]{0,1:S(1)}, f32[64,4096]{0,1}, u32[]{:S(2)}) copy-start(f32[64,4096]{0,1} %fusion.51) | copy-start | bytes 3145732
  62.7 13.7 %collective-permute-start = (f32[64,64,16]{0,2,1:T(8,128)}, f32[64,64,16]{0,2,1:T(8,128)S(1)}, u32[]{:S(2)}, u32[]{:S(2)}) collective-permute-start(f32[64,64,16]{0,2,1:T(8,128)} %get-tuple-element.11), channel_id=1, source_target_pairs={{0,1},{1,2},{2,3},{3,4},{4,5},{5,6},{6,7},{7,8},{8,9},{9,10},{10,1... | collective-permute-start | bytes 786440 | tf_op jit(solution)/shard_map/ppermute | solution.py:18
  65.7 14.0 %collective-permute-start.1 = (f32[64,64,16]{0,2,1:T(8,128)S(1)}, f32[64,64,16]{0,2,1:T(8,128)}, u32[]{:S(2)}, u32[]{:S(2)}) collective-permute-start(f32[64,64,16]{0,2,1:T(8,128)S(1)} %get-tuple-element.12), channel_id=1, source_target_pairs={{1,0},{2,1},{3,2},{4,3},{5,4},{6,5},{7,6},{8,7},{9,8},{10,9},{11,1... | collective-permute-start | bytes 786440 | tf_op jit(solution)/shard_map/ppermute | solution.py:18
  67.8 22.2 %all-to-all-start.1 = ((f32[32,1,8]{2,1,0:T(1,128)}), f32[32,1,8]{2,1,0:T(1,128)S(1)}, u32[]{:S(2)}, u32[]{:S(2)}) async-start(f32[32,1,8]{2,1,0:T(1,128)} %broadcast_in_dim.113), calls=%async_computation.1 | async-start | bytes 32768 | tf_op jit(solution)/shard_map/all_to_all | solution.py:88
  76.4 0.8 copy-start.2
  81.1 21.2 %copy-start.3 = (f32[2,2,2]{2,1,0:T(2,128)S(1)}, f32[2,2,2]{2,1,0:T(2,128)}, u32[]{:S(2)}) copy-start(f32[2,2,2]{2,1,0:T(2,128)} %param.5) | copy-start | bytes 100
  81.1 10.2 %collective-permute-start.2 = (f32[64,16,32]{0,2,1:T(8,128)S(1)}, f32[64,16,32]{0,2,1:T(8,128)S(1)}, u32[]{:S(2)}, u32[]{:S(2)}) collective-permute-start(f32[64,16,32]{0,2,1:T(8,128)S(1)} %get-tuple-element.13), channel_id=1, source_target_pairs={{0,32},{32,64},{64,96},{1,33},{33,65},{65,97},{2,34},{34,66},{66,9... | collective-permute-start | bytes 393224 | tf_op jit(solution)/shard_map/ppermute | solution.py:18
  88.0 10.2 %collective-permute-start.3 = (f32[64,16,32]{0,2,1:T(8,128)S(1)}, f32[64,16,32]{0,2,1:T(8,128)S(1)}, u32[]{:S(2)}, u32[]{:S(2)}) collective-permute-start(f32[64,16,32]{0,2,1:T(8,128)S(1)} %get-tuple-element.14), channel_id=1, source_target_pairs={{32,0},{64,32},{96,64},{33,1},{65,33},{97,65},{34,2},{66,34},{98,6... | collective-permute-start | bytes 393224 | tf_op jit(solution)/shard_map/ppermute | solution.py:18
  99.3 8.0 %collective-permute-start.4 = (f32[16,32,32]{0,2,1:T(8,128)}, f32[16,32,32]{0,2,1:T(8,128)S(1)}, u32[]{:S(2)}, u32[]{:S(2)}) collective-permute-start(f32[16,32,32]{0,2,1:T(8,128)} %get-tuple-element.15), channel_id=1, source_target_pairs={{0,128},{128,256},{256,384},{384,512},{512,640},{640,768},{768,896... | collective-permute-start | bytes 196616 | tf_op jit(solution)/shard_map/ppermute | solution.py:18
  100.9 20.1 %collective-permute-start.5 = (f32[16,32,32]{0,2,1:T(8,128)S(1)}, f32[16,32,32]{0,2,1:T(8,128)S(1)}, u32[]{:S(2)}, u32[]{:S(2)}) collective-permute-start(f32[16,32,32]{0,2,1:T(8,128)S(1)} %get-tuple-element.16), channel_id=1, source_target_pairs={{128,0},{256,128},{384,256},{512,384},{640,512},{768,640},{896,768... | collective-permute-start | bytes 196616 | tf_op jit(solution)/shard_map/ppermute | solution.py:18

commit v5 on v3

--- a/solution.py
+++ b/solution.py
@@ -37,6 +37,20 @@
     return jnp.einsum(form, table, data, preferred_element_type=jnp.float32)
 
 
+def forward_stage(form, table_cos, table_sin, parts):
+    table = jnp.concatenate([table_cos.T, table_sin.T], axis=1)
+    half = table_cos.shape[0]
+    prods = [jnp.einsum(form, part, table, preferred_element_type=jnp.float32) for part in parts]
+    return [(prod[..., :half], prod[..., half:]) for prod in prods]
+
+
+def inverse_stage(form, table_cos, table_sin, parts):
+    table = jnp.concatenate([table_cos, table_sin], axis=0)
+    half = table_cos.shape[0]
+    prods = [jnp.einsum(form, table, part, preferred_element_type=jnp.float32) for part in parts]
+    return [(prod[:half], prod[half:]) for prod in prods]
+
+
 def local_box(patch, green_spectrum):
     bf = jnp.bfloat16
     px, py, pz = patch.shape
@@ -45,22 +59,21 @@
     cosx, sinx = angle_tables(bx, px, px // 2, bx, 1.0)
     cosy, siny = angle_tables(by, py, py // 2, by, 1.0)
     cosz, sinz = angle_tables(bz, pz, pz // 2, bz, 1.0)
-    real = mixed("kn,nyz->kyz", cosx, wb).astype(bf)
-    imag = (-mixed("kn,nyz->kyz", sinx, wb)).astype(bf)
-    for form, cosv, sinv in (("ky,xyz->xkz", cosy, siny), ("kz,xyz->xyk", cosz, sinz)):
-        new_real = (mixed(form, cosv, real) + mixed(form, sinv, imag)).astype(bf)
-        imag = (mixed(form, cosv, imag) - mixed(form, sinv, real)).astype(bf)
-        real = new_real
+    ((rc, rs),) = forward_stage("xyz,xm->yzm", cosx, -sinx, (wb,))
+    real, imag = rc.astype(bf), rs.astype(bf)
+    for form, cosv, sinv in (("yzk,ym->zkm", cosy, siny), ("zab,zm->abm", cosz, sinz)):
+        (rc, rs), (ic, is_) = forward_stage(form, cosv, sinv, (real, imag))
+        real, imag = (rc + is_).astype(bf), (ic - rs).astype(bf)
     real = (real.astype(jnp.float32) * green_spectrum).astype(bf)
     imag = (imag.astype(jnp.float32) * green_spectrum).astype(bf)
     icosz, isinz = angle_tables(bz, bz, 0, bz, 1.0 / bz)
     icosy, isiny = angle_tables(by, by, 0, by, 1.0 / by)
     icosx, isinx = angle_tables(bx, bx, 0, bx, 1.0 / bx)
-    for form, cosv, sinv in (("nk,xyk->xyn", icosz, isinz), ("nk,xkz->xnz", icosy, isiny)):
-        new_real = (mixed(form, cosv, real) - mixed(form, sinv, imag)).astype(bf)
-        imag = (mixed(form, cosv, imag) + mixed(form, sinv, real)).astype(bf)
-        real = new_real
-    return mixed("nk,kyz->nyz", icosx, real) - mixed("nk,kyz->nyz", isinx, imag)
+    for cosv, sinv in ((icosz, isinz), (icosy, isiny)):
+        (rc, rs), (ic, is_) = inverse_stage("mk,abk->mab", cosv, sinv, (real, imag))
+        real, imag = (rc - is_).astype(bf), (ic + rs).astype(bf)
+    (rc, rs), (ic, is_) = inverse_stage("mk,abk->mab", icosx, isinx, (real, imag))
+    return rc - is_
 
 
 def move_x(part, step):

time: 124 us -> 147 us (1.19)
  waiting for transfers between devices: 27.2 us -> 45.5 us
  other arithmetic: 7.53 us -> 11.6 us
  starting transfers between devices: 54 us -> 55.6 us
    all_to_all x2, waiting for transfers between devices: 0.01 us -> 21.1 us  [gather_rows(): return lax.all_to_all(rows, axes, 0, 0, tiled=True)]
    convert_element_type x2 -> x5, other arithmetic: 0.09 us -> 4.25 us  [the longest x2 3.32 us: local_box(): real, imag = ((rc - is_).astype(bf), (ic + rs).astype(bf))]
    unnamed x4 -> x1, matrix products: 4.34 us -> 0.27 us
    dot_general x16 -> x10, matrix products: 11.1 us -> 14.1 us  [the longest x6 10.9 us: inverse_stage(): jnp.einsum(form, table, part, preferred_element_type=jnp.float32)]
    ppermute x6, waiting for transfers between devices: 27.2 us -> 24.4 us  [from_behind(): return lax.ppermute(block, axis, route)]
    convert_element_type x2 -> x4, local copies, waits for them, and re-layouts: 7.28 us -> 9.14 us  [local_box(): real, imag = ((rc - is_).astype(bf), (ic + rs).astype(bf))]
  transfers between devices with their start and end apart: 8 -> 8, of which waited for: 5 -> 5; matrix products, arithmetic and copies ran while one was open for 25% -> 6% of each run, Pallas kernels for 0% -> 0%
where the time goes in v5:
time: 147 us
  starting transfers between devices  55.6 us (38%)
  waiting for transfers between devices  45.5 us (31%)
  local copies, waits for them, and re-layouts  19.4 us (13%)
  matrix products  14.4 us (10%)
  other arithmetic  11.6 us (8%)
    all_to_all x2, starting transfers between devices, gather_rows(): return lax.all_to_all(rows, axes, 0, 0, tiled=True)  39.1 us
    ppermute x6, waiting for transfers between devices, from_behind(): return lax.ppermute(block, axis, route)  24.4 us
    all_to_all x2, waiting for transfers between devices, gather_rows(): return lax.all_to_all(rows, axes, 0, 0, tiled=True)  21.1 us
    ppermute x6, starting transfers between devices, from_behind(): return lax.ppermute(block, axis, route)  16.5 us
    dot_general x6, matrix products, inverse_stage(): jnp.einsum(form, table, part, preferred_element_type=jnp.float32)  10.9 us
    convert_element_type x4, local copies, waits for them, and re-layouts, local_box(): real, imag = ((rc - is_).astype(bf), (ic + rs).astype(bf))  9.14 us
    convert_element_type x2, other arithmetic, local_box(): real, imag = ((rc - is_).astype(bf), (ic + rs).astype(bf))  3.32 us
    dot_general x4, matrix products, forward_stage(): jnp.einsum(form, part, table, preferred_element_type=jnp.float32)  3.16 us
  transfers between devices with their start and end apart: 8, of which 5 were waited for; matrix products, arithmetic and copies ran while one was open for 6% of the time, Pallas kernels for 0%

profile of v5, /device:TPU:1, one launch (start us, length us, event | category | flops | bytes accessed | tf_op | source)
XLA Modules:
  0.0 146.8 jit_solution(13750975468555273956)
XLA Ops:
  4.7 1.9 %fusion.19 = f32[64,64,128]{2,1,0:T(8,128)} fusion(bf16[32,128,1]{1,0,2:T(8,128)(2,1)S(1)} %maximum_bitcast_fusion.1, bf16[32,64,64]{2,1,0:T(8,128)(2,1)S(1)} %get-tuple-element.35), kind=kOutput, calls=%fused_computation.44 | convolution fusion | flops 33554432 | bytes 2367488 | tf_op jit(solution)/shard_map/zab,zm->abm/dot_general | solution.py:43
  6.6 2.2 %reshape.128 = f32[64,64,64]{2,1,0:T(8,128)} reshape(f32[64,4096]{1,0:T(8,128)S(1)} %copy-done.2) | data formatting | bytes 2097152 | tf_op jit(solution)/shard_map/reshape | solution.py:132
  8.9 3.1 %fusion.6 = f32[128,64,64]{0,2,1:T(8,128)S(1)} fusion(bf16[128,64,1]{0,1,2:T(8,128)(2,1)S(1)} %maximum_bitcast_fusion, f32[64,64,64]{2,1,0:T(8,128)} %reshape.128, f32[64,64,128]{2,1,0:T(8,128)S(1)} %fusion.17, f32[64,64,128]{2,1,0:T(8,128)} %fusion.19), kind=kOutput, calls=%fused_computation.21 | convolution fusion | flops 68419584 | bytes 7356416 | tf_op jit(solution)/shard_map/mk,abk->mab/dot_general | solution.py:50
  14.3 2.5 %copy.29 = bf16[64,64,64]{2,1,0:T(8,128)(2,1)} copy(bf16[64,64,64]{0,2,1:T(8,128)(2,1)S(1)} %get-tuple-element.30) | data formatting | bytes 1048576 | tf_op jit(solution)/shard_map/convert_element_type | solution.py:74
  16.8 1.6 %fusion.64 = f32[128,64,64]{0,2,1:T(8,128)S(1)} fusion(bf16[128,64,1]{0,1,2:T(8,128)(2,1)S(1)} %maximum_bitcast_fusion, bf16[64,64,64]{2,1,0:T(8,128)(2,1)} %copy.29), kind=kOutput, calls=%fused_computation.122 | convolution fusion | flops 67108864 | bytes 2637824 | tf_op jit(solution)/shard_map/mk,abk->mab/dot_general | solution.py:50
  18.4 2.4 %copy.28 = bf16[64,64,64]{2,1,0:T(8,128)(2,1)} copy(bf16[64,64,64]{0,2,1:T(8,128)(2,1)S(1)} %get-tuple-element.29) | data formatting | bytes 1048576 | tf_op jit(solution)/shard_map/convert_element_type | solution.py:74
  20.8 1.6 %fusion.63 = f32[128,64,64]{0,2,1:T(8,128)S(1)} fusion(bf16[128,64,1]{0,1,2:T(8,128)(2,1)S(1)} %maximum_bitcast_fusion, bf16[64,64,64]{2,1,0:T(8,128)(2,1)} %copy.28), kind=kOutput, calls=%fused_computation.121 | convolution fusion | flops 67108864 | bytes 2637824 | tf_op jit(solution)/shard_map/mk,abk->mab/dot_general | solution.py:50
  22.4 2.1 %fusion = (bf16[64,64,64]{0,2,1:T(8,128)(2,1)S(1)}, bf16[64,64,64]{0,2,1:T(8,128)(2,1)}) fusion(f32[128,64,64]{0,2,1:T(8,128)S(1)} %fusion.63, f32[128,64,64]{0,2,1:T(8,128)S(1)} %fusion.64), kind=kLoop, calls=%fused_computation.1 | loop fusion | flops 1048576 | bytes 5242880 | tf_op jit(solution)/shard_map/convert_element_type | solution.py:74
  24.6 2.6 %copy.30 = bf16[64,64,64]{2,1,0:T(8,128)(2,1)S(1)} copy(bf16[64,64,64]{0,2,1:T(8,128)(2,1)} %get-tuple-element.28) | data formatting | bytes 1048576 | tf_op jit(solution)/shard_map/convert_element_type | solution.py:74
  27.2 1.8 %fusion.40 = f32[64,64,64]{0,2,1:T(8,128)} fusion(bf16[64,64,64]{2,1,0:T(8,128)(2,1)S(1)} %copy.30, bf16[128,64,1]{0,1,2:T(8,128)(2,1)S(1)} %maximum_bitcast_fusion), kind=kOutput, calls=%fused_computation.76 | convolution fusion | flops 33554432 | bytes 1589248 | tf_op jit(solution)/shard_map/mk,abk->mab/dot_general | solution.py:50
  29.0 1.6 %copy.31 = bf16[64,64,64]{2,1,0:T(8,128)(2,1)S(1)} copy(bf16[64,64,64]{0,2,1:T(8,128)(2,1)S(1)} %get-tuple-element.27) | data formatting | bytes 1048576 | tf_op jit(solution)/shard_map/convert_element_type | solution.py:74
  30.6 2.1 %convolution_subtract_fusion = f32[64,64,64]{0,2,1:T(8,128)S(1)} fusion(f32[64,64,64]{0,2,1:T(8,128)} %fusion.40, bf16[64,64,64]{2,1,0:T(8,128)(2,1)S(1)} %copy.31, bf16[128,64,1]{0,1,2:T(8,128)(2,1)S(1)} %maximum_bitcast_fusion), kind=kOutput, calls=%fused_computation.14 | convolution fusion | flops 33816576 | bytes 2637824 | tf_op jit(solution)/shard_map/mk,abk->mab/dot_general | solution.py:50
  33.8 5.2 %collective-permute-start = (f32[64,64,16]{0,2,1:T(8,128)}, f32[64,64,16]{0,2,1:T(8,128)}, u32[]{:S(2)}, u32[]{:S(2)}) collective-permute-start(f32[64,64,16]{0,2,1:T(8,128)} %get-tuple-element.11), channel_id=1, source_target_pairs={{0,1},{1,2},{2,3},{3,4},{4,5},{5,6},{6,7},{7,8},{8,9},{9,10},{10,1... | collective-permute-start | bytes 786440 | tf_op jit(solution)/shard_map/ppermute | solution.py:17
  44.5 29.3 %all-to-all-start = ((f32[32,1,8]{2,1,0:T(1,128)}), f32[32,1,8]{2,1,0:T(1,128)S(1)}, u32[]{:S(2)}, u32[]{:S(2)}) async-start(f32[32,1,8]{2,1,0:T(1,128)} %broadcast_in_dim.106), calls=%async_computation | async-start | bytes 32768 | tf_op jit(solution)/shard_map/all_to_all | solution.py:106
  73.9 21.1 %all-to-all-done = f32[32,1,8]{2,1,0:T(1,128)S(1)} async-done(((f32[32,1,8]{2,1,0:T(1,128)}), f32[32,1,8]{2,1,0:T(1,128)S(1)}, u32[]{:S(2)}, u32[]{:S(2)}) %all-to-all-start) | async-done | bytes 1056 | tf_op jit(solution)/shard_map/all_to_all | solution.py:106
  95.7 9.7 %all-to-all-start.1 = ((f32[32,1,8]{2,1,0:T(1,128)}), f32[32,1,8]{2,1,0:T(1,128)S(1)}, u32[]{:S(2)}, u32[]{:S(2)}) async-start(f32[32,1,8]{2,1,0:T(1,128)} %broadcast_in_dim.113), calls=%async_computation.1 | async-start | bytes 32768 | tf_op jit(solution)/shard_map/all_to_all | solution.py:106
  106.8 5.0 %collective-permute-start.2 = (f32[64,16,32]{0,2,1:T(8,128)S(1)}, f32[64,16,32]{0,2,1:T(8,128)S(1)}, u32[]{:S(2)}, u32[]{:S(2)}) collective-permute-start(f32[64,16,32]{0,2,1:T(8,128)S(1)} %get-tuple-element.13), channel_id=1, source_target_pairs={{0,32},{32,64},{64,96},{1,33},{33,65},{65,97},{2,34},{34,66},{66,9... | collective-permute-start | bytes 393224 | tf_op jit(solution)/shard_map/ppermute | solution.py:17
  111.9 1.9 %collective-permute-start.3 = (f32[64,16,32]{0,2,1:T(8,128)S(1)}, f32[64,16,32]{0,2,1:T(8,128)S(1)}, u32[]{:S(2)}, u32[]{:S(2)}) collective-permute-start(f32[64,16,32]{0,2,1:T(8,128)S(1)} %get-tuple-element.14), channel_id=1, source_target_pairs={{32,0},{64,32},{96,64},{33,1},{65,33},{97,65},{34,2},{66,34},{98,6... | collective-permute-start | bytes 393224 | tf_op jit(solution)/shard_map/ppermute | solution.py:17
  115.2 6.8 %collective-permute-done.3 = f32[64,16,32]{0,2,1:T(8,128)S(1)} collective-permute-done((f32[64,16,32]{0,2,1:T(8,128)S(1)}, f32[64,16,32]{0,2,1:T(8,128)S(1)}, u32[]{:S(2)}, u32[]{:S(2)}) %collective-permute-start.3) | collective-permute-done | bytes 131104 | tf_op jit(solution)/shard_map/ppermute | solution.py:17
  123.1 1.6 %collective-permute-start.4 = (f32[16,32,32]{0,2,1:T(8,128)}, f32[16,32,32]{0,2,1:T(8,128)S(1)}, u32[]{:S(2)}, u32[]{:S(2)}) collective-permute-start(f32[16,32,32]{0,2,1:T(8,128)} %get-tuple-element.15), channel_id=1, source_target_pairs={{0,128},{128,256},{256,384},{384,512},{512,640},{640,768},{768,896... | collective-permute-start | bytes 196616 | tf_op jit(solution)/shard_map/ppermute | solution.py:17
  124.7 1.5 %collective-permute-start.5 = (f32[16,32,32]{0,2,1:T(8,128)S(1)}, f32[16,32,32]{0,2,1:T(8,128)S(1)}, u32[]{:S(2)}, u32[]{:S(2)}) collective-permute-start(f32[16,32,32]{0,2,1:T(8,128)S(1)} %get-tuple-element.16), channel_id=1, source_target_pairs={{128,0},{256,128},{384,256},{512,384},{640,512},{768,640},{896,768... | collective-permute-start | bytes 196616 | tf_op jit(solution)/shard_map/ppermute | solution.py:17
  126.9 1.4 reshape.129
  128.3 2.8 %collective-permute-done.4 = f32[16,32,32]{0,2,1:T(8,128)S(1)} collective-permute-done((f32[16,32,32]{0,2,1:T(8,128)}, f32[16,32,32]{0,2,1:T(8,128)S(1)}, u32[]{:S(2)}, u32[]{:S(2)}) %collective-permute-start.4) | collective-permute-done | bytes 65568 | tf_op jit(solution)/shard_map/ppermute | solution.py:17
  131.1 13.7 %collective-permute-done.5 = f32[16,32,32]{0,2,1:T(8,128)S(1)} collective-permute-done((f32[16,32,32]{0,2,1:T(8,128)S(1)}, f32[16,32,32]{0,2,1:T(8,128)S(1)}, u32[]{:S(2)}, u32[]{:S(2)}) %collective-permute-start.5) | collective-permute-done | bytes 65568 | tf_op jit(solution)/shard_map/ppermute | solution.py:17
  (64 shorter events, 20.8 us)
Async XLA Ops:
  4.1 2.5 %copy-start.2 = (f32[64,4096]{1,0:T(8,128)S(1)}, f32[64,4096]{1,0:T(8,128)}, u32[]{:S(2)}) copy-start(f32[64,4096]{1,0:T(8,128)} %param.4) | copy-start | bytes 3145732
  8.9 3.1 %copy-start = (f32[64,64,128]{2,1,0:T(8,128)S(1)}, f32[64,64,128]{2,1,0:T(8,128)}, u32[]{:S(2)}) copy-start(f32[64,64,128]{2,1,0:T(8,128)} %fusion.19) | copy-start | bytes 6291460
  8.9 3.5 %copy-start.1 = (f32[64,64,64]{2,1,0:T(8,128)S(1)}, f32[64,64,64]{2,1,0:T(8,128)}, u32[]{:S(2)}) copy-start(f32[64,64,64]{2,1,0:T(8,128)} %reshape.128) | copy-start | bytes 3145732
  32.7 8.1 %copy-start.3 = (f32[1,1,1,32768]{3,2,1,0:T(1,128)S(1)}, f32[1,1,1,32768]{3,2,1,0:T(1,128)}, u32[]{:S(2)}) copy-start(f32[1,1,1,32768]{3,2,1,0:T(1,128)} %param.3) | copy-start | bytes 393220
  33.8 71.6 %collective-permute-start = (f32[64,64,16]{0,2,1:T(8,128)}, f32[64,64,16]{0,2,1:T(8,128)}, u32[]{:S(2)}, u32[]{:S(2)}) collective-permute-start(f32[64,64,16]{0,2,1:T(8,128)} %get-tuple-element.11), channel_id=1, source_target_pairs={{0,1},{1,2},{2,3},{3,4},{4,5},{5,6},{6,7},{7,8},{8,9},{9,10},{10,1... | collective-permute-start | bytes 786440 | tf_op jit(solution)/shard_map/ppermute | solution.py:17
  39.0 66.5 %collective-permute-start.1 = (f32[64,64,16]{0,2,1:T(8,128)}, f32[64,64,16]{0,2,1:T(8,128)}, u32[]{:S(2)}, u32[]{:S(2)}) collective-permute-start(f32[64,64,16]{0,2,1:T(8,128)} %get-tuple-element.12), channel_id=1, source_target_pairs={{1,0},{2,1},{3,2},{4,3},{5,4},{6,5},{7,6},{8,7},{9,8},{10,9},{11,1... | collective-permute-start | bytes 786440 | tf_op jit(solution)/shard_map/ppermute | solution.py:17
  44.5 50.5 %all-to-all-start = ((f32[32,1,8]{2,1,0:T(1,128)}), f32[32,1,8]{2,1,0:T(1,128)S(1)}, u32[]{:S(2)}, u32[]{:S(2)}) async-start(f32[32,1,8]{2,1,0:T(1,128)} %broadcast_in_dim.106), calls=%async_computation | async-start | bytes 32768 | tf_op jit(solution)/shard_map/all_to_all | solution.py:106
  95.7 18.3 %all-to-all-start.1 = ((f32[32,1,8]{2,1,0:T(1,128)}), f32[32,1,8]{2,1,0:T(1,128)S(1)}, u32[]{:S(2)}, u32[]{:S(2)}) async-start(f32[32,1,8]{2,1,0:T(1,128)} %broadcast_in_dim.113), calls=%async_computation.1 | async-start | bytes 32768 | tf_op jit(solution)/shard_map/all_to_all | solution.py:106
  106.8 19.5 %copy-start.4 = (f32[2,2,2]{2,1,0:T(2,128)S(1)}, f32[2,2,2]{2,1,0:T(2,128)}, u32[]{:S(2)}) copy-start(f32[2,2,2]{2,1,0:T(2,128)} %param.5) | copy-start | bytes 100
  106.8 8.3 %collective-permute-start.2 = (f32[64,16,32]{0,2,1:T(8,128)S(1)}, f32[64,16,32]{0,2,1:T(8,128)S(1)}, u32[]{:S(2)}, u32[]{:S(2)}) collective-permute-start(f32[64,16,32]{0,2,1:T(8,128)S(1)} %get-tuple-element.13), channel_id=1, source_target_pairs={{0,32},{32,64},{64,96},{1,33},{33,65},{65,97},{2,34},{34,66},{66,9... | collective-permute-start | bytes 393224 | tf_op jit(solution)/shard_map/ppermute | solution.py:17
  111.9 10.1 %collective-permute-start.3 = (f32[64,16,32]{0,2,1:T(8,128)S(1)}, f32[64,16,32]{0,2,1:T(8,128)S(1)}, u32[]{:S(2)}, u32[]{:S(2)}) collective-permute-start(f32[64,16,32]{0,2,1:T(8,128)S(1)} %get-tuple-element.14), channel_id=1, source_target_pairs={{32,0},{64,32},{96,64},{33,1},{65,33},{97,65},{34,2},{66,34},{98,6... | collective-permute-start | bytes 393224 | tf_op jit(solution)/shard_map/ppermute | solution.py:17
  123.1 8.0 %collective-permute-start.4 = (f32[16,32,32]{0,2,1:T(8,128)}, f32[16,32,32]{0,2,1:T(8,128)S(1)}, u32[]{:S(2)}, u32[]{:S(2)}) collective-permute-start(f32[16,32,32]{0,2,1:T(8,128)} %get-tuple-element.15), channel_id=1, source_target_pairs={{0,128},{128,256},{256,384},{384,512},{512,640},{640,768},{768,896... | collective-permute-start | bytes 196616 | tf_op jit(solution)/shard_map/ppermute | solution.py:17
  124.7 20.1 %collective-permute-start.5 = (f32[16,32,32]{0,2,1:T(8,128)S(1)}, f32[16,32,32]{0,2,1:T(8,128)S(1)}, u32[]{:S(2)}, u32[]{:S(2)}) collective-permute-start(f32[16,32,32]{0,2,1:T(8,128)S(1)} %get-tuple-element.16), channel_id=1, source_target_pairs={{128,0},{256,128},{384,256},{512,384},{640,512},{768,640},{896,768... | collective-permute-start | bytes 196616 | tf_op jit(solution)/shard_map/ppermute | solution.py:17

commit v6 on v3

--- a/solution.py
+++ b/solution.py
@@ -89,8 +89,9 @@
 
 def gather_rows(value, axes):
     count = lax.axis_size(axes)
-    rows = jnp.broadcast_to(value[None, :], (count, value.shape[0]))
-    return lax.all_to_all(rows, axes, 0, 0, tiled=True)
+    width = max(value.shape[0], (1 << 18) // count)
+    padded = jnp.concatenate([value, jnp.zeros((width - value.shape[0],), value.dtype)])
+    return lax.all_gather(padded, axes)[:, : value.shape[0]]
 
 
 def level_sums(rows, me, first_level, group_of):

time: 124 us -> 243 us (1.96); the launches traced: 123 us -> 239 us
  waiting for transfers between devices: 27.2 us -> 148 us
  starting transfers between devices: 54 us -> 35.2 us
  between operations: 0.43 us -> 13.8 us
    all_gather x0 -> x2, waiting for transfers between devices: none -> 110 us  [gather_rows(): return lax.all_gather(padded, axes)[:, :value.shape[0]]]
    all_to_all x2 -> x0, starting transfers between devices: 38 us -> none  [gather_rows(): return lax.all_to_all(rows, axes, 0, 0, tiled=True)]
    ppermute x6, starting transfers between devices: 16 us -> 35.1 us  [from_behind(): return lax.ppermute(block, axis, route)]
    ppermute x6, waiting for transfers between devices: 27.2 us -> 38.3 us  [from_behind(): return lax.ppermute(block, axis, route)]
    dot_general x16, matrix products: 11.1 us -> 14 us  [mixed(): return jnp.einsum(form, table, data, preferred_element_type=jnp.float32)]
    all_gather x0 -> x2, local copies, waits for them, and re-layouts: none -> 2.83 us  [gather_rows(): return lax.all_gather(padded, axes)[:, :value.shape[0]]]
    unnamed x4, matrix products: 4.34 us -> 1.78 us
  transfers between devices with their start and end apart: 8 -> 8, of which waited for: 5 -> 8; matrix products, arithmetic and copies ran while one was open for 25% -> 12% of each run, Pallas kernels for 0% -> 0%
where the time goes in v6:
time: 243 us; the launch traced here: 239 us
  waiting for transfers between devices  148 us (61%)
  starting transfers between devices  35.2 us (14%)
  local copies, waits for them, and re-layouts  19.8 us (8%)
  matrix products  15.8 us (7%)
  between operations  13.8 us (6%)
  other arithmetic  6.7 us (3%)
    all_gather x2, waiting for transfers between devices, gather_rows(): return lax.all_gather(padded, axes)[:, :value.shape[0]]  110 us
    ppermute x6, waiting for transfers between devices, from_behind(): return lax.ppermute(block, axis, route)  38.3 us
    ppermute x6, starting transfers between devices, from_behind(): return lax.ppermute(block, axis, route)  35.1 us
    dot_general x16, matrix products, mixed(): return jnp.einsum(form, table, data, preferred_element_type=jnp.float32)  14 us
  transfers between devices with their start and end apart: 8, of which 8 were waited for; matrix products, arithmetic and copies ran while one was open for 12% of the time, Pallas kernels for 0%

profile of v6, /device:TPU:1, one launch (start us, length us, event | category | flops | bytes accessed | tf_op | source)
XLA Modules:
  0.0 239.3 jit_solution(14453170700174404977)
XLA Ops:
  7.1 1.9 reduce.5
  8.9 1.4 reshape_reshape.3
  15.2 2.2 reshape.113
  22.5 1.9 fusion.45
  24.4 3.1 %fusion = bf16[64,64,64]{1,2,0:T(8,128)(2,1)} fusion(f32[64,64,64]{2,1,0:T(8,128)} %fusion.45, bf16[64,64,64]{2,1,0:T(8,128)(2,1)S(1)} %add_convert_fusion.1), kind=kOutput, calls=%fused_computation.14 | convolution fusion | flops 34144256 | bytes 2097152 | tf_op jit(solution)/shard_map/nk,xkz->xnz/dot_general | solution.py:37
  27.6 3.3 %copy.71 = bf16[64,64,64]{0,2,1:T(8,128)(2,1)S(1)} copy(bf16[64,64,64]{1,2,0:T(8,128)(2,1)} %fusion) | data formatting | bytes 1048576 | tf_op jit(solution)/shard_map/convert_element_type | solution.py:60
  31.4 1.6 fusion.1
  33.0 3.3 %copy.74 = bf16[64,64,64]{0,2,1:T(8,128)(2,1)S(1)} copy(bf16[64,64,64]{1,2,0:T(8,128)(2,1)} %fusion.1) | data formatting | bytes 1048576 | tf_op jit(solution)/shard_map/convert_element_type | solution.py:61
  37.9 97.9 %all-gather.5.cloned.1.call-done = f32[262144]{0:T(1024)} async-done(((f32[8192]{0:T(1024)}), f32[262144]{0:T(1024)}) %all-gather.5.cloned.1.call-update) | async-done | bytes 1048592 | tf_op jit(solution)/shard_map/all_gather | solution.py:94
  135.8 1.4 reshape.118
  138.9 2.1 collective-permute-start
  142.3 5.4 %collective-permute-done = f32[64,64,16]{0,2,1:T(8,128)S(1)} collective-permute-done((f32[64,64,16]{0,2,1:T(8,128)}, f32[64,64,16]{0,2,1:T(8,128)S(1)}, u32[]{:S(2)}, u32[]{:S(2)}) %collective-permute-start) | collective-permute-done | bytes 262176 | tf_op jit(solution)/shard_map/ppermute | solution.py:17
  148.5 3.1 %collective-permute-done.1 = f32[64,64,16]{0,2,1:T(8,128)} collective-permute-done((f32[64,64,16]{0,2,1:T(8,128)S(1)}, f32[64,64,16]{0,2,1:T(8,128)}, u32[]{:S(2)}, u32[]{:S(2)}) %collective-permute-start.1) | collective-permute-done | bytes 262176 | tf_op jit(solution)/shard_map/ppermute | solution.py:17
  151.6 1.3 slice_add_fusion
  153.0 27.0 %collective-permute-start.2 = (f32[64,16,32]{0,2,1:T(8,128)S(1)}, f32[64,16,32]{0,2,1:T(8,128)S(1)}, u32[]{:S(2)}, u32[]{:S(2)}) collective-permute-start(f32[64,16,32]{0,2,1:T(8,128)S(1)} %get-tuple-element.13), channel_id=1, source_target_pairs={{0,32},{32,64},{64,96},{1,33},{33,65},{65,97},{2,34},{34,66},{66,9... | collective-permute-start | bytes 393224 | tf_op jit(solution)/shard_map/ppermute | solution.py:17
  180.0 1.9 collective-permute-start.3
  182.0 2.0 collective-permute-done.2
  184.0 8.1 %collective-permute-done.3 = f32[64,16,32]{0,2,1:T(8,128)S(1)} collective-permute-done((f32[64,16,32]{0,2,1:T(8,128)S(1)}, f32[64,16,32]{0,2,1:T(8,128)S(1)}, u32[]{:S(2)}, u32[]{:S(2)}) %collective-permute-start.3) | collective-permute-done | bytes 131104 | tf_op jit(solution)/shard_map/ppermute | solution.py:17
  193.8 1.5 collective-permute-start.5
  195.3 5.0 %collective-permute-done.4 = f32[16,32,32]{0,2,1:T(8,128)S(1)} collective-permute-done((f32[16,32,32]{0,2,1:T(8,128)S(1)}, f32[16,32,32]{0,2,1:T(8,128)S(1)}, u32[]{:S(2)}, u32[]{:S(2)}) %collective-permute-start.4) | collective-permute-done | bytes 65568 | tf_op jit(solution)/shard_map/ppermute | solution.py:17
  200.3 14.6 %collective-permute-done.5 = f32[16,32,32]{0,2,1:T(8,128)S(1)} collective-permute-done((f32[16,32,32]{0,2,1:T(8,128)S(1)}, f32[16,32,32]{0,2,1:T(8,128)S(1)}, u32[]{:S(2)}, u32[]{:S(2)}) %collective-permute-start.5) | collective-permute-done | bytes 65568 | tf_op jit(solution)/shard_map/ppermute | solution.py:17
  216.2 11.8 %all-gather.7.cloned.1.call-done = f32[262144]{0:T(1024)} async-done(((f32[8192]{0:T(1024)}), f32[262144]{0:T(1024)}) %all-gather.7.cloned.1.call-update) | async-done | bytes 1048592 | tf_op jit(solution)/shard_map/all_gather | solution.py:94
  228.0 1.4 reshape.119
  230.2 1.4 reshape.114
  (63 shorter events, 20.7 us)
Async XLA Ops:
  6.5 5.2 %copy-start = (f32[1,1,1,32768]{3,2,1,0:T(1,128)S(1)}, f32[1,1,1,32768]{3,2,1,0:T(1,128)}, u32[]{:S(2)}) copy-start(f32[1,1,1,32768]{3,2,1,0:T(1,128)} %param.3) | copy-start | bytes 393220
  6.5 129.2 %all-gather.5.cloned.1.call-start = ((), (), s32[]{:S(2)}) async-start(), calls=%async_computation | async-start | bytes 1081344 | tf_op jit(solution)/shard_map/all_gather | solution.py:94
  11.7 216.3 %all-gather.7.cloned.1.call-start = ((), (), s32[]{:S(2)}) async-start(), calls=%async_computation.1 | async-start | bytes 1081344 | tf_op jit(solution)/shard_map/all_gather | solution.py:94
  138.9 8.9 %collective-permute-start = (f32[64,64,16]{0,2,1:T(8,128)}, f32[64,64,16]{0,2,1:T(8,128)S(1)}, u32[]{:S(2)}, u32[]{:S(2)}) collective-permute-start(f32[64,64,16]{0,2,1:T(8,128)} %get-tuple-element.11), channel_id=1, source_target_pairs={{0,1},{1,2},{2,3},{3,4},{4,5},{5,6},{6,7},{7,8},{8,9},{9,10},{10,1... | collective-permute-start | bytes 786440 | tf_op jit(solution)/shard_map/ppermute | solution.py:17
  141.0 10.6 %collective-permute-start.1 = (f32[64,64,16]{0,2,1:T(8,128)S(1)}, f32[64,64,16]{0,2,1:T(8,128)}, u32[]{:S(2)}, u32[]{:S(2)}) collective-permute-start(f32[64,64,16]{0,2,1:T(8,128)S(1)} %get-tuple-element.12), channel_id=1, source_target_pairs={{1,0},{2,1},{3,2},{4,3},{5,4},{6,5},{7,6},{8,7},{9,8},{10,9},{11,1... | collective-permute-start | bytes 786440 | tf_op jit(solution)/shard_map/ppermute | solution.py:17
  147.7 0.8 copy-start.1
  153.0 31.0 %collective-permute-start.2 = (f32[64,16,32]{0,2,1:T(8,128)S(1)}, f32[64,16,32]{0,2,1:T(8,128)S(1)}, u32[]{:S(2)}, u32[]{:S(2)}) collective-permute-start(f32[64,16,32]{0,2,1:T(8,128)S(1)} %get-tuple-element.13), channel_id=1, source_target_pairs={{0,32},{32,64},{64,96},{1,33},{33,65},{65,97},{2,34},{34,66},{66,9... | collective-permute-start | bytes 393224 | tf_op jit(solution)/shard_map/ppermute | solution.py:17
  180.0 12.1 %collective-permute-start.3 = (f32[64,16,32]{0,2,1:T(8,128)S(1)}, f32[64,16,32]{0,2,1:T(8,128)S(1)}, u32[]{:S(2)}, u32[]{:S(2)}) collective-permute-start(f32[64,16,32]{0,2,1:T(8,128)S(1)} %get-tuple-element.14), channel_id=1, source_target_pairs={{32,0},{64,32},{96,64},{33,1},{65,33},{97,65},{34,2},{66,34},{98,6... | collective-permute-start | bytes 393224 | tf_op jit(solution)/shard_map/ppermute | solution.py:17
  192.4 7.9 %collective-permute-start.4 = (f32[16,32,32]{0,2,1:T(8,128)S(1)}, f32[16,32,32]{0,2,1:T(8,128)S(1)}, u32[]{:S(2)}, u32[]{:S(2)}) collective-permute-start(f32[16,32,32]{0,2,1:T(8,128)S(1)} %get-tuple-element.15), channel_id=1, source_target_pairs={{0,128},{128,256},{256,384},{384,512},{512,640},{640,768},{768,896... | collective-permute-start | bytes 196616 | tf_op jit(solution)/shard_map/ppermute | solution.py:17
  193.8 21.2 %collective-permute-start.5 = (f32[16,32,32]{0,2,1:T(8,128)S(1)}, f32[16,32,32]{0,2,1:T(8,128)S(1)}, u32[]{:S(2)}, u32[]{:S(2)}) collective-permute-start(f32[16,32,32]{0,2,1:T(8,128)S(1)} %get-tuple-element.16), channel_id=1, source_target_pairs={{128,0},{256,128},{384,256},{512,384},{640,512},{768,640},{896,768... | collective-permute-start | bytes 196616 | tf_op jit(solution)/shard_map/ppermute | solution.py:17
  215.5 14.2 %copy-start.2 = (f32[2,2,2]{2,1,0:T(2,128)S(1)}, f32[2,2,2]{2,1,0:T(2,128)}, u32[]{:S(2)}) copy-start(f32[2,2,2]{2,1,0:T(2,128)} %param.5) | copy-start | bytes 100
Sparse Core Ops, SparseCore 0:
  11.8 123.8 all-gather.4
  138.5 89.4 all-gather.6

commit v7 on v3

--- a/solution.py
+++ b/solution.py
@@ -81,9 +81,11 @@
     first = lax.slice_in_dim(field, quarter, 2 * quarter, axis=dim)
     second = lax.slice_in_dim(field, 2 * quarter, 3 * quarter, axis=dim)
     high_rim = lax.slice_in_dim(field, 3 * quarter, 4 * quarter, axis=dim)
+    shape = low_rim.shape
+    low_rim, high_rim = (rim.reshape(-1, 128) for rim in (low_rim, high_rim))
     low_rim, high_rim = lax.optimization_barrier((low_rim, high_rim))
-    from_left = mover(high_rim, 1)
-    from_right = mover(low_rim, -1)
+    from_left = mover(high_rim, 1).reshape(shape)
+    from_right = mover(low_rim, -1).reshape(shape)
     return jnp.concatenate([first + from_left, second + from_right], axis=dim)
 
 

time: 124 us -> 125 us (level)
  local copies, waits for them, and re-layouts: 18.5 us -> 40.8 us
  waiting for transfers between devices: 27.2 us -> 7.52 us
    ppermute x6, waiting for transfers between devices: 27.2 us -> 7.52 us  [from_behind(): return lax.ppermute(block, axis, route)]
    reshape x0 -> x18, local copies, waits for them, and re-layouts: none -> 17.1 us  [the longest x6 6.13 us: fold_margin(): from_left = mover(high_rim, 1).reshape(shape)]
    slice x0 -> x3, local copies, waits for them, and re-layouts: none -> 3.39 us  [fold_margin(): low_rim = lax.slice_in_dim(field, 0, quarter, axis=dim)]
    slice x1 -> x4, local copies, waits for them, and re-layouts: 0.91 us -> 3.49 us  [fold_margin(): high_rim = lax.slice_in_dim(field, 3 * quarter, 4 * quarter, axis=dim)]
    ppermute x6, starting transfers between devices: 16 us -> 14.7 us  [from_behind(): return lax.ppermute(block, axis, route)]
  transfers between devices with their start and end apart: 8 -> 8, of which waited for: 5 -> 2; matrix products, arithmetic and copies ran while one was open for 25% -> 43% of each run, Pallas kernels for 0% -> 0%
where the time goes in v7:
time: 125 us; the launch traced here: 124 us
  starting transfers between devices  52.8 us (42%)
  local copies, waits for them, and re-layouts  40.8 us (33%)
  matrix products  15.4 us (12%)
  waiting for transfers between devices  7.52 us (6%)
  other arithmetic  6.75 us (5%)
    all_to_all x2, starting transfers between devices, gather_rows(): return lax.all_to_all(rows, axes, 0, 0, tiled=True)  38 us
    ppermute x6, starting transfers between devices, from_behind(): return lax.ppermute(block, axis, route)  14.7 us
    dot_general x16, matrix products, mixed(): return jnp.einsum(form, table, data, preferred_element_type=jnp.float32)  11.1 us
    ppermute x6, waiting for transfers between devices, from_behind(): return lax.ppermute(block, axis, route)  7.52 us
    reshape x6, local copies, waits for them, and re-layouts, fold_margin(): from_left = mover(high_rim, 1).reshape(shape)  6.13 us
    reshape x6, local copies, waits for them, and re-layouts, fold_margin(): from_right = mover(low_rim, -1).reshape(shape)  6.12 us
    reshape x6, local copies, waits for them, and re-layouts, fold_margin(): low_rim, high_rim = (rim.reshape(-1, 128) for rim in (low_rim, high_rim))  4.89 us
    unnamed x4, matrix products  4.34 us
  transfers between devices with their start and end apart: 8, of which 2 were waited for; matrix products, arithmetic and copies ran while one was open for 43% of the time, Pallas kernels for 0%

profile of v7, /device:TPU:1, one launch (start us, length us, event | category | flops | bytes accessed | tf_op | source)
XLA Modules:
  0.0 123.8 jit_solution(7921464154873930430)
XLA Ops:
  0.5 1.9 %reduce.6 = f32[32768]{0:T(1024)S(1)} reduce(f32[1,1,1,32768]{3,2,1,0:T(1,128)} %param.3, f32[]{:T(128)} %broadcast.410), dimensions={0,1,2}, to_apply=%param.3.reduce_sub_computation.3 | reduce | bytes 262148 | tf_op args[0]
  5.1 29.5 %all-to-all-start = ((f32[32,1,8]{2,1,0:T(1,128)}), f32[32,1,8]{2,1,0:T(1,128)S(1)}, u32[]{:S(2)}, u32[]{:S(2)}) async-start(f32[32,1,8]{2,1,0:T(1,128)} %broadcast_in_dim.106), calls=%async_computation | async-start | bytes 32768 | tf_op jit(solution)/shard_map/all_to_all | solution.py:95
  38.0 2.0 %reshape.164 = f32[64,64,64]{2,1,0:T(8,128)S(1)} reshape(f32[64,4096]{1,0:T(8,128)} %param.4) | data formatting | bytes 2097152 | tf_op jit(solution)/shard_map/reshape | solution.py:121
  46.3 1.6 %fusion = bf16[64,64,64]{1,2,0:T(8,128)(2,1)} fusion(f32[64,64,64]{2,1,0:T(8,128)S(1)} %fusion.45, bf16[64,64,64]{2,1,0:T(8,128)(2,1)S(1)} %add_convert_fusion.1), kind=kOutput, calls=%fused_computation.14 | convolution fusion | flops 34144256 | bytes 2097152 | tf_op jit(solution)/shard_map/nk,xkz->xnz/dot_general | solution.py:37
  47.9 4.0 %copy.49 = bf16[64,64,64]{0,2,1:T(8,128)(2,1)} copy(bf16[64,64,64]{1,2,0:T(8,128)(2,1)} %fusion) | data formatting | bytes 1048576 | tf_op jit(solution)/shard_map/convert_element_type | solution.py:60
  51.8 3.1 %fusion.51 = f32[64,4096]{0,1} fusion(bf16[64,4096]{0,1:T(8,128)(2,1)} %bitcast.68), kind=kOutput, calls=%fused_computation.100 | convolution fusion | flops 33619968 | bytes 1572864
  55.0 1.6 %fusion.1 = bf16[64,64,64]{1,2,0:T(8,128)(2,1)} fusion(f32[64,64,64]{2,1,0:T(8,128)S(1)} %fusion.41, bf16[64,64,64]{2,1,0:T(8,128)(2,1)S(1)} %subtract_convert_fusion.1), kind=kOutput, calls=%fused_computation.15 | convolution fusion | flops 34144256 | bytes 2097152 | tf_op jit(solution)/shard_map/nk,xkz->xnz/dot_general | solution.py:37
  56.5 3.3 %copy.52 = bf16[64,64,64]{0,2,1:T(8,128)(2,1)S(1)} copy(bf16[64,64,64]{1,2,0:T(8,128)(2,1)} %fusion.1) | data formatting | bytes 1048576 | tf_op jit(solution)/shard_map/convert_element_type | solution.py:61
  61.9 2.8 %copy.54 = f32[64,64,16]{2,1,0:T(8,128)} copy(f32[64,64,16]{0,2,1:T(8,128)S(1)} %get-tuple-element.29) | data formatting | bytes 524288 | tf_op jit(solution)/shard_map/slice | solution.py:83
  64.8 2.2 %reshape.166 = f32[512,128]{1,0:T(8,128)S(1)} reshape(f32[64,64,16]{2,1,0:T(8,128)} %copy.54) | data formatting | bytes 524288 | tf_op jit(solution)/shard_map/reshape | solution.py:85
  66.9 2.8 %copy.53 = f32[64,64,16]{2,1,0:T(8,128)} copy(f32[64,64,16]{0,2,1:T(8,128)S(1)} %get-tuple-element.30) | data formatting | bytes 524288 | tf_op jit(solution)/shard_map/slice | solution.py:80
  69.8 2.2 %reshape.165 = f32[512,128]{1,0:T(8,128)S(1)} reshape(f32[64,64,16]{2,1,0:T(8,128)} %copy.53) | data formatting | bytes 524288 | tf_op jit(solution)/shard_map/reshape | solution.py:85
  72.0 3.0 %collective-permute-start = (f32[512,128]{1,0:T(8,128)S(1)}, f32[512,128]{1,0:T(8,128)S(1)}, u32[]{:S(2)}, u32[]{:S(2)}) collective-permute-start(f32[512,128]{1,0:T(8,128)S(1)} %reshape.166), channel_id=1, source_target_pairs={{0,1},{1,2},{2,3},{3,4},{4,5},{5,6},{6,7},{7,8},{8,9},{9,10},{10,1... | collective-permute-start | bytes 786440 | tf_op jit(solution)/shard_map/ppermute | solution.py:17
  77.0 8.6 %all-to-all-start.1 = ((f32[32,1,8]{2,1,0:T(1,128)}), f32[32,1,8]{2,1,0:T(1,128)S(1)}, u32[]{:S(2)}, u32[]{:S(2)}) async-start(f32[32,1,8]{2,1,0:T(1,128)} %broadcast_in_dim.113), calls=%async_computation.1 | async-start | bytes 32768 | tf_op jit(solution)/shard_map/all_to_all | solution.py:95
  85.7 1.9 %reshape.168 = f32[64,64,16]{2,1,0:T(8,128)} reshape(f32[512,128]{1,0:T(8,128)S(1)} %collective-permute-done.1) | data formatting | bytes 524288 | tf_op jit(solution)/shard_map/reshape | solution.py:88
  87.6 3.4 %copy.56 = f32[64,64,16]{0,2,1:T(8,128)} copy(f32[64,64,16]{2,1,0:T(8,128)} %reshape.168) | data formatting | bytes 524288 | tf_op jit(solution)/shard_map/reshape | solution.py:88
  91.0 1.9 %reshape.167 = f32[64,64,16]{2,1,0:T(8,128)} reshape(f32[512,128]{1,0:T(8,128)S(1)} %collective-permute-done) | data formatting | bytes 524288 | tf_op jit(solution)/shard_map/reshape | solution.py:87
  93.0 3.4 %copy.55 = f32[64,64,16]{0,2,1:T(8,128)} copy(f32[64,64,16]{2,1,0:T(8,128)} %reshape.167) | data formatting | bytes 524288 | tf_op jit(solution)/shard_map/reshape | solution.py:87
  98.7 5.0 %collective-permute-start.2 = (f32[256,128]{1,0:T(8,128)S(1)}, f32[256,128]{1,0:T(8,128)S(1)}, u32[]{:S(2)}, u32[]{:S(2)}) collective-permute-start(f32[256,128]{1,0:T(8,128)S(1)} %reshape.170), channel_id=1, source_target_pairs={{0,32},{32,64},{64,96},{1,33},{33,65},{65,97},{2,34},{34,66},{66,9... | collective-permute-start | bytes 393224 | tf_op jit(solution)/shard_map/ppermute | solution.py:17
  103.8 1.9 %collective-permute-start.3 = (f32[256,128]{1,0:T(8,128)S(1)}, f32[256,128]{1,0:T(8,128)S(1)}, u32[]{:S(2)}, u32[]{:S(2)}) collective-permute-start(f32[256,128]{1,0:T(8,128)S(1)} %reshape.169), channel_id=1, source_target_pairs={{32,0},{64,32},{96,64},{33,1},{65,33},{97,65},{34,2},{66,34},{98,6... | collective-permute-start | bytes 393224 | tf_op jit(solution)/shard_map/ppermute | solution.py:17
  105.9 5.6 %collective-permute-done.3 = f32[256,128]{1,0:T(8,128)S(1)} collective-permute-done((f32[256,128]{1,0:T(8,128)S(1)}, f32[256,128]{1,0:T(8,128)S(1)}, u32[]{:S(2)}, u32[]{:S(2)}) %collective-permute-start.3) | collective-permute-done | bytes 131104 | tf_op jit(solution)/shard_map/ppermute | solution.py:17
  113.5 2.2 %collective-permute-start.4 = (f32[128,128]{1,0:T(8,128)S(1)}, f32[128,128]{1,0:T(8,128)S(1)}, u32[]{:S(2)}, u32[]{:S(2)}) collective-permute-start(f32[128,128]{1,0:T(8,128)S(1)} %reshape.174), channel_id=1, source_target_pairs={{0,128},{128,256},{256,384},{384,512},{512,640},{640,768},{768,896... | collective-permute-start | bytes 196616 | tf_op jit(solution)/shard_map/ppermute | solution.py:17
  117.7 1.4 %reshape.177 = f32[1,1,1,32768]{3,2,1,0:T(1,128)S(1)} reshape(f32[2,16,2,16,2,16]{5,4,3,2,1,0:T(2,128)S(1)} %broadcast_in_dim.118) | data formatting | bytes 262144 | tf_op jit(solution)/shard_map/reshape | solution.py:133
  119.5 1.9 %collective-permute-done.5 = f32[128,128]{1,0:T(8,128)S(1)} collective-permute-done((f32[128,128]{1,0:T(8,128)S(1)}, f32[128,128]{1,0:T(8,128)S(1)}, u32[]{:S(2)}, u32[]{:S(2)}) %collective-permute-start.5) | collective-permute-done | bytes 65568 | tf_op jit(solution)/shard_map/ppermute | solution.py:17
  (84 shorter events, 26.0 us)
Async XLA Ops:
  0.0 34.6 %copy-start.1 = (f32[1,1,1,32768]{3,2,1,0:T(1,128)S(1)}, f32[1,1,1,32768]{3,2,1,0:T(1,128)}, u32[]{:S(2)}) copy-start(f32[1,1,1,32768]{3,2,1,0:T(1,128)} %param.3) | copy-start | bytes 393220
  5.1 71.2 %all-to-all-start = ((f32[32,1,8]{2,1,0:T(1,128)}), f32[32,1,8]{2,1,0:T(1,128)S(1)}, u32[]{:S(2)}, u32[]{:S(2)}) async-start(f32[32,1,8]{2,1,0:T(1,128)} %broadcast_in_dim.106), calls=%async_computation | async-start | bytes 32768 | tf_op jit(solution)/shard_map/all_to_all | solution.py:95
  59.8 1.6 %copy-start = (f32[64,4096]{0,1:S(1)}, f32[64,4096]{0,1}, u32[]{:S(2)}) copy-start(f32[64,4096]{0,1} %fusion.51) | copy-start | bytes 3145732
  72.0 19.1 %collective-permute-start = (f32[512,128]{1,0:T(8,128)S(1)}, f32[512,128]{1,0:T(8,128)S(1)}, u32[]{:S(2)}, u32[]{:S(2)}) collective-permute-start(f32[512,128]{1,0:T(8,128)S(1)} %reshape.166), channel_id=1, source_target_pairs={{0,1},{1,2},{2,3},{3,4},{4,5},{5,6},{6,7},{7,8},{8,9},{9,10},{10,1... | collective-permute-start | bytes 786440 | tf_op jit(solution)/shard_map/ppermute | solution.py:17
  75.0 10.7 %collective-permute-start.1 = (f32[512,128]{1,0:T(8,128)S(1)}, f32[512,128]{1,0:T(8,128)S(1)}, u32[]{:S(2)}, u32[]{:S(2)}) collective-permute-start(f32[512,128]{1,0:T(8,128)S(1)} %reshape.165), channel_id=1, source_target_pairs={{1,0},{2,1},{3,2},{4,3},{5,4},{6,5},{7,6},{8,7},{9,8},{10,9},{11,1... | collective-permute-start | bytes 786440 | tf_op jit(solution)/shard_map/ppermute | solution.py:17
  77.0 28.8 %all-to-all-start.1 = ((f32[32,1,8]{2,1,0:T(1,128)}), f32[32,1,8]{2,1,0:T(1,128)S(1)}, u32[]{:S(2)}, u32[]{:S(2)}) async-start(f32[32,1,8]{2,1,0:T(1,128)} %broadcast_in_dim.113), calls=%async_computation.1 | async-start | bytes 32768 | tf_op jit(solution)/shard_map/all_to_all | solution.py:95
  98.7 13.3 %collective-permute-start.2 = (f32[256,128]{1,0:T(8,128)S(1)}, f32[256,128]{1,0:T(8,128)S(1)}, u32[]{:S(2)}, u32[]{:S(2)}) collective-permute-start(f32[256,128]{1,0:T(8,128)S(1)} %reshape.170), channel_id=1, source_target_pairs={{0,32},{32,64},{64,96},{1,33},{33,65},{65,97},{2,34},{34,66},{66,9... | collective-permute-start | bytes 393224 | tf_op jit(solution)/shard_map/ppermute | solution.py:17
  103.8 7.8 %collective-permute-start.3 = (f32[256,128]{1,0:T(8,128)S(1)}, f32[256,128]{1,0:T(8,128)S(1)}, u32[]{:S(2)}, u32[]{:S(2)}) collective-permute-start(f32[256,128]{1,0:T(8,128)S(1)} %reshape.169), channel_id=1, source_target_pairs={{32,0},{64,32},{96,64},{33,1},{65,33},{97,65},{34,2},{66,34},{98,6... | collective-permute-start | bytes 393224 | tf_op jit(solution)/shard_map/ppermute | solution.py:17
  112.5 4.6 %copy-start.2 = (f32[2,2,2]{2,1,0:T(2,128)S(1)}, f32[2,2,2]{2,1,0:T(2,128)}, u32[]{:S(2)}) copy-start(f32[2,2,2]{2,1,0:T(2,128)} %param.5) | copy-start | bytes 100
  113.5 5.6 %collective-permute-start.4 = (f32[128,128]{1,0:T(8,128)S(1)}, f32[128,128]{1,0:T(8,128)S(1)}, u32[]{:S(2)}, u32[]{:S(2)}) collective-permute-start(f32[128,128]{1,0:T(8,128)S(1)} %reshape.174), channel_id=1, source_target_pairs={{0,128},{128,256},{256,384},{384,512},{512,640},{640,768},{768,896... | collective-permute-start | bytes 196616 | tf_op jit(solution)/shard_map/ppermute | solution.py:17
  115.7 5.6 %collective-permute-start.5 = (f32[128,128]{1,0:T(8,128)S(1)}, f32[128,128]{1,0:T(8,128)S(1)}, u32[]{:S(2)}, u32[]{:S(2)}) collective-permute-start(f32[128,128]{1,0:T(8,128)S(1)} %reshape.173), channel_id=1, source_target_pairs={{128,0},{256,128},{384,256},{512,384},{640,512},{768,640},{896,768... | collective-permute-start | bytes 196616 | tf_op jit(solution)/shard_map/ppermute | solution.py:17

commit v8 on v7

--- a/solution.py
+++ b/solution.py
@@ -75,14 +75,15 @@
     return from_behind(part, "gz", step)
 
 
-def fold_margin(field, dim, mover):
+def fold_margin(field, dim, mover, dense):
     quarter = field.shape[dim] // 4
     low_rim = lax.slice_in_dim(field, 0, quarter, axis=dim)
     first = lax.slice_in_dim(field, quarter, 2 * quarter, axis=dim)
     second = lax.slice_in_dim(field, 2 * quarter, 3 * quarter, axis=dim)
     high_rim = lax.slice_in_dim(field, 3 * quarter, 4 * quarter, axis=dim)
     shape = low_rim.shape
-    low_rim, high_rim = (rim.reshape(-1, 128) for rim in (low_rim, high_rim))
+    if dense:
+        low_rim, high_rim = (rim.reshape(-1, 128) for rim in (low_rim, high_rim))
     low_rim, high_rim = lax.optimization_barrier((low_rim, high_rim))
     from_left = mover(high_rim, 1).reshape(shape)
     from_right = mover(low_rim, -1).reshape(shape)
@@ -123,7 +124,7 @@
     order = ((2, move_z), (1, move_y), (0, move_x))
     near = box
     for dim, mover in order:
-        near = fold_margin(near, dim, mover)
+        near = fold_margin(near, dim, mover, dim != 2)
     cx, cy, cz = (px // CB, py // CB, pz // CB)
     scale = 1.0 / math.sqrt(CB**3)
     coarse = patch.reshape(cx, CB, cy, CB, cz, CB).sum(axis=(1, 3, 5)) * scale

time: 125 us -> 111 us (0.89)
  local copies, waits for them, and re-layouts: 40.8 us -> 21.7 us
  waiting for transfers between devices: 7.52 us -> 10.1 us
  starting transfers between devices: 52.8 us -> 54.7 us
    reshape x6 -> x4, local copies, waits for them, and re-layouts: 6.13 us -> 0.77 us  [fold_margin(): from_left = mover(high_rim, 1).reshape(shape)]
    reshape x6 -> x4, local copies, waits for them, and re-layouts: 6.12 us -> 0.77 us  [fold_margin(): from_right = mover(low_rim, -1).reshape(shape)]
    reshape x6 -> x4, local copies, waits for them, and re-layouts: 4.89 us -> 0.56 us  [fold_margin(): low_rim, high_rim = (rim.reshape(-1, 128) for rim in (low_rim, high_rim))]
    slice x3 -> x2, local copies, waits for them, and re-layouts: 3.39 us -> 0.55 us  [fold_margin(): low_rim = lax.slice_in_dim(field, 0, quarter, axis=dim)]
    ppermute x6, waiting for transfers between devices: 7.52 us -> 10.1 us  [from_behind(): return lax.ppermute(block, axis, route)]
    slice x4 -> x3, local copies, waits for them, and re-layouts: 3.49 us -> 1.47 us  [fold_margin(): high_rim = lax.slice_in_dim(field, 3 * quarter, 4 * quarter, axis=dim)]
    ppermute x6, starting transfers between devices: 14.7 us -> 16.6 us  [from_behind(): return lax.ppermute(block, axis, route)]
  transfers between devices with their start and end apart: 8 -> 8, of which waited for: 2 -> 3; matrix products, arithmetic and copies ran while one was open for 43% -> 30% of each run, Pallas kernels for 0% -> 0%
where the time goes in v8:
time: 111 us; the launch traced here: 109 us
  starting transfers between devices  54.7 us (49%)
  local copies, waits for them, and re-layouts  21.7 us (20%)
  matrix products  15.4 us (14%)
  waiting for transfers between devices  10.1 us (9%)
  other arithmetic  6.75 us (6%)
    all_to_all x2, starting transfers between devices, gather_rows(): return lax.all_to_all(rows, axes, 0, 0, tiled=True)  38 us
    ppermute x6, starting transfers between devices, from_behind(): return lax.ppermute(block, axis, route)  16.6 us
    dot_general x16, matrix products, mixed(): return jnp.einsum(form, table, data, preferred_element_type=jnp.float32)  11.1 us
    ppermute x6, waiting for transfers between devices, from_behind(): return lax.ppermute(block, axis, route)  10.1 us
    unnamed x4, matrix products  4.34 us
    convert_element_type x1, local copies, waits for them, and re-layouts, local_box(): new_real = (mixed(form, cosv, real) - mixed(form, sinv, imag)).astype(bf)  3.98 us
    convert_element_type x1, local copies, waits for them, and re-layouts, local_box(): imag = (mixed(form, cosv, imag) + mixed(form, sinv, real)).astype(bf)  3.3 us
    unnamed x9, local copies, waits for them, and re-layouts  2.36 us
  transfers between devices with their start and end apart: 8, of which 3 were waited for; matrix products, arithmetic and copies ran while one was open for 30% of the time, Pallas kernels for 0%

profile of v8, /device:TPU:1, one launch (start us, length us, event | category | flops | bytes accessed | tf_op | source)
XLA Modules:
  0.0 109.1 jit_solution(17491343689982914370)
XLA Ops:
  0.5 1.9 %reduce.6 = f32[32768]{0:T(1024)S(1)} reduce(f32[1,1,1,32768]{3,2,1,0:T(1,128)} %param.3, f32[]{:T(128)} %broadcast.410), dimensions={0,1,2}, to_apply=%param.3.reduce_sub_computation.3 | reduce | bytes 262148 | tf_op args[0]
  2.4 1.4 %reshape_reshape.3 = f32[2,16,2,16,2,16]{5,4,3,2,1,0:T(2,128)S(1)} reshape(f32[32768]{0:T(1024)S(1)} %reduce.6) | data formatting | bytes 262144 | tf_op jit(solution)/shard_map/reshape;reshape | solution.py:130
  5.1 29.5 %all-to-all-start = ((f32[32,1,8]{2,1,0:T(1,128)}), f32[32,1,8]{2,1,0:T(1,128)S(1)}, u32[]{:S(2)}, u32[]{:S(2)}) async-start(f32[32,1,8]{2,1,0:T(1,128)} %broadcast_in_dim.106), calls=%async_computation | async-start | bytes 32768 | tf_op jit(solution)/shard_map/all_to_all | solution.py:96
  38.0 2.0 %reshape.152 = f32[64,64,64]{2,1,0:T(8,128)S(1)} reshape(f32[64,4096]{1,0:T(8,128)} %param.4) | data formatting | bytes 2097152 | tf_op jit(solution)/shard_map/reshape | solution.py:122
  46.3 1.6 %fusion = bf16[64,64,64]{1,2,0:T(8,128)(2,1)} fusion(f32[64,64,64]{2,1,0:T(8,128)S(1)} %fusion.45, bf16[64,64,64]{2,1,0:T(8,128)(2,1)S(1)} %add_convert_fusion.1), kind=kOutput, calls=%fused_computation.14 | convolution fusion | flops 34144256 | bytes 2097152 | tf_op jit(solution)/shard_map/nk,xkz->xnz/dot_general | solution.py:37
  47.9 4.0 %copy.45 = bf16[64,64,64]{0,2,1:T(8,128)(2,1)} copy(bf16[64,64,64]{1,2,0:T(8,128)(2,1)} %fusion) | data formatting | bytes 1048576 | tf_op jit(solution)/shard_map/convert_element_type | solution.py:60
  51.8 3.1 %fusion.51 = f32[64,4096]{0,1} fusion(bf16[64,4096]{0,1:T(8,128)(2,1)} %bitcast.68), kind=kOutput, calls=%fused_computation.100 | convolution fusion | flops 33619968 | bytes 1572864
  55.0 1.6 %fusion.1 = bf16[64,64,64]{1,2,0:T(8,128)(2,1)} fusion(f32[64,64,64]{2,1,0:T(8,128)S(1)} %fusion.41, bf16[64,64,64]{2,1,0:T(8,128)(2,1)S(1)} %subtract_convert_fusion.1), kind=kOutput, calls=%fused_computation.15 | convolution fusion | flops 34144256 | bytes 2097152 | tf_op jit(solution)/shard_map/nk,xkz->xnz/dot_general | solution.py:37
  56.5 3.3 %copy.48 = bf16[64,64,64]{0,2,1:T(8,128)(2,1)S(1)} copy(bf16[64,64,64]{1,2,0:T(8,128)(2,1)} %fusion.1) | data formatting | bytes 1048576 | tf_op jit(solution)/shard_map/convert_element_type | solution.py:61
  60.4 1.0 copy-done
  61.8 0.9 fusion.164
  62.7 3.0 %collective-permute-start = (f32[64,64,16]{0,2,1:T(8,128)}, f32[64,64,16]{0,2,1:T(8,128)S(1)}, u32[]{:S(2)}, u32[]{:S(2)}) collective-permute-start(f32[64,64,16]{0,2,1:T(8,128)} %get-tuple-element.11), channel_id=1, source_target_pairs={{0,1},{1,2},{2,3},{3,4},{4,5},{5,6},{6,7},{7,8},{8,9},{9,10},{10,1... | collective-permute-start | bytes 786440 | tf_op jit(solution)/shard_map/ppermute | solution.py:17
  65.7 1.3 %collective-permute-start.1 = (f32[64,64,16]{0,2,1:T(8,128)S(1)}, f32[64,64,16]{0,2,1:T(8,128)}, u32[]{:S(2)}, u32[]{:S(2)}) collective-permute-start(f32[64,64,16]{0,2,1:T(8,128)S(1)} %get-tuple-element.12), channel_id=1, source_target_pairs={{1,0},{2,1},{3,2},{4,3},{5,4},{6,5},{7,6},{8,7},{9,8},{10,9},{11,1... | collective-permute-start | bytes 786440 | tf_op jit(solution)/shard_map/ppermute | solution.py:17
  67.8 8.6 %all-to-all-start.1 = ((f32[32,1,8]{2,1,0:T(1,128)}), f32[32,1,8]{2,1,0:T(1,128)S(1)}, u32[]{:S(2)}, u32[]{:S(2)}) async-start(f32[32,1,8]{2,1,0:T(1,128)} %broadcast_in_dim.113), calls=%async_computation.1 | async-start | bytes 32768 | tf_op jit(solution)/shard_map/all_to_all | solution.py:96
  76.5 0.8 copy-done.2
  77.3 2.5 %collective-permute-done.1 = f32[64,64,16]{0,2,1:T(8,128)} collective-permute-done((f32[64,64,16]{0,2,1:T(8,128)S(1)}, f32[64,64,16]{0,2,1:T(8,128)}, u32[]{:S(2)}, u32[]{:S(2)}) %collective-permute-start.1) | collective-permute-done | bytes 262176 | tf_op jit(solution)/shard_map/ppermute | solution.py:17
  79.7 1.3 %slice_add_fusion = (f32[64,64,16]{0,2,1:T(8,128)S(1)}, f32[64,64,16]{0,2,1:T(8,128)S(1)}) fusion(f32[64,64,16]{0,2,1:T(8,128)} %collective-permute-done.1, f32[64,64,64]{0,2,1:T(8,128)S(1)} %sub.21, f32[64,64,16]{0,2,1:T(8,128)} %copy-done.2), kind=kLoop, calls=%fused_computation.34 | loop fusion | flops 131072 | bytes 1572864 | tf_op jit(solution)/shard_map/add | solution.py:90
  82.0 6.9 %collective-permute-start.2 = (f32[256,128]{1,0:T(8,128)S(1)}, f32[256,128]{1,0:T(8,128)S(1)}, u32[]{:S(2)}, u32[]{:S(2)}) collective-permute-start(f32[256,128]{1,0:T(8,128)S(1)} %reshape.154), channel_id=1, source_target_pairs={{0,32},{32,64},{64,96},{1,33},{33,65},{65,97},{2,34},{34,66},{66,9... | collective-permute-start | bytes 393224 | tf_op jit(solution)/shard_map/ppermute | solution.py:17
  88.9 1.9 %collective-permute-start.3 = (f32[256,128]{1,0:T(8,128)S(1)}, f32[256,128]{1,0:T(8,128)S(1)}, u32[]{:S(2)}, u32[]{:S(2)}) collective-permute-start(f32[256,128]{1,0:T(8,128)S(1)} %reshape.153), channel_id=1, source_target_pairs={{32,0},{64,32},{96,64},{33,1},{65,33},{97,65},{34,2},{66,34},{98,6... | collective-permute-start | bytes 393224 | tf_op jit(solution)/shard_map/ppermute | solution.py:17
  91.1 5.6 %collective-permute-done.3 = f32[256,128]{1,0:T(8,128)S(1)} collective-permute-done((f32[256,128]{1,0:T(8,128)S(1)}, f32[256,128]{1,0:T(8,128)S(1)}, u32[]{:S(2)}, u32[]{:S(2)}) %collective-permute-start.3) | collective-permute-done | bytes 131104 | tf_op jit(solution)/shard_map/ppermute | solution.py:17
  98.7 2.2 %collective-permute-start.4 = (f32[128,128]{1,0:T(8,128)S(1)}, f32[128,128]{1,0:T(8,128)S(1)}, u32[]{:S(2)}, u32[]{:S(2)}) collective-permute-start(f32[128,128]{1,0:T(8,128)S(1)} %reshape.158), channel_id=1, source_target_pairs={{0,128},{128,256},{256,384},{384,512},{512,640},{640,768},{768,896... | collective-permute-start | bytes 196616 | tf_op jit(solution)/shard_map/ppermute | solution.py:17
  100.9 1.3 %collective-permute-start.5 = (f32[128,128]{1,0:T(8,128)S(1)}, f32[128,128]{1,0:T(8,128)S(1)}, u32[]{:S(2)}, u32[]{:S(2)}) collective-permute-start(f32[128,128]{1,0:T(8,128)S(1)} %reshape.157), channel_id=1, source_target_pairs={{128,0},{256,128},{384,256},{512,384},{640,512},{768,640},{896,768... | collective-permute-start | bytes 196616 | tf_op jit(solution)/shard_map/ppermute | solution.py:17
  102.9 1.4 %reshape.161 = f32[1,1,1,32768]{3,2,1,0:T(1,128)S(1)} reshape(f32[2,16,2,16,2,16]{5,4,3,2,1,0:T(2,128)S(1)} %broadcast_in_dim.118) | data formatting | bytes 262144 | tf_op jit(solution)/shard_map/reshape | solution.py:134
  104.7 2.0 %collective-permute-done.5 = f32[128,128]{1,0:T(8,128)S(1)} collective-permute-done((f32[128,128]{1,0:T(8,128)S(1)}, f32[128,128]{1,0:T(8,128)S(1)}, u32[]{:S(2)}, u32[]{:S(2)}) %collective-permute-start.5) | collective-permute-done | bytes 65568 | tf_op jit(solution)/shard_map/ppermute | solution.py:17
  (78 shorter events, 19.6 us)
Async XLA Ops:
  0.0 34.6 %copy-start.1 = (f32[1,1,1,32768]{3,2,1,0:T(1,128)S(1)}, f32[1,1,1,32768]{3,2,1,0:T(1,128)}, u32[]{:S(2)}) copy-start(f32[1,1,1,32768]{3,2,1,0:T(1,128)} %param.3) | copy-start | bytes 393220
  5.1 62.0 %all-to-all-start = ((f32[32,1,8]{2,1,0:T(1,128)}), f32[32,1,8]{2,1,0:T(1,128)S(1)}, u32[]{:S(2)}, u32[]{:S(2)}) async-start(f32[32,1,8]{2,1,0:T(1,128)} %broadcast_in_dim.106), calls=%async_computation | async-start | bytes 32768 | tf_op jit(solution)/shard_map/all_to_all | solution.py:96
  59.8 1.6 %copy-start = (f32[64,4096]{0,1:S(1)}, f32[64,4096]{0,1}, u32[]{:S(2)}) copy-start(f32[64,4096]{0,1} %fusion.51) | copy-start | bytes 3145732
  62.7 13.7 %collective-permute-start = (f32[64,64,16]{0,2,1:T(8,128)}, f32[64,64,16]{0,2,1:T(8,128)S(1)}, u32[]{:S(2)}, u32[]{:S(2)}) collective-permute-start(f32[64,64,16]{0,2,1:T(8,128)} %get-tuple-element.11), channel_id=1, source_target_pairs={{0,1},{1,2},{2,3},{3,4},{4,5},{5,6},{6,7},{7,8},{8,9},{9,10},{10,1... | collective-permute-start | bytes 786440 | tf_op jit(solution)/shard_map/ppermute | solution.py:17
  65.7 14.0 %collective-permute-start.1 = (f32[64,64,16]{0,2,1:T(8,128)S(1)}, f32[64,64,16]{0,2,1:T(8,128)}, u32[]{:S(2)}, u32[]{:S(2)}) collective-permute-start(f32[64,64,16]{0,2,1:T(8,128)S(1)} %get-tuple-element.12), channel_id=1, source_target_pairs={{1,0},{2,1},{3,2},{4,3},{5,4},{6,5},{7,6},{8,7},{9,8},{10,9},{11,1... | collective-permute-start | bytes 786440 | tf_op jit(solution)/shard_map/ppermute | solution.py:17
  67.8 23.2 %all-to-all-start.1 = ((f32[32,1,8]{2,1,0:T(1,128)}), f32[32,1,8]{2,1,0:T(1,128)S(1)}, u32[]{:S(2)}, u32[]{:S(2)}) async-start(f32[32,1,8]{2,1,0:T(1,128)} %broadcast_in_dim.113), calls=%async_computation.1 | async-start | bytes 32768 | tf_op jit(solution)/shard_map/all_to_all | solution.py:96
  76.4 0.8 copy-start.2
  82.0 15.1 %collective-permute-start.2 = (f32[256,128]{1,0:T(8,128)S(1)}, f32[256,128]{1,0:T(8,128)S(1)}, u32[]{:S(2)}, u32[]{:S(2)}) collective-permute-start(f32[256,128]{1,0:T(8,128)S(1)} %reshape.154), channel_id=1, source_target_pairs={{0,32},{32,64},{64,96},{1,33},{33,65},{65,97},{2,34},{34,66},{66,9... | collective-permute-start | bytes 393224 | tf_op jit(solution)/shard_map/ppermute | solution.py:17
  88.9 7.8 %collective-permute-start.3 = (f32[256,128]{1,0:T(8,128)S(1)}, f32[256,128]{1,0:T(8,128)S(1)}, u32[]{:S(2)}, u32[]{:S(2)}) collective-permute-start(f32[256,128]{1,0:T(8,128)S(1)} %reshape.153), channel_id=1, source_target_pairs={{32,0},{64,32},{96,64},{33,1},{65,33},{97,65},{34,2},{66,34},{98,6... | collective-permute-start | bytes 393224 | tf_op jit(solution)/shard_map/ppermute | solution.py:17
  97.7 4.7 %copy-start.3 = (f32[2,2,2]{2,1,0:T(2,128)S(1)}, f32[2,2,2]{2,1,0:T(2,128)}, u32[]{:S(2)}) copy-start(f32[2,2,2]{2,1,0:T(2,128)} %param.5) | copy-start | bytes 100
  98.7 5.6 %collective-permute-start.4 = (f32[128,128]{1,0:T(8,128)S(1)}, f32[128,128]{1,0:T(8,128)S(1)}, u32[]{:S(2)}, u32[]{:S(2)}) collective-permute-start(f32[128,128]{1,0:T(8,128)S(1)} %reshape.158), channel_id=1, source_target_pairs={{0,128},{128,256},{256,384},{384,512},{512,640},{640,768},{768,896... | collective-permute-start | bytes 196616 | tf_op jit(solution)/shard_map/ppermute | solution.py:17
  100.9 5.7 %collective-permute-start.5 = (f32[128,128]{1,0:T(8,128)S(1)}, f32[128,128]{1,0:T(8,128)S(1)}, u32[]{:S(2)}, u32[]{:S(2)}) collective-permute-start(f32[128,128]{1,0:T(8,128)S(1)} %reshape.157), channel_id=1, source_target_pairs={{128,0},{256,128},{384,256},{512,384},{640,512},{768,640},{896,768... | collective-permute-start | bytes 196616 | tf_op jit(solution)/shard_map/ppermute | solution.py:17

commit v9 on v8

--- a/solution.py
+++ b/solution.py
@@ -106,14 +106,13 @@
 
 
 def far_sum(flat):
-    nz = lax.axis_size("gz")
-    zlevels = nz.bit_length() - 1
-    line = gather_rows(flat, "gz")
-    total = level_sums(line, lax.axis_index("gz"), 1, lambda level: 2**level)
+    inner = ("gy", "gz")
+    inner_levels = lax.axis_size(inner).bit_length() - 1
+    line = gather_rows(flat, inner)
+    total = level_sums(line, lax.axis_index(inner), 1, lambda level: 2**level)
     line_sum = jnp.sum(line, axis=0)
-    plane = gather_rows(line_sum, ("gx", "gy"))
-    ab = lax.axis_index(("gx", "gy"))
-    return total + level_sums(plane, ab, 1, lambda level: 2 ** (level + zlevels))
+    plane = gather_rows(line_sum, "gx")
+    return total + level_sums(plane, lax.axis_index("gx"), 1, lambda level: 2 ** (level + inner_levels))
 
 
 def local(vorticity, green_spectrum, coupling):

time: 111 us -> 116 us (1.045)
  waiting for transfers between devices: 10.1 us -> 15.2 us
    ppermute x6, waiting for transfers between devices: 10.1 us -> 15.2 us  [from_behind(): return lax.ppermute(block, axis, route)]
  transfers between devices with their start and end apart: 8 -> 8, of which waited for: 3 -> 4; matrix products, arithmetic and copies ran while one was open for 30% -> 29% of each run, Pallas kernels for 0% -> 0%
where the time goes in v9:
time: 116 us; the launch traced here: 114 us
  starting transfers between devices  54.3 us (47%)
  local copies, waits for them, and re-layouts  21.7 us (19%)
  matrix products  15.4 us (13%)
  waiting for transfers between devices  15.2 us (13%)
  other arithmetic  6.93 us (6%)
    all_to_all x2, starting transfers between devices, gather_rows(): return lax.all_to_all(rows, axes, 0, 0, tiled=True)  38 us
    ppermute x6, starting transfers between devices, from_behind(): return lax.ppermute(block, axis, route)  16.4 us
    ppermute x6, waiting for transfers between devices, from_behind(): return lax.ppermute(block, axis, route)  15.2 us
    dot_general x16, matrix products, mixed(): return jnp.einsum(form, table, data, preferred_element_type=jnp.float32)  11.1 us
    unnamed x4, matrix products  4.35 us
    convert_element_type x1, local copies, waits for them, and re-layouts, local_box(): new_real = (mixed(form, cosv, real) - mixed(form, sinv, imag)).astype(bf)  3.98 us
    convert_element_type x1, local copies, waits for them, and re-layouts, local_box(): imag = (mixed(form, cosv, imag) + mixed(form, sinv, real)).astype(bf)  3.3 us
    unnamed x9, local copies, waits for them, and re-layouts  2.37 us
  transfers between devices with their start and end apart: 8, of which 4 were waited for; matrix products, arithmetic and copies ran while one was open for 29% of the time, Pallas kernels for 0%

profile of v9, /device:TPU:1, one launch (start us, length us, event | category | flops | bytes accessed | tf_op | source)
XLA Modules:
  0.0 114.1 jit_solution(10176516369618534231)
XLA Ops:
  0.5 1.9 %reduce.6 = f32[32768]{0:T(1024)S(1)} reduce(f32[1,1,1,32768]{3,2,1,0:T(1,128)} %param.3, f32[]{:T(128)} %broadcast.400), dimensions={0,1,2}, to_apply=%param.3.reduce_sub_computation.3 | reduce | bytes 262148 | tf_op args[0]
  2.4 1.4 %reshape_reshape.3 = f32[2,16,2,16,2,16]{5,4,3,2,1,0:T(2,128)S(1)} reshape(f32[32768]{0:T(1024)S(1)} %reduce.6) | data formatting | bytes 262144 | tf_op jit(solution)/shard_map/reshape;reshape | solution.py:129
  5.2 33.7 %all-to-all-start = ((f32[128,1,8]{2,1,0:T(1,128)}), f32[128,1,8]{2,1,0:T(1,128)S(1)}, u32[]{:S(2)}, u32[]{:S(2)}) async-start(f32[128,1,8]{2,1,0:T(1,128)} %broadcast_in_dim.112), calls=%async_computation | async-start | bytes 131072 | tf_op jit(solution)/shard_map/all_to_all | solution.py:96
  42.4 2.0 %reshape.161 = f32[64,64,64]{2,1,0:T(8,128)S(1)} reshape(f32[64,4096]{1,0:T(8,128)} %param.4) | data formatting | bytes 2097152 | tf_op jit(solution)/shard_map/reshape | solution.py:121
  50.6 1.6 %fusion = bf16[64,64,64]{1,2,0:T(8,128)(2,1)} fusion(f32[64,64,64]{2,1,0:T(8,128)S(1)} %fusion.45, bf16[64,64,64]{2,1,0:T(8,128)(2,1)S(1)} %add_convert_fusion.1), kind=kOutput, calls=%fused_computation.14 | convolution fusion | flops 34144256 | bytes 2097152 | tf_op jit(solution)/shard_map/nk,xkz->xnz/dot_general | solution.py:37
  52.2 4.0 %copy.45 = bf16[64,64,64]{0,2,1:T(8,128)(2,1)} copy(bf16[64,64,64]{1,2,0:T(8,128)(2,1)} %fusion) | data formatting | bytes 1048576 | tf_op jit(solution)/shard_map/convert_element_type | solution.py:60
  56.2 3.1 %fusion.51 = f32[64,4096]{0,1} fusion(bf16[64,4096]{0,1:T(8,128)(2,1)} %bitcast.68), kind=kOutput, calls=%fused_computation.97 | convolution fusion | flops 33619968 | bytes 1572864
  59.3 1.6 %fusion.1 = bf16[64,64,64]{1,2,0:T(8,128)(2,1)} fusion(f32[64,64,64]{2,1,0:T(8,128)S(1)} %fusion.41, bf16[64,64,64]{2,1,0:T(8,128)(2,1)S(1)} %subtract_convert_fusion.1), kind=kOutput, calls=%fused_computation.15 | convolution fusion | flops 34144256 | bytes 2097152 | tf_op jit(solution)/shard_map/nk,xkz->xnz/dot_general | solution.py:37
  60.9 3.3 %copy.48 = bf16[64,64,64]{0,2,1:T(8,128)(2,1)S(1)} copy(bf16[64,64,64]{1,2,0:T(8,128)(2,1)} %fusion.1) | data formatting | bytes 1048576 | tf_op jit(solution)/shard_map/convert_element_type | solution.py:61
  64.7 1.0 copy-done
  66.2 0.9 fusion.154
  67.1 3.3 %collective-permute-start = (f32[64,64,16]{0,2,1:T(8,128)}, f32[64,64,16]{0,2,1:T(8,128)S(1)}, u32[]{:S(2)}, u32[]{:S(2)}) collective-permute-start(f32[64,64,16]{0,2,1:T(8,128)} %get-tuple-element.11), channel_id=1, source_target_pairs={{0,1},{1,2},{2,3},{3,4},{4,5},{5,6},{6,7},{7,8},{8,9},{9,10},{10,1... | collective-permute-start | bytes 786440 | tf_op jit(solution)/shard_map/ppermute | solution.py:17
  70.4 1.3 %collective-permute-start.1 = (f32[64,64,16]{0,2,1:T(8,128)S(1)}, f32[64,64,16]{0,2,1:T(8,128)}, u32[]{:S(2)}, u32[]{:S(2)}) collective-permute-start(f32[64,64,16]{0,2,1:T(8,128)S(1)} %get-tuple-element.12), channel_id=1, source_target_pairs={{1,0},{2,1},{3,2},{4,3},{5,4},{6,5},{7,6},{8,7},{9,8},{10,9},{11,1... | collective-permute-start | bytes 786440 | tf_op jit(solution)/shard_map/ppermute | solution.py:17
  72.5 4.2 %all-to-all-start.1 = ((f32[8,1,8]{2,1,0:T(1,128)}), f32[8,1,8]{2,1,0:T(1,128)S(1)}, u32[]{:S(2)}, u32[]{:S(2)}) async-start(f32[8,1,8]{2,1,0:T(1,128)} %broadcast_in_dim.121), calls=%async_computation.1 | async-start | bytes 8192 | tf_op jit(solution)/shard_map/all_to_all | solution.py:96
  76.8 4.9 %collective-permute-done = f32[64,64,16]{0,2,1:T(8,128)S(1)} collective-permute-done((f32[64,64,16]{0,2,1:T(8,128)}, f32[64,64,16]{0,2,1:T(8,128)S(1)}, u32[]{:S(2)}, u32[]{:S(2)}) %collective-permute-start) | collective-permute-done | bytes 262176 | tf_op jit(solution)/shard_map/ppermute | solution.py:17
  82.4 2.8 %collective-permute-done.1 = f32[64,64,16]{0,2,1:T(8,128)} collective-permute-done((f32[64,64,16]{0,2,1:T(8,128)S(1)}, f32[64,64,16]{0,2,1:T(8,128)}, u32[]{:S(2)}, u32[]{:S(2)}) %collective-permute-start.1) | collective-permute-done | bytes 262176 | tf_op jit(solution)/shard_map/ppermute | solution.py:17
  85.3 1.3 %slice_add_fusion = (f32[64,64,16]{0,2,1:T(8,128)S(1)}, f32[64,64,16]{0,2,1:T(8,128)S(1)}) fusion(f32[64,64,16]{0,2,1:T(8,128)} %collective-permute-done.1, f32[64,64,64]{0,2,1:T(8,128)S(1)} %sub.21, f32[64,64,16]{0,2,1:T(8,128)} %copy-done.2), kind=kLoop, calls=%fused_computation.34 | loop fusion | flops 131072 | bytes 1572864 | tf_op jit(solution)/shard_map/add | solution.py:90
  87.6 6.4 %collective-permute-start.2 = (f32[256,128]{1,0:T(8,128)S(1)}, f32[256,128]{1,0:T(8,128)S(1)}, u32[]{:S(2)}, u32[]{:S(2)}) collective-permute-start(f32[256,128]{1,0:T(8,128)S(1)} %reshape.163), channel_id=1, source_target_pairs={{0,32},{32,64},{64,96},{1,33},{33,65},{65,97},{2,34},{34,66},{66,9... | collective-permute-start | bytes 393224 | tf_op jit(solution)/shard_map/ppermute | solution.py:17
  94.0 1.9 %collective-permute-start.3 = (f32[256,128]{1,0:T(8,128)S(1)}, f32[256,128]{1,0:T(8,128)S(1)}, u32[]{:S(2)}, u32[]{:S(2)}) collective-permute-start(f32[256,128]{1,0:T(8,128)S(1)} %reshape.162), channel_id=1, source_target_pairs={{32,0},{64,32},{96,64},{33,1},{65,33},{97,65},{34,2},{66,34},{98,6... | collective-permute-start | bytes 393224 | tf_op jit(solution)/shard_map/ppermute | solution.py:17
  96.2 5.6 %collective-permute-done.3 = f32[256,128]{1,0:T(8,128)S(1)} collective-permute-done((f32[256,128]{1,0:T(8,128)S(1)}, f32[256,128]{1,0:T(8,128)S(1)}, u32[]{:S(2)}, u32[]{:S(2)}) %collective-permute-start.3) | collective-permute-done | bytes 131104 | tf_op jit(solution)/shard_map/ppermute | solution.py:17
  103.7 2.2 %collective-permute-start.4 = (f32[128,128]{1,0:T(8,128)S(1)}, f32[128,128]{1,0:T(8,128)S(1)}, u32[]{:S(2)}, u32[]{:S(2)}) collective-permute-start(f32[128,128]{1,0:T(8,128)S(1)} %reshape.167), channel_id=1, source_target_pairs={{0,128},{128,256},{256,384},{384,512},{512,640},{640,768},{768,896... | collective-permute-start | bytes 196616 | tf_op jit(solution)/shard_map/ppermute | solution.py:17
  105.9 1.3 %collective-permute-start.5 = (f32[128,128]{1,0:T(8,128)S(1)}, f32[128,128]{1,0:T(8,128)S(1)}, u32[]{:S(2)}, u32[]{:S(2)}) collective-permute-start(f32[128,128]{1,0:T(8,128)S(1)} %reshape.166), channel_id=1, source_target_pairs={{128,0},{256,128},{384,256},{512,384},{640,512},{768,640},{896,768... | collective-permute-start | bytes 196616 | tf_op jit(solution)/shard_map/ppermute | solution.py:17
  107.9 1.4 %reshape.170 = f32[1,1,1,32768]{3,2,1,0:T(1,128)S(1)} reshape(f32[2,16,2,16,2,16]{5,4,3,2,1,0:T(2,128)S(1)} %broadcast_in_dim.125) | data formatting | bytes 262144 | tf_op jit(solution)/shard_map/reshape | solution.py:133
  109.7 2.0 %collective-permute-done.5 = f32[128,128]{1,0:T(8,128)S(1)} collective-permute-done((f32[128,128]{1,0:T(8,128)S(1)}, f32[128,128]{1,0:T(8,128)S(1)}, u32[]{:S(2)}, u32[]{:S(2)}) %collective-permute-start.5) | collective-permute-done | bytes 65568 | tf_op jit(solution)/shard_map/ppermute | solution.py:17
  (78 shorter events, 20.6 us)
Async XLA Ops:
  0.0 39.0 %copy-start.1 = (f32[1,1,1,32768]{3,2,1,0:T(1,128)S(1)}, f32[1,1,1,32768]{3,2,1,0:T(1,128)}, u32[]{:S(2)}) copy-start(f32[1,1,1,32768]{3,2,1,0:T(1,128)} %param.3) | copy-start | bytes 393220
  5.2 66.6 %all-to-all-start = ((f32[128,1,8]{2,1,0:T(1,128)}), f32[128,1,8]{2,1,0:T(1,128)S(1)}, u32[]{:S(2)}, u32[]{:S(2)}) async-start(f32[128,1,8]{2,1,0:T(1,128)} %broadcast_in_dim.112), calls=%async_computation | async-start | bytes 131072 | tf_op jit(solution)/shard_map/all_to_all | solution.py:96
  64.2 1.6 %copy-start = (f32[64,4096]{0,1:S(1)}, f32[64,4096]{0,1}, u32[]{:S(2)}) copy-start(f32[64,4096]{0,1} %fusion.51) | copy-start | bytes 3145732
  67.1 14.5 %collective-permute-start = (f32[64,64,16]{0,2,1:T(8,128)}, f32[64,64,16]{0,2,1:T(8,128)S(1)}, u32[]{:S(2)}, u32[]{:S(2)}) collective-permute-start(f32[64,64,16]{0,2,1:T(8,128)} %get-tuple-element.11), channel_id=1, source_target_pairs={{0,1},{1,2},{2,3},{3,4},{4,5},{5,6},{6,7},{7,8},{8,9},{9,10},{10,1... | collective-permute-start | bytes 786440 | tf_op jit(solution)/shard_map/ppermute | solution.py:17
  70.4 14.9 %collective-permute-start.1 = (f32[64,64,16]{0,2,1:T(8,128)S(1)}, f32[64,64,16]{0,2,1:T(8,128)}, u32[]{:S(2)}, u32[]{:S(2)}) collective-permute-start(f32[64,64,16]{0,2,1:T(8,128)S(1)} %get-tuple-element.12), channel_id=1, source_target_pairs={{1,0},{2,1},{3,2},{4,3},{5,4},{6,5},{7,6},{8,7},{9,8},{10,9},{11,1... | collective-permute-start | bytes 786440 | tf_op jit(solution)/shard_map/ppermute | solution.py:17
  72.5 23.6 %all-to-all-start.1 = ((f32[8,1,8]{2,1,0:T(1,128)}), f32[8,1,8]{2,1,0:T(1,128)S(1)}, u32[]{:S(2)}, u32[]{:S(2)}) async-start(f32[8,1,8]{2,1,0:T(1,128)} %broadcast_in_dim.121), calls=%async_computation.1 | async-start | bytes 8192 | tf_op jit(solution)/shard_map/all_to_all | solution.py:96
  81.6 0.8 copy-start.2
  87.6 14.6 %collective-permute-start.2 = (f32[256,128]{1,0:T(8,128)S(1)}, f32[256,128]{1,0:T(8,128)S(1)}, u32[]{:S(2)}, u32[]{:S(2)}) collective-permute-start(f32[256,128]{1,0:T(8,128)S(1)} %reshape.163), channel_id=1, source_target_pairs={{0,32},{32,64},{64,96},{1,33},{33,65},{65,97},{2,34},{34,66},{66,9... | collective-permute-start | bytes 393224 | tf_op jit(solution)/shard_map/ppermute | solution.py:17
  94.0 7.8 %collective-permute-start.3 = (f32[256,128]{1,0:T(8,128)S(1)}, f32[256,128]{1,0:T(8,128)S(1)}, u32[]{:S(2)}, u32[]{:S(2)}) collective-permute-start(f32[256,128]{1,0:T(8,128)S(1)} %reshape.162), channel_id=1, source_target_pairs={{32,0},{64,32},{96,64},{33,1},{65,33},{97,65},{34,2},{66,34},{98,6... | collective-permute-start | bytes 393224 | tf_op jit(solution)/shard_map/ppermute | solution.py:17
  102.7 4.7 %copy-start.3 = (f32[2,2,2]{2,1,0:T(2,128)S(1)}, f32[2,2,2]{2,1,0:T(2,128)}, u32[]{:S(2)}) copy-start(f32[2,2,2]{2,1,0:T(2,128)} %param.5) | copy-start | bytes 100
  103.7 5.6 %collective-permute-start.4 = (f32[128,128]{1,0:T(8,128)S(1)}, f32[128,128]{1,0:T(8,128)S(1)}, u32[]{:S(2)}, u32[]{:S(2)}) collective-permute-start(f32[128,128]{1,0:T(8,128)S(1)} %reshape.167), channel_id=1, source_target_pairs={{0,128},{128,256},{256,384},{384,512},{512,640},{640,768},{768,896... | collective-permute-start | bytes 196616 | tf_op jit(solution)/shard_map/ppermute | solution.py:17
  105.9 5.7 %collective-permute-start.5 = (f32[128,128]{1,0:T(8,128)S(1)}, f32[128,128]{1,0:T(8,128)S(1)}, u32[]{:S(2)}, u32[]{:S(2)}) collective-permute-start(f32[128,128]{1,0:T(8,128)S(1)} %reshape.166), channel_id=1, source_target_pairs={{128,0},{256,128},{384,256},{512,384},{640,512},{768,640},{896,768... | collective-permute-start | bytes 196616 | tf_op jit(solution)/shard_map/ppermute | solution.py:17

commit v10 on v8

--- a/solution.py
+++ b/solution.py
@@ -90,10 +90,10 @@
     return jnp.concatenate([first + from_left, second + from_right], axis=dim)
 
 
-def gather_rows(value, axes):
-    count = lax.axis_size(axes)
+def gather_rows(value, axes, groups=None):
+    count = lax.axis_size(axes) if groups is None else len(groups[0])
     rows = jnp.broadcast_to(value[None, :], (count, value.shape[0]))
-    return lax.all_to_all(rows, axes, 0, 0, tiled=True)
+    return lax.all_to_all(rows, axes, 0, 0, tiled=True, axis_index_groups=groups)
 
 
 def level_sums(rows, me, first_level, group_of):
@@ -105,12 +105,21 @@
     return total
 
 
-def far_sum(flat):
+def line_sums(flat):
     nz = lax.axis_size("gz")
-    zlevels = nz.bit_length() - 1
-    line = gather_rows(flat, "gz")
-    total = level_sums(line, lax.axis_index("gz"), 1, lambda level: 2**level)
-    line_sum = jnp.sum(line, axis=0)
+    c = lax.axis_index("gz")
+    near = 4
+    groups = [[start + i for i in range(near)] for start in range(0, nz, near)]
+    local_rows = gather_rows(flat, "gz", groups)
+    total = level_sums(local_rows, c % near, 1, lambda level: 2**level)
+    strided = [[start + near * i for i in range(nz // near)] for start in range(near)]
+    group_rows = gather_rows(jnp.sum(local_rows, axis=0), "gz", strided)
+    total = total + level_sums(group_rows, c // near, 1, lambda level: near * 2**level)
+    return total, jnp.sum(group_rows, axis=0)
+
+
+def plane_sums(total, line_sum):
+    zlevels = lax.axis_size("gz").bit_length() - 1
     plane = gather_rows(line_sum, ("gx", "gy"))
     ab = lax.axis_index(("gx", "gy"))
     return total + level_sums(plane, ab, 1, lambda level: 2 ** (level + zlevels))
@@ -120,16 +129,18 @@
     px, py, pz = (PX, PY, PZ)
     patch = vorticity.reshape(px, py, pz)
     spectrum = green_spectrum.reshape(2 * px, 2 * py, 2 * pz)
+    cx, cy, cz = (px // CB, py // CB, pz // CB)
+    scale = 1.0 / math.sqrt(CB**3)
+    coarse = patch.reshape(cx, CB, cy, CB, cz, CB).sum(axis=(1, 3, 5)) * scale
+    flat = coarse.reshape(-1)
+    partial, line_sum = line_sums(flat)
+    partial, line_sum, patch = lax.optimization_barrier((partial, line_sum, patch))
     box = local_box(patch, spectrum)
     order = ((2, move_z), (1, move_y), (0, move_x))
     near = box
     for dim, mover in order:
         near = fold_margin(near, dim, mover, dim != 2)
-    cx, cy, cz = (px // CB, py // CB, pz // CB)
-    scale = 1.0 / math.sqrt(CB**3)
-    coarse = patch.reshape(cx, CB, cy, CB, cz, CB).sum(axis=(1, 3, 5)) * scale
-    flat = coarse.reshape(-1)
-    total = far_sum(flat)
+    total = plane_sums(partial, line_sum)
     far = total.reshape(cx, cy, cz) * coupling
     far_cells = jnp.broadcast_to(far[:, None, :, None, :, None], (cx, CB, cy, CB, cz, CB)).reshape(
         px, py, pz

time: 111 us -> 136 us (1.23)
  waiting for transfers between devices: 10.1 us -> 31.8 us
  starting transfers between devices: 54.7 us -> 59.4 us
    all_to_all x2 -> x3, waiting for transfers between devices: 0.01 us -> 24.1 us  [gather_rows(): lax.all_to_all(rows, axes, 0, 0, tiled=True, axis_index_groups=groups)]
    all_to_all x2 -> x3, starting transfers between devices: 38 us -> 42.7 us  [gather_rows(): lax.all_to_all(rows, axes, 0, 0, tiled=True, axis_index_groups=groups)]
    ppermute x6, waiting for transfers between devices: 10.1 us -> 7.7 us  [from_behind(): return lax.ppermute(block, axis, route)]
  transfers between devices with their start and end apart: 8 -> 9, of which waited for: 3 -> 4; matrix products, arithmetic and copies ran while one was open for 30% -> 5% of each run, Pallas kernels for 0% -> 0%
where the time goes in v10:
time: 136 us; the launch traced here: 135 us
  starting transfers between devices  59.4 us (44%)
  waiting for transfers between devices  31.8 us (23%)
  local copies, waits for them, and re-layouts  21.1 us (16%)
  matrix products  15.4 us (11%)
  other arithmetic  6.48 us (5%)
    all_to_all x3, starting transfers between devices, gather_rows(): lax.all_to_all(rows, axes, 0, 0, tiled=True, axis_index_groups=groups)  42.7 us
    all_to_all x3, waiting for transfers between devices, gather_rows(): lax.all_to_all(rows, axes, 0, 0, tiled=True, axis_index_groups=groups)  24.1 us
    ppermute x6, starting transfers between devices, from_behind(): return lax.ppermute(block, axis, route)  16.7 us
    dot_general x16, matrix products, mixed(): return jnp.einsum(form, table, data, preferred_element_type=jnp.float32)  11.1 us
    ppermute x6, waiting for transfers between devices, from_behind(): return lax.ppermute(block, axis, route)  7.7 us
    unnamed x4, matrix products  4.34 us
    convert_element_type x1, local copies, waits for them, and re-layouts, local_box(): new_real = (mixed(form, cosv, real) - mixed(form, sinv, imag)).astype(bf)  3.98 us
    convert_element_type x1, local copies, waits for them, and re-layouts, local_box(): imag = (mixed(form, cosv, imag) + mixed(form, sinv, real)).astype(bf)  3.3 us
  transfers between devices with their start and end apart: 9, of which 4 were waited for; matrix products, arithmetic and copies ran while one was open for 5% of the time, Pallas kernels for 0%

profile of v10, /device:TPU:1, one launch (start us, length us, event | category | flops | bytes accessed | tf_op | source)
XLA Modules:
  0.0 134.7 jit_solution(14918809515008679854)
XLA Ops:
  0.5 1.9 %reduce.7 = f32[32768]{0:T(1024)S(1)} reduce(f32[1,1,1,32768]{3,2,1,0:T(1,128)} %param.3, f32[]{:T(128)} %broadcast.386), dimensions={0,1,2}, to_apply=%param.3.reduce_sub_computation.5 | reduce | bytes 262148 | tf_op args[0]
  2.4 1.4 %reshape_reshape.3 = f32[2,16,2,16,2,16]{5,4,3,2,1,0:T(2,128)S(1)} reshape(f32[32768]{0:T(1024)S(1)} %reduce.7) | data formatting | bytes 262144 | tf_op jit(solution)/shard_map/reshape;reshape | solution.py:134
  5.1 6.4 %all-to-all-start = ((f32[4,1,8]{2,1,0:T(1,128)}), f32[4,1,8]{2,1,0:T(1,128)S(1)}, u32[]{:S(2)}, u32[]{:S(2)}) async-start(f32[4,1,8]{2,1,0:T(1,128)} %broadcast_in_dim.124), calls=%async_computation | async-start | bytes 4096 | tf_op jit(solution)/shard_map/all_to_all | solution.py:96
  12.7 3.2 %all-to-all-done = f32[4,1,8]{2,1,0:T(1,128)S(1)} async-done(((f32[4,1,8]{2,1,0:T(1,128)}), f32[4,1,8]{2,1,0:T(1,128)S(1)}, u32[]{:S(2)}, u32[]{:S(2)}) %all-to-all-start) | async-done | bytes 160 | tf_op jit(solution)/shard_map/all_to_all | solution.py:96
  16.5 25.6 %all-to-all-start.1 = ((f32[8,1,8]{2,1,0:T(1,128)}), f32[8,1,8]{2,1,0:T(1,128)S(1)}, u32[]{:S(2)}, u32[]{:S(2)}) async-start(f32[8,1,8]{2,1,0:T(1,128)} %broadcast_in_dim.128), calls=%async_computation.1 | async-start | bytes 8192 | tf_op jit(solution)/shard_map/all_to_all | solution.py:96
  42.3 20.8 %all-to-all-done.1 = f32[8,1,8]{2,1,0:T(1,128)S(1)} async-done(((f32[8,1,8]{2,1,0:T(1,128)}), f32[8,1,8]{2,1,0:T(1,128)S(1)}, u32[]{:S(2)}, u32[]{:S(2)}) %all-to-all-start.1) | async-done | bytes 288 | tf_op jit(solution)/shard_map/all_to_all | solution.py:96
  72.4 1.6 %fusion = bf16[64,64,64]{1,2,0:T(8,128)(2,1)} fusion(f32[64,64,64]{2,1,0:T(8,128)S(1)} %fusion.45, bf16[64,64,64]{2,1,0:T(8,128)(2,1)S(1)} %add_convert_fusion.1), kind=kOutput, calls=%fused_computation.14 | convolution fusion | flops 34144256 | bytes 2097152 | tf_op jit(solution)/shard_map/nk,xkz->xnz/dot_general | solution.py:37
  73.9 4.0 %copy.42 = bf16[64,64,64]{0,2,1:T(8,128)(2,1)} copy(bf16[64,64,64]{1,2,0:T(8,128)(2,1)} %fusion) | data formatting | bytes 1048576 | tf_op jit(solution)/shard_map/convert_element_type | solution.py:60
  77.9 3.1 %fusion.51 = f32[64,4096]{0,1} fusion(bf16[64,4096]{0,1:T(8,128)(2,1)} %bitcast.70), kind=kOutput, calls=%fused_computation.94 | convolution fusion | flops 33619968 | bytes 1572864
  81.0 1.6 %fusion.1 = bf16[64,64,64]{1,2,0:T(8,128)(2,1)} fusion(f32[64,64,64]{2,1,0:T(8,128)S(1)} %fusion.41, bf16[64,64,64]{2,1,0:T(8,128)(2,1)S(1)} %subtract_convert_fusion.1), kind=kOutput, calls=%fused_computation.15 | convolution fusion | flops 34144256 | bytes 2097152 | tf_op jit(solution)/shard_map/nk,xkz->xnz/dot_general | solution.py:37
  82.6 3.3 %copy.45 = bf16[64,64,64]{0,2,1:T(8,128)(2,1)S(1)} copy(bf16[64,64,64]{1,2,0:T(8,128)(2,1)} %fusion.1) | data formatting | bytes 1048576 | tf_op jit(solution)/shard_map/convert_element_type | solution.py:61
  86.5 1.0 copy-done
  87.9 0.9 fusion.154
  88.8 2.3 %collective-permute-start = (f32[64,64,16]{0,2,1:T(8,128)}, f32[64,64,16]{0,2,1:T(8,128)S(1)}, u32[]{:S(2)}, u32[]{:S(2)}) collective-permute-start(f32[64,64,16]{0,2,1:T(8,128)} %get-tuple-element.15), channel_id=1, source_target_pairs={{0,1},{1,2},{2,3},{3,4},{4,5},{5,6},{6,7},{7,8},{8,9},{9,10},{10,1... | collective-permute-start | bytes 786440 | tf_op jit(solution)/shard_map/ppermute | solution.py:17
  91.1 1.5 %collective-permute-start.1 = (f32[64,64,16]{0,2,1:T(8,128)S(1)}, f32[64,64,16]{0,2,1:T(8,128)}, u32[]{:S(2)}, u32[]{:S(2)}) collective-permute-start(f32[64,64,16]{0,2,1:T(8,128)S(1)} %get-tuple-element.16), channel_id=1, source_target_pairs={{1,0},{2,1},{3,2},{4,3},{5,4},{6,5},{7,6},{8,7},{9,8},{10,9},{11,1... | collective-permute-start | bytes 786440 | tf_op jit(solution)/shard_map/ppermute | solution.py:17
  93.3 10.6 %all-to-all-start.2 = ((f32[32,1,8]{2,1,0:T(1,128)}), f32[32,1,8]{2,1,0:T(1,128)S(1)}, u32[]{:S(2)}, u32[]{:S(2)}) async-start(f32[32,1,8]{2,1,0:T(1,128)} %broadcast_in_dim.133), calls=%async_computation.2 | async-start | bytes 32768 | tf_op jit(solution)/shard_map/all_to_all | solution.py:96
  104.8 1.3 slice_add_fusion
  107.1 7.5 %collective-permute-start.2 = (f32[256,128]{1,0:T(8,128)S(1)}, f32[256,128]{1,0:T(8,128)S(1)}, u32[]{:S(2)}, u32[]{:S(2)}) collective-permute-start(f32[256,128]{1,0:T(8,128)S(1)} %reshape.138), channel_id=1, source_target_pairs={{0,32},{32,64},{64,96},{1,33},{33,65},{65,97},{2,34},{34,66},{66,9... | collective-permute-start | bytes 393224 | tf_op jit(solution)/shard_map/ppermute | solution.py:17
  114.6 1.9 %collective-permute-start.3 = (f32[256,128]{1,0:T(8,128)S(1)}, f32[256,128]{1,0:T(8,128)S(1)}, u32[]{:S(2)}, u32[]{:S(2)}) collective-permute-start(f32[256,128]{1,0:T(8,128)S(1)} %reshape.137), channel_id=1, source_target_pairs={{32,0},{64,32},{96,64},{33,1},{65,33},{97,65},{34,2},{66,34},{98,6... | collective-permute-start | bytes 393224 | tf_op jit(solution)/shard_map/ppermute | solution.py:17
  116.7 5.7 %collective-permute-done.3 = f32[256,128]{1,0:T(8,128)S(1)} collective-permute-done((f32[256,128]{1,0:T(8,128)S(1)}, f32[256,128]{1,0:T(8,128)S(1)}, u32[]{:S(2)}, u32[]{:S(2)}) %collective-permute-start.3) | collective-permute-done | bytes 131104 | tf_op jit(solution)/shard_map/ppermute | solution.py:17
  124.3 2.2 %collective-permute-start.4 = (f32[128,128]{1,0:T(8,128)S(1)}, f32[128,128]{1,0:T(8,128)S(1)}, u32[]{:S(2)}, u32[]{:S(2)}) collective-permute-start(f32[128,128]{1,0:T(8,128)S(1)} %reshape.142), channel_id=1, source_target_pairs={{0,128},{128,256},{256,384},{384,512},{512,640},{640,768},{768,896... | collective-permute-start | bytes 196616 | tf_op jit(solution)/shard_map/ppermute | solution.py:17
  126.6 1.3 collective-permute-start.5
  128.5 1.4 %reshape.146 = f32[1,1,1,32768]{3,2,1,0:T(1,128)S(1)} reshape(f32[2,16,2,16,2,16]{5,4,3,2,1,0:T(2,128)S(1)} %broadcast_in_dim.139) | data formatting | bytes 262144 | tf_op jit(solution)/shard_map/reshape | solution.py:145
  130.3 2.0 %collective-permute-done.5 = f32[128,128]{1,0:T(8,128)S(1)} collective-permute-done((f32[128,128]{1,0:T(8,128)S(1)}, f32[128,128]{1,0:T(8,128)S(1)}, u32[]{:S(2)}, u32[]{:S(2)}) %collective-permute-start.5) | collective-permute-done | bytes 65568 | tf_op jit(solution)/shard_map/ppermute | solution.py:17
  (85 shorter events, 21.5 us)
Async XLA Ops:
  0.0 11.6 %copy-start.2 = (f32[1,1,1,32768]{3,2,1,0:T(1,128)S(1)}, f32[1,1,1,32768]{3,2,1,0:T(1,128)}, u32[]{:S(2)}) copy-start(f32[1,1,1,32768]{3,2,1,0:T(1,128)} %param.3) | copy-start | bytes 393220
  0.0 11.8 %copy-start.1 = (f32[64,4096]{1,0:T(8,128)S(1)}, f32[64,4096]{1,0:T(8,128)}, u32[]{:S(2)}) copy-start(f32[64,4096]{1,0:T(8,128)} %param.4) | copy-start | bytes 3145732
  5.1 10.8 %all-to-all-start = ((f32[4,1,8]{2,1,0:T(1,128)}), f32[4,1,8]{2,1,0:T(1,128)S(1)}, u32[]{:S(2)}, u32[]{:S(2)}) async-start(f32[4,1,8]{2,1,0:T(1,128)} %broadcast_in_dim.124), calls=%async_computation | async-start | bytes 4096 | tf_op jit(solution)/shard_map/all_to_all | solution.py:96
  16.5 46.5 %all-to-all-start.1 = ((f32[8,1,8]{2,1,0:T(1,128)}), f32[8,1,8]{2,1,0:T(1,128)S(1)}, u32[]{:S(2)}, u32[]{:S(2)}) async-start(f32[8,1,8]{2,1,0:T(1,128)} %broadcast_in_dim.128), calls=%async_computation.1 | async-start | bytes 8192 | tf_op jit(solution)/shard_map/all_to_all | solution.py:96
  85.9 1.6 %copy-start = (f32[64,4096]{0,1:S(1)}, f32[64,4096]{0,1}, u32[]{:S(2)}) copy-start(f32[64,4096]{0,1} %fusion.51) | copy-start | bytes 3145732
  88.8 15.2 %collective-permute-start = (f32[64,64,16]{0,2,1:T(8,128)}, f32[64,64,16]{0,2,1:T(8,128)S(1)}, u32[]{:S(2)}, u32[]{:S(2)}) collective-permute-start(f32[64,64,16]{0,2,1:T(8,128)} %get-tuple-element.15), channel_id=1, source_target_pairs={{0,1},{1,2},{2,3},{3,4},{4,5},{5,6},{6,7},{7,8},{8,9},{9,10},{10,1... | collective-permute-start | bytes 786440 | tf_op jit(solution)/shard_map/ppermute | solution.py:17
  91.1 13.6 %collective-permute-start.1 = (f32[64,64,16]{0,2,1:T(8,128)S(1)}, f32[64,64,16]{0,2,1:T(8,128)}, u32[]{:S(2)}, u32[]{:S(2)}) collective-permute-start(f32[64,64,16]{0,2,1:T(8,128)S(1)} %get-tuple-element.16), channel_id=1, source_target_pairs={{1,0},{2,1},{3,2},{4,3},{5,4},{6,5},{7,6},{8,7},{9,8},{10,9},{11,1... | collective-permute-start | bytes 786440 | tf_op jit(solution)/shard_map/ppermute | solution.py:17
  93.3 23.2 %all-to-all-start.2 = ((f32[32,1,8]{2,1,0:T(1,128)}), f32[32,1,8]{2,1,0:T(1,128)S(1)}, u32[]{:S(2)}, u32[]{:S(2)}) async-start(f32[32,1,8]{2,1,0:T(1,128)} %broadcast_in_dim.133), calls=%async_computation.2 | async-start | bytes 32768 | tf_op jit(solution)/shard_map/all_to_all | solution.py:96
  104.0 0.8 copy-start.3
  107.1 15.7 %collective-permute-start.2 = (f32[256,128]{1,0:T(8,128)S(1)}, f32[256,128]{1,0:T(8,128)S(1)}, u32[]{:S(2)}, u32[]{:S(2)}) collective-permute-start(f32[256,128]{1,0:T(8,128)S(1)} %reshape.138), channel_id=1, source_target_pairs={{0,32},{32,64},{64,96},{1,33},{33,65},{65,97},{2,34},{34,66},{66,9... | collective-permute-start | bytes 393224 | tf_op jit(solution)/shard_map/ppermute | solution.py:17
  114.6 7.8 %collective-permute-start.3 = (f32[256,128]{1,0:T(8,128)S(1)}, f32[256,128]{1,0:T(8,128)S(1)}, u32[]{:S(2)}, u32[]{:S(2)}) collective-permute-start(f32[256,128]{1,0:T(8,128)S(1)} %reshape.137), channel_id=1, source_target_pairs={{32,0},{64,32},{96,64},{33,1},{65,33},{97,65},{34,2},{66,34},{98,6... | collective-permute-start | bytes 393224 | tf_op jit(solution)/shard_map/ppermute | solution.py:17
  123.3 4.6 %copy-start.4 = (f32[2,2,2]{2,1,0:T(2,128)S(1)}, f32[2,2,2]{2,1,0:T(2,128)}, u32[]{:S(2)}) copy-start(f32[2,2,2]{2,1,0:T(2,128)} %param.5) | copy-start | bytes 100
  124.3 5.6 %collective-permute-start.4 = (f32[128,128]{1,0:T(8,128)S(1)}, f32[128,128]{1,0:T(8,128)S(1)}, u32[]{:S(2)}, u32[]{:S(2)}) collective-permute-start(f32[128,128]{1,0:T(8,128)S(1)} %reshape.142), channel_id=1, source_target_pairs={{0,128},{128,256},{256,384},{384,512},{512,640},{640,768},{768,896... | collective-permute-start | bytes 196616 | tf_op jit(solution)/shard_map/ppermute | solution.py:17
  126.6 5.7 %collective-permute-start.5 = (f32[128,128]{1,0:T(8,128)S(1)}, f32[128,128]{1,0:T(8,128)S(1)}, u32[]{:S(2)}, u32[]{:S(2)}) collective-permute-start(f32[128,128]{1,0:T(8,128)S(1)} %reshape.141), channel_id=1, source_target_pairs={{128,0},{256,128},{384,256},{512,384},{640,512},{768,640},{896,768... | collective-permute-start | bytes 196616 | tf_op jit(solution)/shard_map/ppermute | solution.py:17

commit v11 on v8

--- a/solution.py
+++ b/solution.py
@@ -127,7 +127,9 @@
         near = fold_margin(near, dim, mover, dim != 2)
     cx, cy, cz = (px // CB, py // CB, pz // CB)
     scale = 1.0 / math.sqrt(CB**3)
-    coarse = patch.reshape(cx, CB, cy, CB, cz, CB).sum(axis=(1, 3, 5)) * scale
+    lanes = 128 // pz
+    rows = vorticity.reshape(cx, CB, cy, py // cy // lanes, lanes * pz).sum(axis=(1, 3))
+    coarse = rows.reshape(cx, cy, lanes, cz, CB).sum(axis=(2, 4)) * scale
     flat = coarse.reshape(-1)
     total = far_sum(flat)
     far = total.reshape(cx, cy, cz) * coupling

time: 111 us -> 109 us (0.982)
  local copies, waits for them, and re-layouts: 21.7 us -> 19.9 us
    unnamed x1 -> x0, other arithmetic: 1.86 us -> none
    another operation x1 -> x0, local copies, waits for them, and re-layouts: 1.36 us -> none  [local(): coarse = patch.reshape(cx, CB, cy, CB, cz, CB).sum(axis=(1, 3, 5)) * scale]
    unnamed x9 -> x6, local copies, waits for them, and re-layouts: 2.36 us -> 1.85 us
  transfers between devices with their start and end apart: 8 -> 8, of which waited for: 3 -> 3; matrix products, arithmetic and copies ran while one was open for 30% -> 32% of each run, Pallas kernels for 0% -> 0%
where the time goes in v11:
time: 109 us; the launch traced here: 107 us
  starting transfers between devices  54.6 us (50%)
  local copies, waits for them, and re-layouts  19.9 us (18%)
  matrix products  15.4 us (14%)
  waiting for transfers between devices  10.1 us (9%)
  other arithmetic  6.13 us (6%)
    all_to_all x2, starting transfers between devices, gather_rows(): return lax.all_to_all(rows, axes, 0, 0, tiled=True)  37.9 us
    ppermute x6, starting transfers between devices, from_behind(): return lax.ppermute(block, axis, route)  16.8 us
    dot_general x16, matrix products, mixed(): return jnp.einsum(form, table, data, preferred_element_type=jnp.float32)  11.1 us
    ppermute x6, waiting for transfers between devices, from_behind(): return lax.ppermute(block, axis, route)  10.1 us
    unnamed x4, matrix products  4.35 us
    convert_element_type x1, local copies, waits for them, and re-layouts, local_box(): new_real = (mixed(form, cosv, real) - mixed(form, sinv, imag)).astype(bf)  3.98 us
    convert_element_type x1, local copies, waits for them, and re-layouts, local_box(): imag = (mixed(form, cosv, imag) + mixed(form, sinv, real)).astype(bf)  3.3 us
  transfers between devices with their start and end apart: 8, of which 3 were waited for; matrix products, arithmetic and copies ran while one was open for 32% of the time, Pallas kernels for 0%

profile of v11, /device:TPU:1, one launch (start us, length us, event | category | flops | bytes accessed | tf_op | source)
XLA Modules:
  0.0 106.7 jit_solution(14987167487300112403)
XLA Ops:
  0.0 0.9 reduce_sum.117
  1.8 29.3 %all-to-all-start = ((f32[32,1,8]{2,1,0:T(1,128)}), f32[32,1,8]{2,1,0:T(1,128)S(1)}, u32[]{:S(2)}, u32[]{:S(2)}) async-start(f32[32,1,8]{2,1,0:T(1,128)} %broadcast_in_dim.106), calls=%async_computation | async-start | bytes 32768 | tf_op jit(solution)/shard_map/all_to_all | solution.py:96
  31.1 1.2 %convert_reduce_fusion = bf16[32768]{0:T(1024)(128)(2,1)S(1)} fusion(f32[1,1,1,32768]{3,2,1,0:T(1,128)} %param.3), kind=kLoop, calls=%fused_computation.56 | loop fusion | flops 32768 | bytes 196608 | tf_op jit(solution)/shard_map/convert_element_type | solution.py:44
  35.4 2.0 %reshape.158 = f32[64,64,64]{2,1,0:T(8,128)S(1)} reshape(f32[64,4096]{1,0:T(8,128)} %param.4) | data formatting | bytes 2097152 | tf_op jit(solution)/shard_map/reshape | solution.py:122
  43.7 1.6 %fusion = bf16[64,64,64]{1,2,0:T(8,128)(2,1)} fusion(f32[64,64,64]{2,1,0:T(8,128)S(1)} %fusion.45, bf16[64,64,64]{2,1,0:T(8,128)(2,1)S(1)} %add_convert_fusion.1), kind=kOutput, calls=%fused_computation.14 | convolution fusion | flops 34144256 | bytes 2097152 | tf_op jit(solution)/shard_map/nk,xkz->xnz/dot_general | solution.py:37
  45.3 4.0 %copy.95 = bf16[64,64,64]{0,2,1:T(8,128)(2,1)} copy(bf16[64,64,64]{1,2,0:T(8,128)(2,1)} %fusion) | data formatting | bytes 1048576 | tf_op jit(solution)/shard_map/convert_element_type | solution.py:60
  49.2 3.1 %fusion.51 = f32[64,4096]{0,1} fusion(bf16[64,4096]{0,1:T(8,128)(2,1)} %bitcast.69), kind=kOutput, calls=%fused_computation.100 | convolution fusion | flops 33619968 | bytes 1572864
  52.4 1.6 %fusion.1 = bf16[64,64,64]{1,2,0:T(8,128)(2,1)} fusion(f32[64,64,64]{2,1,0:T(8,128)S(1)} %fusion.41, bf16[64,64,64]{2,1,0:T(8,128)(2,1)S(1)} %subtract_convert_fusion.1), kind=kOutput, calls=%fused_computation.15 | convolution fusion | flops 34144256 | bytes 2097152 | tf_op jit(solution)/shard_map/nk,xkz->xnz/dot_general | solution.py:37
  53.9 3.3 %copy.98 = bf16[64,64,64]{0,2,1:T(8,128)(2,1)S(1)} copy(bf16[64,64,64]{1,2,0:T(8,128)(2,1)} %fusion.1) | data formatting | bytes 1048576 | tf_op jit(solution)/shard_map/convert_element_type | solution.py:61
  57.8 1.0 copy-done
  59.2 0.9 fusion.164
  60.1 3.2 %collective-permute-start = (f32[64,64,16]{0,2,1:T(8,128)}, f32[64,64,16]{0,2,1:T(8,128)S(1)}, u32[]{:S(2)}, u32[]{:S(2)}) collective-permute-start(f32[64,64,16]{0,2,1:T(8,128)} %get-tuple-element.11), channel_id=1, source_target_pairs={{0,1},{1,2},{2,3},{3,4},{4,5},{5,6},{6,7},{7,8},{8,9},{9,10},{10,1... | collective-permute-start | bytes 786440 | tf_op jit(solution)/shard_map/ppermute | solution.py:17
  63.3 1.3 %collective-permute-start.1 = (f32[64,64,16]{0,2,1:T(8,128)S(1)}, f32[64,64,16]{0,2,1:T(8,128)}, u32[]{:S(2)}, u32[]{:S(2)}) collective-permute-start(f32[64,64,16]{0,2,1:T(8,128)S(1)} %get-tuple-element.12), channel_id=1, source_target_pairs={{1,0},{2,1},{3,2},{4,3},{5,4},{6,5},{7,6},{8,7},{9,8},{10,9},{11,1... | collective-permute-start | bytes 786440 | tf_op jit(solution)/shard_map/ppermute | solution.py:17
  65.4 8.6 %all-to-all-start.1 = ((f32[32,1,8]{2,1,0:T(1,128)}), f32[32,1,8]{2,1,0:T(1,128)S(1)}, u32[]{:S(2)}, u32[]{:S(2)}) async-start(f32[32,1,8]{2,1,0:T(1,128)} %broadcast_in_dim.113), calls=%async_computation.1 | async-start | bytes 32768 | tf_op jit(solution)/shard_map/all_to_all | solution.py:96
  74.0 0.8 copy-done.1
  74.8 2.5 %collective-permute-done.1 = f32[64,64,16]{0,2,1:T(8,128)} collective-permute-done((f32[64,64,16]{0,2,1:T(8,128)S(1)}, f32[64,64,16]{0,2,1:T(8,128)}, u32[]{:S(2)}, u32[]{:S(2)}) %collective-permute-start.1) | collective-permute-done | bytes 262176 | tf_op jit(solution)/shard_map/ppermute | solution.py:17
  77.3 1.3 %slice_add_fusion = (f32[64,64,16]{0,2,1:T(8,128)S(1)}, f32[64,64,16]{0,2,1:T(8,128)S(1)}) fusion(f32[64,64,16]{0,2,1:T(8,128)} %collective-permute-done.1, f32[64,64,64]{0,2,1:T(8,128)S(1)} %sub.21, f32[64,64,16]{0,2,1:T(8,128)} %copy-done.1), kind=kLoop, calls=%fused_computation.34 | loop fusion | flops 131072 | bytes 1572864 | tf_op jit(solution)/shard_map/add | solution.py:90
  79.6 6.9 %collective-permute-start.2 = (f32[256,128]{1,0:T(8,128)S(1)}, f32[256,128]{1,0:T(8,128)S(1)}, u32[]{:S(2)}, u32[]{:S(2)}) collective-permute-start(f32[256,128]{1,0:T(8,128)S(1)} %reshape.160), channel_id=1, source_target_pairs={{0,32},{32,64},{64,96},{1,33},{33,65},{65,97},{2,34},{34,66},{66,9... | collective-permute-start | bytes 393224 | tf_op jit(solution)/shard_map/ppermute | solution.py:17
  86.5 1.9 %collective-permute-start.3 = (f32[256,128]{1,0:T(8,128)S(1)}, f32[256,128]{1,0:T(8,128)S(1)}, u32[]{:S(2)}, u32[]{:S(2)}) collective-permute-start(f32[256,128]{1,0:T(8,128)S(1)} %reshape.159), channel_id=1, source_target_pairs={{32,0},{64,32},{96,64},{33,1},{65,33},{97,65},{34,2},{66,34},{98,6... | collective-permute-start | bytes 393224 | tf_op jit(solution)/shard_map/ppermute | solution.py:17
  88.7 5.6 %collective-permute-done.3 = f32[256,128]{1,0:T(8,128)S(1)} collective-permute-done((f32[256,128]{1,0:T(8,128)S(1)}, f32[256,128]{1,0:T(8,128)S(1)}, u32[]{:S(2)}, u32[]{:S(2)}) %collective-permute-start.3) | collective-permute-done | bytes 131104 | tf_op jit(solution)/shard_map/ppermute | solution.py:17
  96.3 2.2 %collective-permute-start.4 = (f32[128,128]{1,0:T(8,128)S(1)}, f32[128,128]{1,0:T(8,128)S(1)}, u32[]{:S(2)}, u32[]{:S(2)}) collective-permute-start(f32[128,128]{1,0:T(8,128)S(1)} %reshape.164), channel_id=1, source_target_pairs={{0,128},{128,256},{256,384},{384,512},{512,640},{640,768},{768,896... | collective-permute-start | bytes 196616 | tf_op jit(solution)/shard_map/ppermute | solution.py:17
  98.5 1.3 %collective-permute-start.5 = (f32[128,128]{1,0:T(8,128)S(1)}, f32[128,128]{1,0:T(8,128)S(1)}, u32[]{:S(2)}, u32[]{:S(2)}) collective-permute-start(f32[128,128]{1,0:T(8,128)S(1)} %reshape.163), channel_id=1, source_target_pairs={{128,0},{256,128},{384,256},{512,384},{640,512},{768,640},{896,768... | collective-permute-start | bytes 196616 | tf_op jit(solution)/shard_map/ppermute | solution.py:17
  100.5 1.4 %reshape.169 = f32[1,1,1,32768]{3,2,1,0:T(1,128)S(1)} reshape(f32[2,16,2,16,2,16]{5,4,3,2,1,0:T(2,128)S(1)} %broadcast_in_dim.118) | data formatting | bytes 262144 | tf_op jit(solution)/shard_map/reshape | solution.py:136
  102.3 2.0 %collective-permute-done.5 = f32[128,128]{1,0:T(8,128)S(1)} collective-permute-done((f32[128,128]{1,0:T(8,128)S(1)}, f32[128,128]{1,0:T(8,128)S(1)}, u32[]{:S(2)}, u32[]{:S(2)}) %collective-permute-start.5) | collective-permute-done | bytes 65568 | tf_op jit(solution)/shard_map/ppermute | solution.py:17
  (75 shorter events, 18.2 us)
Async XLA Ops:
  1.8 62.9 %all-to-all-start = ((f32[32,1,8]{2,1,0:T(1,128)}), f32[32,1,8]{2,1,0:T(1,128)S(1)}, u32[]{:S(2)}, u32[]{:S(2)}) async-start(f32[32,1,8]{2,1,0:T(1,128)} %broadcast_in_dim.106), calls=%async_computation | async-start | bytes 32768 | tf_op jit(solution)/shard_map/all_to_all | solution.py:96
  57.3 1.6 %copy-start = (f32[64,4096]{0,1:S(1)}, f32[64,4096]{0,1}, u32[]{:S(2)}) copy-start(f32[64,4096]{0,1} %fusion.51) | copy-start | bytes 3145732
  60.1 13.9 %collective-permute-start = (f32[64,64,16]{0,2,1:T(8,128)}, f32[64,64,16]{0,2,1:T(8,128)S(1)}, u32[]{:S(2)}, u32[]{:S(2)}) collective-permute-start(f32[64,64,16]{0,2,1:T(8,128)} %get-tuple-element.11), channel_id=1, source_target_pairs={{0,1},{1,2},{2,3},{3,4},{4,5},{5,6},{6,7},{7,8},{8,9},{9,10},{10,1... | collective-permute-start | bytes 786440 | tf_op jit(solution)/shard_map/ppermute | solution.py:17
  63.3 14.0 %collective-permute-start.1 = (f32[64,64,16]{0,2,1:T(8,128)S(1)}, f32[64,64,16]{0,2,1:T(8,128)}, u32[]{:S(2)}, u32[]{:S(2)}) collective-permute-start(f32[64,64,16]{0,2,1:T(8,128)S(1)} %get-tuple-element.12), channel_id=1, source_target_pairs={{1,0},{2,1},{3,2},{4,3},{5,4},{6,5},{7,6},{8,7},{9,8},{10,9},{11,1... | collective-permute-start | bytes 786440 | tf_op jit(solution)/shard_map/ppermute | solution.py:17
  65.4 23.2 %all-to-all-start.1 = ((f32[32,1,8]{2,1,0:T(1,128)}), f32[32,1,8]{2,1,0:T(1,128)S(1)}, u32[]{:S(2)}, u32[]{:S(2)}) async-start(f32[32,1,8]{2,1,0:T(1,128)} %broadcast_in_dim.113), calls=%async_computation.1 | async-start | bytes 32768 | tf_op jit(solution)/shard_map/all_to_all | solution.py:96
  74.0 0.8 copy-start.1
  79.6 15.1 %collective-permute-start.2 = (f32[256,128]{1,0:T(8,128)S(1)}, f32[256,128]{1,0:T(8,128)S(1)}, u32[]{:S(2)}, u32[]{:S(2)}) collective-permute-start(f32[256,128]{1,0:T(8,128)S(1)} %reshape.160), channel_id=1, source_target_pairs={{0,32},{32,64},{64,96},{1,33},{33,65},{65,97},{2,34},{34,66},{66,9... | collective-permute-start | bytes 393224 | tf_op jit(solution)/shard_map/ppermute | solution.py:17
  86.5 7.8 %collective-permute-start.3 = (f32[256,128]{1,0:T(8,128)S(1)}, f32[256,128]{1,0:T(8,128)S(1)}, u32[]{:S(2)}, u32[]{:S(2)}) collective-permute-start(f32[256,128]{1,0:T(8,128)S(1)} %reshape.159), channel_id=1, source_target_pairs={{32,0},{64,32},{96,64},{33,1},{65,33},{97,65},{34,2},{66,34},{98,6... | collective-permute-start | bytes 393224 | tf_op jit(solution)/shard_map/ppermute | solution.py:17
  95.3 4.7 %copy-start.2 = (f32[2,2,2]{2,1,0:T(2,128)S(1)}, f32[2,2,2]{2,1,0:T(2,128)}, u32[]{:S(2)}) copy-start(f32[2,2,2]{2,1,0:T(2,128)} %param.5) | copy-start | bytes 100
  96.3 5.6 %collective-permute-start.4 = (f32[128,128]{1,0:T(8,128)S(1)}, f32[128,128]{1,0:T(8,128)S(1)}, u32[]{:S(2)}, u32[]{:S(2)}) collective-permute-start(f32[128,128]{1,0:T(8,128)S(1)} %reshape.164), channel_id=1, source_target_pairs={{0,128},{128,256},{256,384},{384,512},{512,640},{640,768},{768,896... | collective-permute-start | bytes 196616 | tf_op jit(solution)/shard_map/ppermute | solution.py:17
  98.5 5.7 %collective-permute-start.5 = (f32[128,128]{1,0:T(8,128)S(1)}, f32[128,128]{1,0:T(8,128)S(1)}, u32[]{:S(2)}, u32[]{:S(2)}) collective-permute-start(f32[128,128]{1,0:T(8,128)S(1)} %reshape.163), channel_id=1, source_target_pairs={{128,0},{256,128},{384,256},{512,384},{640,512},{768,640},{896,768... | collective-permute-start | bytes 196616 | tf_op jit(solution)/shard_map/ppermute | solution.py:17
